TPU v7x, 128 devices: a whole 4x4x4 slice. The times are simulated.
128 devices in a mesh: dp: 8 (over y, z_lo), ctx: 16 (over z_hi, x, core).
Axes of the slice: x: 4, y: 4, z: 4 (z_hi: 2, z_lo: 2; z = z_hi * 2 + z_lo), core: 2. Of those that a mesh axis runs over, the one named last changes fastest.
Arguments:
- queries: bfloat16 [8, 12288, 2048], P('dp', 'ctx'), may hold values from -200 to 200
- keys: bfloat16 [8, 12288, 2048], P('dp', 'ctx'), may hold values from -6 to 6
- values: bfloat16 [8, 12288, 2048], P('dp', 'ctx'), may hold values from -6 to 6
- grad_out: bfloat16 [8, 12288, 2048], P('dp', 'ctx'), may hold values from -6 to 6
- out_weight: bfloat16 [2048, 2048], P('dp'), may hold values from -0.125 to 0.125
- pattern: int32 [8, 96, 2], P('dp', 'ctx'), may hold values from 0 to 95, as said below
Outputs:
- mixed: bfloat16 [8, 12288, 2048], P('dp', 'ctx')
- query_grad: bfloat16 [8, 12288, 2048], P('dp', 'ctx')
- weight_grad: float32 [2048, 2048], P('dp')
Inputs may be any that keep to these rules, and one draw needn't show every extreme that they name: `pattern`: key block c of a trace holds positions 128 * c onward and lies on ctx device c // 6. For each trace, the 12 entries of the query blocks of one ctx device name key blocks on pairwise distinct ctx devices.
All inputs are finite; a program needn't handle non-finite values.
Results may differ from a plain program's by a relative error of at most 0.014.
Values may be sent and summed in bfloat16 or wider, within the bound.
No kernel may reach another device: no remote copies, remote signals or barrier semaphores. Data moves between devices by JAX's collectives and lax.ppermute only.
A program may use at most 192 MiB of HBM per device.

v0:
```python
import math

import jax
import jax.numpy as jnp
from jax import lax
from jax.sharding import PartitionSpec as P

HEADS = 16
DH = 128
BLK = 128
KSEL = 2


def softmax_rows(scores):
    top = jnp.max(scores, axis=-1, keepdims=True)
    weights = jnp.exp(scores - top)
    return weights / jnp.sum(weights, axis=-1, keepdims=True)


def local(queries, keys, values, grad_out, out_weight, pattern):
    ctx_count = lax.axis_size("ctx")
    data_count = lax.axis_size("dp")
    own_index = lax.axis_index("ctx")
    rows = queries.shape[1]
    blocks = rows // BLK
    width = HEADS * DH
    scale = 1.0 / math.sqrt(DH)
    query_rows = queries[0].reshape(blocks, BLK, HEADS, DH)
    key_blocks = keys[0].reshape(blocks, BLK, width)
    value_blocks = values[0].reshape(blocks, BLK, width)
    table = pattern[0]
    owner = table // blocks
    every_table = lax.all_gather(table, "ctx", axis=0, tiled=True).reshape(ctx_count, blocks * KSEL)
    wanted = every_table // blocks == own_index
    send_index = jnp.sum(jnp.where(wanted, every_table % blocks, 0), axis=1)
    send_flag = jnp.any(wanted, axis=1)
    flag = send_flag[:, None, None]
    empty = jnp.zeros((), jnp.bfloat16)
    send_keys = jnp.where(flag, jnp.take(key_blocks, send_index, axis=0), empty)
    send_values = jnp.where(flag, jnp.take(value_blocks, send_index, axis=0), empty)
    got_keys, got_values = (
        lax.all_to_all(send_keys, "ctx", split_axis=0, concat_axis=0, tiled=True),
        lax.all_to_all(send_values, "ctx", split_axis=0, concat_axis=0, tiled=True),
    )
    order = owner.reshape(-1)
    picked_keys = jnp.take(got_keys, order, axis=0).reshape(blocks, KSEL * BLK, HEADS, DH)
    picked_values = jnp.take(got_values, order, axis=0).reshape(blocks, KSEL * BLK, HEADS, DH)
    scores = (
        jnp.einsum("qrhd,qkhd->qhrk", query_rows, picked_keys, preferred_element_type=jnp.float32)
        * scale
    )
    probs = softmax_rows(scores)
    attention = jnp.einsum(
        "qhrk,qkhd->qrhd",
        probs.astype(jnp.bfloat16),
        picked_values,
        preferred_element_type=jnp.float32,
    )
    attention = attention.astype(jnp.bfloat16)
    attention_flat = attention.reshape(rows, width)
    grad_flat = grad_out[0]
    piece = lax.all_gather(out_weight, "dp", axis=0, tiled=True)
    columns = attention_flat
    total = jnp.dot(columns, piece, preferred_element_type=jnp.float32)
    part_back = lax.dot_general(
        grad_flat, piece, (((1,), (1,)), ((), ())), preferred_element_type=jnp.float32
    )
    back_sum = part_back
    mixed_sum, back_sum = (total, back_sum)
    mixed = mixed_sum.astype(jnp.bfloat16)
    back = back_sum.astype(jnp.bfloat16)
    columns = attention_flat
    shard = lax.psum_scatter(
        lax.dot_general(
            columns, grad_flat, (((0,), (0,)), ((), ())), preferred_element_type=jnp.float32
        ),
        ("dp", "ctx"),
        scatter_dimension=0,
        tiled=True,
    )
    weight_sum = lax.all_gather(shard.astype(jnp.bfloat16), "ctx", axis=0, tiled=True).astype(
        shard.dtype
    )
    weight_grad = weight_sum / math.sqrt(rows * ctx_count * data_count)
    back_rows = back.reshape(blocks, BLK, HEADS, DH)
    dprobs = jnp.einsum(
        "qrhd,qkhd->qhrk", back_rows, picked_values, preferred_element_type=jnp.float32
    )
    delta = jnp.einsum("qrhd,qrhd->qhr", back_rows, attention, preferred_element_type=jnp.float32)[
        ..., None
    ]
    dscores = (probs * (dprobs - delta)).astype(jnp.bfloat16)
    query_sum = (
        jnp.einsum("qhrk,qkhd->qrhd", dscores, picked_keys, preferred_element_type=jnp.float32)
        * scale
    )
    query_grad = query_sum.astype(jnp.bfloat16).reshape(rows, width)
    return (mixed[None], query_grad[None], weight_grad)


def solution(mesh):
    return jax.shard_map(
        local,
        mesh=mesh,
        in_specs=(
            P("dp", "ctx", None),
            P("dp", "ctx", None),
            P("dp", "ctx", None),
            P("dp", "ctx", None),
            P("dp", None),
            P("dp", "ctx", None),
        ),
        out_specs=(P("dp", "ctx", None), P("dp", "ctx", None), P("dp", None)),
        check_vma=False,
    )
```

profile of v0, /device:TPU:1, one launch (start us, length us, event | category | flops | bytes accessed | tf_op | source)
XLA Modules:
  0.0 1188.7 jit_solution(648756658406002467)
XLA Ops:
  8.1 26.6 %all-gather = s32[1,96,2]{2,0,1:T(1,128)S(1)} all-gather(s32[1,6,2]{2,0,1:T(1,128)S(1)} %copy.44), channel_id=2, replica_groups=mesh['dp'=8,'ctx'=16] {'ctx'}, dimensions={1}, use_global_device_ids=true | all-gather | bytes 816 | tf_op jit(solution)/shard_map/all_gather | solution.py:33
  35.1 4.7 gather_fusion
  39.8 6.6 gather_fusion.2
  46.6 11.8 select_select_fusion.1
  58.4 4.7 all-to-all-start
  63.8 141.9 %all-to-all-done = bf16[16,128,2048]{2,1,0:T(8,128)(2,1)} async-done(((bf16[16,128,2048]{2,1,0:T(8,128)(2,1)}), bf16[16,128,2048]{2,1,0:T(8,128)(2,1)}, u32[]{:S(2)}, u32[]{:S(2)}) %all-to-all-start) | async-done | bytes 8388640 | tf_op jit(solution)/shard_map/all_to_all | solution.py:43
  205.6 7.6 all-to-all-start.1
  213.8 2.9 copy.70
  216.8 7.6 gather_fusion.1
  224.4 127.8 %all-to-all-done.1 = bf16[16,128,2048]{2,1,0:T(8,128)(2,1)} async-done(((bf16[16,128,2048]{2,1,0:T(8,128)(2,1)}), bf16[16,128,2048]{2,1,0:T(8,128)(2,1)}, u32[]{:S(2)}, u32[]{:S(2)}) %all-to-all-start.1) | async-done | bytes 8388640 | tf_op jit(solution)/shard_map/all_to_all | solution.py:42
  352.2 7.6 gather_fusion.3
  359.9 8.4 broadcast_select_fusion.1
  368.3 5.0 copy.69
  373.4 9.0 copy.56
  382.4 7.9 copy.68
  390.3 5.7 fusion.21
  396.0 16.2 %fusion.43 = (f32[6,16,128]{2,1,0:T(8,128)S(1)}, f32[6,16,128,256]{2,3,1,0:T(8,128)}) fusion(f32[6,16,256,128]{3,2,1,0:T(8,128)} %fusion.21), kind=kOutput, calls=%fused_computation.62 | output fusion | flops 12583167 | bytes 25214976 | tf_op jit(solution)/shard_map/sub | solution.py:16
  412.2 9.1 fusion.33
  422.3 3.2 bitcast_convert_fusion
  425.5 6.5 copy.66
  432.1 12.9 %multiply_reduce_fusion = (f32[6,16,128]{2,1,0:T(8,128)S(1)}, bf16[6,16,128,128]{3,2,1,0:T(8,128)(2,1)}) fusion(f32[6,16,128,128]{2,3,1,0:T(8,128)} %copy.66, f32[6,16,128,256]{2,3,1,0:T(8,128)} %get-tuple-element.14, f32[6,16,128]{2,1,0:T(8,128)S(1)} %get-tuple-element.13, bf16[6,256,16,128]{3,2,1,0:T(8,128)(2,1)} %bitcast.91), kind=kOutput, calls=%fused_computation.14 | convolution fusion | flops 817876992 | bytes 28409856 | tf_op jit(solution)/shard_map/qhrk,qkhd->qrhd/dot_general | solution.py:53
  445.0 4.9 copy.52
  449.9 12.6 %fusion.15 = f32[2048,2048]{1,0:T(8,128)} fusion(bf16[1,768,2048]{2,1,0:T(8,128)(2,1)} %param.13, bf16[96,8,16,128]{3,2,1,0:T(8,128)(2,1)} %bitcast.98), kind=kOutput, calls=%fused_computation.29 | convolution fusion | flops 6442450944 | bytes 23068672 | tf_op jit(solution)/shard_map/dot_general | solution.py:74
  462.9 9.0 fusion.12
  471.9 658.6 %reduce-scatter.2.cloned.1.call-done = f32[16,2048]{1,0:T(8,128)} async-done(((f32[2048,2048]{1,0:T(8,128)}), f32[16,2048]{1,0:T(8,128)}) %reduce-scatter.2.cloned.1.call-update) | async-done | bytes 131088 | tf_op jit(solution)/shard_map/reduce_scatter | solution.py:73
  1130.5 1.5 convert_element_type.38
  1132.0 14.0 %fusion.14 = bf16[6,128,16,128]{1,3,2,0:T(8,128)(2,1)} fusion(bf16[6,256,16,128]{1,3,2,0:T(8,128)(2,1)} %copy.56, f32[6,16,128,256]{2,3,1,0:T(8,128)} %fusion.12, f32[6,16,128]{2,1,0:T(8,128)S(1)} %get-tuple-element.15, f32[6,16,128,256]{2,3,1,0:T(8,128)} %get-tuple-element.14, f32[6,16,128]{2,1,0:T(8,128)S(1)} %get-tuple-element.13), kind=kOutput, calls=%fused_computation.28 | convolution fusion | flops 821035008 | bytes 34701312 | tf_op jit(solution)/shard_map/qhrk,qkhd->qrhd/dot_general | solution.py:94
  1146.1 3.8 copy.58
  1149.9 3.3 broadcast_in_dim_reshape.3
  1153.2 12.0 %fusion.23 = bf16[1,768,2048]{2,1,0:T(8,128)(2,1)} fusion(bf16[2048,2048]{1,0:T(8,128)(2,1)} %all-gather.4.cloned.1.call-done, bf16[96,8,16,128]{3,2,1,0:T(8,128)(2,1)} %bitcast.99), kind=kOutput, calls=%fused_computation.38 | convolution fusion | flops 6444023808 | bytes 14680064 | tf_op jit(solution)/shard_map/dot_general | solution.py:64
  1165.2 14.2 %all-gather.6.cloned.1.call-done = bf16[256,2048]{1,0:T(8,128)(2,1)} async-done(((bf16[16,2048]{1,0:T(8,128)(2,1)}), bf16[256,2048]{1,0:T(8,128)(2,1)}) %all-gather.6.cloned.1.call-update) | async-done | bytes 1048592 | tf_op jit(solution)/shard_map/all_gather | solution.py:81
  1179.4 2.8 convert_multiply_fusion
  (37 shorter events, 4.2 us)
Async XLA Ops:
  7.2 27.9 %copy-start = (bf16[1,768,2048]{2,1,0:T(8,128)(2,1)S(1)}, bf16[1,768,2048]{2,1,0:T(8,128)(2,1)}, u32[]{:S(2)}) copy-start(bf16[1,768,2048]{2,1,0:T(8,128)(2,1)} %param.12) | copy-start | bytes 9437188
  58.4 147.3 %all-to-all-start = ((bf16[16,128,2048]{2,1,0:T(8,128)(2,1)}), bf16[16,128,2048]{2,1,0:T(8,128)(2,1)}, u32[]{:S(2)}, u32[]{:S(2)}) async-start(bf16[16,128,2048]{2,1,0:T(8,128)(2,1)} %get-tuple-element.9), calls=%async_computation | async-start | bytes 16777216 | tf_op jit(solution)/shard_map/all_to_all | solution.py:43
  63.0 349.2 %all-gather.4.cloned.1.call-start = ((), (), s32[]{:S(2)}) async-start(), calls=%async_computation.3 | async-start | bytes 9437184 | tf_op jit(solution)/shard_map/all_gather | solution.py:62
  205.6 7.8 copy-start.3
  205.6 146.6 %all-to-all-start.1 = ((bf16[16,128,2048]{2,1,0:T(8,128)(2,1)}), bf16[16,128,2048]{2,1,0:T(8,128)(2,1)}, u32[]{:S(2)}, u32[]{:S(2)}) async-start(bf16[16,128,2048]{2,1,0:T(8,128)(2,1)} %get-tuple-element.10), calls=%async_computation.1 | async-start | bytes 16777216 | tf_op jit(solution)/shard_map/all_to_all | solution.py:42
  213.2 917.3 %reduce-scatter.2.cloned.1.call-start = ((), (), s32[]{:S(2)}) async-start(), calls=%async_computation.4 | async-start | bytes 16908288 | tf_op jit(solution)/shard_map/reduce_scatter | solution.py:73
  382.4 7.9 copy-start.2
  396.0 16.2 %copy-start.4 = (bf16[1,768,2048]{2,1,0:T(8,128)(2,1)S(1)}, bf16[1,768,2048]{2,1,0:T(8,128)(2,1)}, u32[]{:S(2)}) copy-start(bf16[1,768,2048]{2,1,0:T(8,128)(2,1)} %param.13) | copy-start | bytes 9437188
  462.6 716.9 %all-gather.6.cloned.1.call-start = ((), (), s32[]{:S(2)}) async-start(), calls=%async_computation.5 | async-start | bytes 1114112 | tf_op jit(solution)/shard_map/all_gather | solution.py:81
  1153.2 29.0 %copy-start.1 = (bf16[1,768,2048]{2,1,0:T(8,128)(2,1)S(1)}, bf16[1,768,2048]{2,1,0:T(8,128)(2,1)}, u32[]{:S(2)}) copy-start(bf16[1,768,2048]{2,1,0:T(8,128)(2,1)} %param.12) | copy-start | bytes 9437188
Sparse Core Ops, SparseCore 0:
  65.5 337.0 all-gather.3
  462.7 667.7 reduce-scatter.1
  1133.5 45.8 all-gather.5
where the time goes:
time: 1190 us
  waiting for transfers between devices  943 us (79%)
  matrix products  75.4 us (6%)
  local copies, waits for them, and re-layouts  72.7 us (6%)
  other arithmetic  44.3 us (4%)
  blocking collectives  26.6 us (2%)
  between operations  13.9 us (1%)
  starting transfers between devices  12.8 us (1%)
    reduce_scatter x1, waiting for transfers between devices, local(): lax.psum_scatter(lax.dot_general(columns, grad_flat, (((0,), (0,)), ((),...  659 us
    all_to_all x1, waiting for transfers between devices, local(): lax.all_to_all(send_values, 'ctx', split_axis=0, concat_axis=0, tiled=True)  142 us
    all_to_all x1, waiting for transfers between devices, local(): lax.all_to_all(send_keys, 'ctx', split_axis=0, concat_axis=0, tiled=True)  128 us
    all_gather x1, blocking collectives, local(): lax.all_gather(table, 'ctx', axis=0, tiled=True)  26.6 us
    unnamed x16, local copies, waits for them, and re-layouts  24.4 us
  transfers between devices with their start and end apart: 5, of which 4 were waited for; matrix products, arithmetic and copies ran while one was open for 10% of the time, Pallas kernels for 0%

commit v1 on v0

--- a/solution.py
+++ b/solution.py
@@ -69,18 +69,18 @@
     mixed_sum, back_sum = (total, back_sum)
     mixed = mixed_sum.astype(jnp.bfloat16)
     back = back_sum.astype(jnp.bfloat16)
-    columns = attention_flat
-    shard = lax.psum_scatter(
-        lax.dot_general(
-            columns, grad_flat, (((0,), (0,)), ((), ())), preferred_element_type=jnp.float32
-        ),
-        ("dp", "ctx"),
-        scatter_dimension=0,
-        tiled=True,
+    split = width // (ctx_count * data_count)
+    columns = (
+        attention_flat.reshape(rows, data_count, ctx_count, split)
+        .transpose(0, 2, 1, 3)
+        .reshape(rows, width)
     )
-    weight_sum = lax.all_gather(shard.astype(jnp.bfloat16), "ctx", axis=0, tiled=True).astype(
-        shard.dtype
+    partial = lax.dot_general(
+        columns, grad_flat, (((0,), (0,)), ((), ())), preferred_element_type=jnp.float32
     )
+    stage = lax.psum_scatter(partial, "ctx", scatter_dimension=0, tiled=True)
+    shard = lax.psum_scatter(stage, "dp", scatter_dimension=0, tiled=True)
+    weight_sum = lax.all_gather(shard, "ctx", axis=0, tiled=True)
     weight_grad = weight_sum / math.sqrt(rows * ctx_count * data_count)
     back_rows = back.reshape(blocks, BLK, HEADS, DH)
     dprobs = jnp.einsum(

time: 1190 us -> 724 us (0.61)
  waiting for transfers between devices: 943 us -> 463 us
  local copies, waits for them, and re-layouts: 72.7 us -> 86.7 us
    reduce_scatter x1 -> x2, waiting for transfers between devices: 659 us -> 171 us  [the longest x1 149 us: local(): stage = lax.psum_scatter(partial, 'ctx', scatter_dimension=0, tiled=True)]
  transfers between devices with their start and end apart: 5 -> 6, of which waited for: 4 -> 5; matrix products, arithmetic and copies ran while one was open for 10% -> 16% of each run, Pallas kernels for 0% -> 0%
where the time goes in v1:
time: 724 us; the launch traced here: 720 us
  waiting for transfers between devices  463 us (64%)
  local copies, waits for them, and re-layouts  86.7 us (12%)
  matrix products  76.7 us (11%)
  other arithmetic  40.4 us (6%)
  blocking collectives  26.6 us (4%)
  between operations  14.4 us (2%)
  starting transfers between devices  12.6 us (2%)
    reduce_scatter x1, waiting for transfers between devices, local(): stage = lax.psum_scatter(partial, 'ctx', scatter_dimension=0, tiled=True)  149 us
    all_to_all x1, waiting for transfers between devices, local(): lax.all_to_all(send_values, 'ctx', split_axis=0, concat_axis=0, tiled=True)  142 us
    all_to_all x1, waiting for transfers between devices, local(): lax.all_to_all(send_keys, 'ctx', split_axis=0, concat_axis=0, tiled=True)  128 us
    all_gather x1, blocking collectives, local(): lax.all_gather(table, 'ctx', axis=0, tiled=True)  26.6 us
    unnamed x16, local copies, waits for them, and re-layouts  21.8 us
    reduce_scatter x1, waiting for transfers between devices, local(): shard = lax.psum_scatter(stage, 'dp', scatter_dimension=0, tiled=True)  21.7 us
    all_gather x1, waiting for transfers between devices, local(): weight_sum = lax.all_gather(shard, 'ctx', axis=0, tiled=True)  21.3 us
    sub x1, other arithmetic, softmax_rows(): weights = jnp.exp(scores - top)  16.2 us
  transfers between devices with their start and end apart: 6, of which 5 were waited for; matrix products, arithmetic and copies ran while one was open for 16% of the time, Pallas kernels for 0%

profile of v1, /device:TPU:1, one launch (start us, length us, event | category | flops | bytes accessed | tf_op | source)
XLA Modules:
  0.0 720.3 jit_solution(5534313445753713615)
XLA Ops:
  8.1 26.6 %all-gather = s32[1,96,2]{2,0,1:T(1,128)S(1)} all-gather(s32[1,6,2]{2,0,1:T(1,128)S(1)} %copy.48), channel_id=2, replica_groups=mesh['dp'=8,'ctx'=16] {'ctx'}, dimensions={1}, use_global_device_ids=true | all-gather | bytes 816 | tf_op jit(solution)/shard_map/all_gather | solution.py:33
  35.1 4.7 gather_fusion.2
  39.8 6.6 gather_fusion
  46.5 11.8 %select_select_fusion.1 = (bf16[16,128,2048]{2,1,0:T(8,128)(2,1)}, bf16[16,128,2048]{2,1,0:T(8,128)(2,1)}) fusion(bf16[16,128,2048]{2,1,0:T(8,128)(2,1)} %gather_fusion, pred[16]{0:T(512)(128)(4,1)S(1)} %compare_and_fusion.1, pred[16]{0:T(512)(128)(4,1)S(1)} %reduce_or.18, bf16[16,128,2048]{2,1,0:T(8,128)(2,1)} %gather_fusion.2), kind=kLoop, calls=%fused_computation.12 | loop fusion | flops 16777216 | bytes 33554464 | tf_op jit(solution)/shard_map/jit(_where)/select_n | solution.py:40
  58.3 4.7 all-to-all-start
  63.7 141.7 %all-to-all-done = bf16[16,128,2048]{2,1,0:T(8,128)(2,1)} async-done(((bf16[16,128,2048]{2,1,0:T(8,128)(2,1)}), bf16[16,128,2048]{2,1,0:T(8,128)(2,1)}, u32[]{:S(2)}, u32[]{:S(2)}) %all-to-all-start) | async-done | bytes 8388640 | tf_op jit(solution)/shard_map/all_to_all | solution.py:43
  205.4 7.6 %all-to-all-start.1 = ((bf16[16,128,2048]{2,1,0:T(8,128)(2,1)}), bf16[16,128,2048]{2,1,0:T(8,128)(2,1)}, u32[]{:S(2)}, u32[]{:S(2)}) async-start(bf16[16,128,2048]{2,1,0:T(8,128)(2,1)} %get-tuple-element.10), calls=%async_computation.1 | async-start | bytes 16777216 | tf_op jit(solution)/shard_map/all_to_all | solution.py:42
  216.6 7.6 %gather_fusion.1 = bf16[12,128,2048]{2,1,0:T(8,128)(2,1)} fusion(bf16[16,128,2048]{2,1,0:T(8,128)(2,1)} %all-to-all-done, s32[1024]{0:T(1024)S(1)} %pad_clamp_fusion), kind=kCustom, calls=%fused_computation.1.clone | custom fusion | bytes 12582960 | tf_op jit(solution)/shard_map/jit(_take)/gather | solution.py:47
  224.1 128.2 %all-to-all-done.1 = bf16[16,128,2048]{2,1,0:T(8,128)(2,1)} async-done(((bf16[16,128,2048]{2,1,0:T(8,128)(2,1)}), bf16[16,128,2048]{2,1,0:T(8,128)(2,1)}, u32[]{:S(2)}, u32[]{:S(2)}) %all-to-all-start.1) | async-done | bytes 8388640 | tf_op jit(solution)/shard_map/all_to_all | solution.py:42
  352.3 7.6 %gather_fusion.3 = bf16[12,128,2048]{2,1,0:T(8,128)(2,1)} fusion(bf16[16,128,2048]{2,1,0:T(8,128)(2,1)} %all-to-all-done.1, s32[1024]{0:T(1024)S(1)} %pad_clamp_fusion), kind=kCustom, calls=%fused_computation.3.clone | custom fusion | bytes 12582960 | tf_op jit(solution)/shard_map/jit(_take)/gather | solution.py:46
  360.0 5.6 broadcast_select_fusion.1
  365.6 4.9 copy.74
  370.5 5.0 copy.75
  375.5 9.2 %copy.60 = bf16[6,256,16,128]{1,3,2,0:T(8,128)(2,1)} copy(bf16[6,256,16,128]{3,2,1,0:T(8,128)(2,1)} %bitcast.93) | data formatting | bytes 12582912 | tf_op jit(solution)/shard_map/reshape | solution.py:46
  384.7 9.3 %fusion.21 = f32[6,16,256,128]{3,2,1,0:T(8,128)} fusion(bf16[6,256,16,128]{1,3,2,0:T(8,128)(2,1)} %copy.60, bf16[6,128,16,128]{3,2,1,0:T(8,128)(2,1)S(1)} %bitcast.102), kind=kOutput, calls=%fused_computation.36 | convolution fusion | flops 805306368 | bytes 22020096 | tf_op jit(solution)/shard_map/qrhd,qkhd->qhrk/dot_general | solution.py:49
  394.0 16.2 %fusion.41 = (f32[6,16,128]{2,1,0:T(8,128)S(1)}, f32[6,16,128,256]{2,3,1,0:T(8,128)}) fusion(f32[6,16,256,128]{3,2,1,0:T(8,128)} %fusion.21), kind=kOutput, calls=%fused_computation.60 | output fusion | flops 12583167 | bytes 25214976 | tf_op jit(solution)/shard_map/sub | solution.py:16
  410.2 9.3 %fusion.31 = bf16[96,8,16,128]{3,1,2,0:T(8,128)(2,1)S(1)} fusion(bf16[2048,2048]{1,0:T(8,128)(2,1)} %all-gather.4.cloned.1.call-done, bf16[1,768,2048]{2,1,0:T(8,128)(2,1)S(1)} %copy-done.3), kind=kOutput, calls=%fused_computation.40 | convolution fusion | flops 6444023808 | bytes 14680064 | tf_op jit(solution)/shard_map/dot_general | solution.py:65
  420.5 3.2 bitcast_convert_fusion
  423.8 6.6 copy.72
  430.3 13.0 %multiply_reduce_fusion = (f32[6,16,128]{2,1,0:T(8,128)S(1)}, bf16[6,16,128,128]{3,2,1,0:T(8,128)(2,1)}) fusion(f32[6,16,128,128]{2,3,1,0:T(8,128)} %copy.72, f32[6,16,128,256]{2,3,1,0:T(8,128)} %get-tuple-element.14, f32[6,16,128]{2,1,0:T(8,128)S(1)} %get-tuple-element.13, bf16[6,256,16,128]{3,2,1,0:T(8,128)(2,1)} %bitcast.94), kind=kOutput, calls=%fused_computation.14 | convolution fusion | flops 817876992 | bytes 28409856 | tf_op jit(solution)/shard_map/qhrk,qkhd->qrhd/dot_general | solution.py:53
  443.3 6.4 copy.63
  449.8 7.7 %reshape_reshape.3 = bf16[768,8,16,16]{0,3,2,1:T(8,128)(2,1)} reshape(bf16[6,128,16,128]{1,0,3,2:T(8,128)(2,1)} %copy.63) | data formatting | bytes 6291456 | tf_op jit(solution)/shard_map/reshape;reshape | solution.py:74
  460.3 9.8 %fusion.17 = f32[2048,2048]{1,0:T(8,128)} fusion(bf16[768,2048]{0,1:T(8,128)(2,1)S(1)} %bitcast.105, bf16[1,768,2048]{2,1,0:T(8,128)(2,1)S(1)} %copy-done.4), kind=kOutput, calls=%fused_computation.31 | convolution fusion | flops 6442450944 | bytes 23068672 | tf_op jit(solution)/shard_map/dot_general | solution.py:78
  470.1 149.5 %reduce-scatter.3.cloned.1.call-done = f32[128,2048]{1,0:T(8,128)} async-done(((f32[2048,2048]{1,0:T(8,128)}), f32[128,2048]{1,0:T(8,128)}) %reduce-scatter.3.cloned.1.call-update) | async-done | bytes 1048592 | tf_op jit(solution)/shard_map/reduce_scatter | solution.py:81
  619.7 5.0 copy.56
  624.7 9.2 %fusion.12 = f32[6,16,128,256]{2,3,1,0:T(8,128)} fusion(bf16[6,256,16,128]{3,2,1,0:T(8,128)(2,1)} %bitcast.95, bf16[6,128,16,128]{3,2,1,0:T(8,128)(2,1)S(1)} %bitcast.92), kind=kOutput, calls=%fused_computation.24 | convolution fusion | flops 805306368 | bytes 22020096 | tf_op jit(solution)/shard_map/qrhd,qkhd->qhrk/dot_general | solution.py:86
  633.8 21.7 %reduce-scatter.5.cloned.1.call-done = f32[16,2048]{1,0:T(8,128)} async-done(((f32[128,2048]{1,0:T(8,128)}), f32[16,2048]{1,0:T(8,128)}) %reduce-scatter.5.cloned.1.call-update) | async-done | bytes 131088 | tf_op jit(solution)/shard_map/reduce_scatter | solution.py:82
  655.5 14.1 %fusion.14 = bf16[6,128,16,128]{1,3,2,0:T(8,128)(2,1)} fusion(bf16[6,256,16,128]{1,3,2,0:T(8,128)(2,1)} %copy.60, f32[6,16,128,256]{2,3,1,0:T(8,128)} %fusion.12, f32[6,16,128]{2,1,0:T(8,128)S(1)} %get-tuple-element.15, f32[6,16,128,256]{2,3,1,0:T(8,128)} %get-tuple-element.14, f32[6,16,128]{2,1,0:T(8,128)S(1)} %get-tuple-element.13), kind=kOutput, calls=%fused_computation.28 | convolution fusion | flops 821035008 | bytes 34701312 | tf_op jit(solution)/shard_map/qhrk,qkhd->qrhd/dot_general | solution.py:94
  669.7 3.9 copy.62
  673.5 3.3 broadcast_in_dim_reshape.3
  676.8 12.0 %fusion.23 = bf16[1,768,2048]{2,1,0:T(8,128)(2,1)} fusion(bf16[2048,2048]{1,0:T(8,128)(2,1)} %all-gather.4.cloned.1.call-done, bf16[96,8,16,128]{3,2,1,0:T(8,128)(2,1)} %bitcast.104), kind=kOutput, calls=%fused_computation.38 | convolution fusion | flops 6444023808 | bytes 14680064 | tf_op jit(solution)/shard_map/dot_general | solution.py:64
  688.9 21.3 %all-gather.6.cloned.1.call-done = f32[256,2048]{1,0:T(8,128)} async-done(((f32[16,2048]{1,0:T(8,128)}), f32[256,2048]{1,0:T(8,128)}) %all-gather.6.cloned.1.call-update) | async-done | bytes 2097168 | tf_op jit(solution)/shard_map/all_gather | solution.py:83
  (42 shorter events, 12.9 us)
Async XLA Ops:
  7.2 28.0 %copy-start = (bf16[1,768,2048]{2,1,0:T(8,128)(2,1)S(1)}, bf16[1,768,2048]{2,1,0:T(8,128)(2,1)}, u32[]{:S(2)}) copy-start(bf16[1,768,2048]{2,1,0:T(8,128)(2,1)} %param.11) | copy-start | bytes 9437188
  58.3 147.1 %all-to-all-start = ((bf16[16,128,2048]{2,1,0:T(8,128)(2,1)}), bf16[16,128,2048]{2,1,0:T(8,128)(2,1)}, u32[]{:S(2)}, u32[]{:S(2)}) async-start(bf16[16,128,2048]{2,1,0:T(8,128)(2,1)} %get-tuple-element.9), calls=%async_computation | async-start | bytes 16777216 | tf_op jit(solution)/shard_map/all_to_all | solution.py:43
  62.9 347.3 %all-gather.4.cloned.1.call-start = ((), (), s32[]{:S(2)}) async-start(), calls=%async_computation.4 | async-start | bytes 9437184 | tf_op jit(solution)/shard_map/all_gather | solution.py:62
  205.4 7.8 %copy-start.2 = (s32[1,6,2]{1,2,0:T(2,128)S(1)}, s32[1,6,2]{1,2,0:T(2,128)}, u32[]{:S(2)}) copy-start(s32[1,6,2]{1,2,0:T(2,128)} %param.15) | copy-start | bytes 148
  205.4 146.9 %all-to-all-start.1 = ((bf16[16,128,2048]{2,1,0:T(8,128)(2,1)}), bf16[16,128,2048]{2,1,0:T(8,128)(2,1)}, u32[]{:S(2)}, u32[]{:S(2)}) async-start(bf16[16,128,2048]{2,1,0:T(8,128)(2,1)} %get-tuple-element.10), calls=%async_computation.1 | async-start | bytes 16777216 | tf_op jit(solution)/shard_map/all_to_all | solution.py:42
  213.0 406.6 %reduce-scatter.3.cloned.1.call-start = ((), (), s32[]{:S(2)}) async-start(), calls=%async_computation.5 | async-start | bytes 17825792 | tf_op jit(solution)/shard_map/reduce_scatter | solution.py:81
  394.0 16.2 %copy-start.3 = (bf16[1,768,2048]{2,1,0:T(8,128)(2,1)S(1)}, bf16[1,768,2048]{2,1,0:T(8,128)(2,1)}, u32[]{:S(2)}) copy-start(bf16[1,768,2048]{2,1,0:T(8,128)(2,1)} %param.13) | copy-start | bytes 9437188
  457.5 2.8 copy-start.4
  470.1 185.4 %reduce-scatter.5.cloned.1.call-start = ((), (), s32[]{:S(2)}) async-start(), calls=%async_computation.6 | async-start | bytes 1179648 | tf_op jit(solution)/shard_map/reduce_scatter | solution.py:82
  619.6 90.5 %all-gather.6.cloned.1.call-start = ((), (), s32[]{:S(2)}) async-start(), calls=%async_computation.7 | async-start | bytes 2228224 | tf_op jit(solution)/shard_map/all_gather | solution.py:83
  676.8 36.5 %copy-start.1 = (bf16[1,768,2048]{2,1,0:T(8,128)(2,1)S(1)}, bf16[1,768,2048]{2,1,0:T(8,128)(2,1)}, u32[]{:S(2)}) copy-start(bf16[1,768,2048]{2,1,0:T(8,128)(2,1)} %param.11) | copy-start | bytes 9437188
Sparse Core Ops, SparseCore 0:
  65.4 337.1 all-gather.3
  470.2 149.3 reduce-scatter.2
  622.0 33.4 reduce-scatter.4
  657.8 52.3 all-gather.5

commit v2 on v1

--- a/solution.py
+++ b/solution.py
@@ -38,10 +38,10 @@
     empty = jnp.zeros((), jnp.bfloat16)
     send_keys = jnp.where(flag, jnp.take(key_blocks, send_index, axis=0), empty)
     send_values = jnp.where(flag, jnp.take(value_blocks, send_index, axis=0), empty)
-    got_keys, got_values = (
-        lax.all_to_all(send_keys, "ctx", split_axis=0, concat_axis=0, tiled=True),
-        lax.all_to_all(send_values, "ctx", split_axis=0, concat_axis=0, tiled=True),
+    got = lax.all_to_all(
+        jnp.concatenate([send_keys, send_values], axis=-1), "ctx", split_axis=0, concat_axis=0, tiled=True
     )
+    got_keys, got_values = got[..., :width], got[..., width:]
     order = owner.reshape(-1)
     picked_keys = jnp.take(got_keys, order, axis=0).reshape(blocks, KSEL * BLK, HEADS, DH)
     picked_values = jnp.take(got_values, order, axis=0).reshape(blocks, KSEL * BLK, HEADS, DH)
@@ -59,14 +59,25 @@
     attention = attention.astype(jnp.bfloat16)
     attention_flat = attention.reshape(rows, width)
     grad_flat = grad_out[0]
-    piece = lax.all_gather(out_weight, "dp", axis=0, tiled=True)
-    columns = attention_flat
-    total = jnp.dot(columns, piece, preferred_element_type=jnp.float32)
-    part_back = lax.dot_general(
-        grad_flat, piece, (((1,), (1,)), ((), ())), preferred_element_type=jnp.float32
+    half = out_weight.shape[1] // 2
+    side = own_index % 2
+    mine = lax.all_gather(
+        lax.dynamic_slice_in_dim(out_weight, side * half, half, axis=1), "dp", axis=0, tiled=True
     )
-    back_sum = part_back
-    mixed_sum, back_sum = (total, back_sum)
+    other = lax.ppermute(mine, "ctx", [(j, j ^ 1) for j in range(ctx_count)])
+    first = jnp.where(side == 0, mine, other)
+    second = jnp.where(side == 0, other, mine)
+    mixed_sum = jnp.concatenate(
+        [
+            jnp.dot(attention_flat, first, preferred_element_type=jnp.float32),
+            jnp.dot(attention_flat, second, preferred_element_type=jnp.float32),
+        ],
+        axis=1,
+    )
+    dims = (((1,), (1,)), ((), ()))
+    back_sum = lax.dot_general(
+        grad_flat[:, :half], first, dims, preferred_element_type=jnp.float32
+    ) + lax.dot_general(grad_flat[:, half:], second, dims, preferred_element_type=jnp.float32)
     mixed = mixed_sum.astype(jnp.bfloat16)
     back = back_sum.astype(jnp.bfloat16)
     split = width // (ctx_count * data_count)
@@ -78,9 +89,11 @@
     partial = lax.dot_general(
         columns, grad_flat, (((0,), (0,)), ((), ())), preferred_element_type=jnp.float32
     )
-    stage = lax.psum_scatter(partial, "ctx", scatter_dimension=0, tiled=True)
-    shard = lax.psum_scatter(stage, "dp", scatter_dimension=0, tiled=True)
-    weight_sum = lax.all_gather(shard, "ctx", axis=0, tiled=True)
+    stage = lax.psum_scatter(partial.astype(jnp.bfloat16), "ctx", scatter_dimension=0, tiled=True)
+    shard = lax.psum_scatter(stage.astype(jnp.float32), "dp", scatter_dimension=0, tiled=True)
+    weight_sum = lax.all_gather(shard.astype(jnp.bfloat16), "ctx", axis=0, tiled=True).astype(
+        jnp.float32
+    )
     weight_grad = weight_sum / math.sqrt(rows * ctx_count * data_count)
     back_rows = back.reshape(blocks, BLK, HEADS, DH)
     dprobs = jnp.einsum(

time: 724 us -> 687 us (0.949)
  waiting for transfers between devices: 463 us -> 404 us
  local copies, waits for them, and re-layouts: 86.7 us -> 104 us
    all_gather x2, waiting for transfers between devices: 21.3 us -> 293 us  [the longest x1 256 us: local(): lax.all_gather(lax.dynamic_slice_in_dim(out_weight, side * half, half, ax...]
    all_to_all x2 -> x1, waiting for transfers between devices: 270 us -> 0.01 us  [local(): lax.all_to_all(jnp.concatenate([send_keys, send_values], axis=-1), 'ctx',...]
    reduce_scatter x2, waiting for transfers between devices: 171 us -> 107 us  [the longest x1 96.4 us: local(): lax.psum_scatter(partial.astype(jnp.bfloat16), 'ctx', scatter_dimension=0...]
    slice x0 -> x1, local copies, waits for them, and re-layouts: none -> 11.8 us  [local(): got_keys, got_values = (got[..., :width], got[..., width:])]
    concatenate x0 -> x2, other arithmetic: none -> 8.73 us  [the longest x1 6.85 us: local(): jnp.concatenate([send_keys, send_values], axis=-1)]
    dot_general x2 -> x4, matrix products: 21.3 us -> 23.7 us  [the longest x1 6.73 us: local(): jnp.dot(attention_flat, second, preferred_element_type=jnp.float32)]
    unnamed x16 -> x26, local copies, waits for them, and re-layouts: 21.8 us -> 23.5 us
  transfers between devices with their start and end apart: 6 -> 6, of which waited for: 5 -> 5; matrix products, arithmetic and copies ran while one was open for 16% -> 12% of each run, Pallas kernels for 0% -> 0%
where the time goes in v2:
time: 687 us; the launch traced here: 678 us
  waiting for transfers between devices  404 us (59%)
  local copies, waits for them, and re-layouts  104 us (15%)
  matrix products  79.2 us (12%)
  other arithmetic  43.6 us (6%)
  blocking collectives  26.6 us (4%)
  between operations  14.2 us (2%)
    all_gather x1, waiting for transfers between devices, local(): lax.all_gather(lax.dynamic_slice_in_dim(out_weight, side * half, half, ax...  256 us
    reduce_scatter x1, waiting for transfers between devices, local(): lax.psum_scatter(partial.astype(jnp.bfloat16), 'ctx', scatter_dimension=0...  96.4 us
    all_gather x1, waiting for transfers between devices, local(): lax.all_gather(shard.astype(jnp.bfloat16), 'ctx', axis=0, tiled=True)  36.9 us
    all_gather x1, blocking collectives, local(): lax.all_gather(table, 'ctx', axis=0, tiled=True)  26.6 us
    unnamed x26, local copies, waits for them, and re-layouts  23.5 us
    sub x1, other arithmetic, softmax_rows(): weights = jnp.exp(scores - top)  16 us
    dot_general x1, matrix products, local(): jnp.einsum('qhrk,qkhd->qrhd', dscores, picked_keys, preferred_element_typ...  14.2 us
  transfers between devices with their start and end apart: 6, of which 5 were waited for; matrix products, arithmetic and copies ran while one was open for 12% of the time, Pallas kernels for 0%

profile of v2, /device:TPU:1, one launch (start us, length us, event | category | flops | bytes accessed | tf_op | source)
XLA Modules:
  0.0 677.8 jit_solution(11107420815461198943)
XLA Ops:
  8.1 26.6 %all-gather = s32[1,96,2]{2,0,1:T(1,128)S(1)} all-gather(s32[1,6,2]{2,0,1:T(1,128)S(1)} %copy.50), channel_id=2, replica_groups=mesh['dp'=8,'ctx'=16] {'ctx'}, dimensions={1}, use_global_device_ids=true | all-gather | bytes 816 | tf_op jit(solution)/shard_map/all_gather | solution.py:33
  35.1 4.7 gather_fusion.1
  39.8 6.6 gather_fusion
  46.5 7.0 %select_select_fusion.1 = (bf16[16,128,2048]{2,1,0:T(8,128)(2,1)S(1)}, bf16[16,128,2048]{2,1,0:T(8,128)(2,1)S(1)}) fusion(bf16[16,128,2048]{2,1,0:T(8,128)(2,1)} %gather_fusion, pred[16]{0:T(512)(128)(4,1)S(1)} %compare_and_fusion.1, pred[16]{0:T(512)(128)(4,1)S(1)} %reduce_or.18, bf16[16,128,2048]{2,1,0:T(8,128)(2,1)} %gather_fusion.1), kind=kLoop, calls=%fused_computation.13 | loop fusion | flops 16777216 | bytes 33554464 | tf_op jit(solution)/shard_map/jit(_where)/select_n | solution.py:39
  53.5 6.8 %pad_maximum_fusion = bf16[16,128,4096]{2,1,0:T(8,128)(2,1)} fusion(bf16[16,128,2048]{2,1,0:T(8,128)(2,1)S(1)} %get-tuple-element.12, bf16[16,128,2048]{2,1,0:T(8,128)(2,1)S(1)} %get-tuple-element.11), kind=kLoop, calls=%fused_computation.5 | loop fusion | flops 33554432 | bytes 33554432 | tf_op jit(solution)/shard_map/concatenate | solution.py:42
  60.4 5.3 all-to-all-start
  67.8 256.0 %all-gather.4.cloned.1.call-done = bf16[2048,1024]{1,0:T(8,128)(2,1)} async-done(((bf16[256,1024]{1,0:T(8,128)(2,1)}), bf16[2048,1024]{1,0:T(8,128)(2,1)}) %all-gather.4.cloned.1.call-update) | async-done | bytes 4194320 | tf_op jit(solution)/shard_map/all_gather | solution.py:64
  327.4 4.0 collective-permute-done
  331.4 5.2 fusion.36
  336.7 6.0 fusion.22
  351.8 6.5 copy.75
  358.3 11.8 %fusion.53 = (bf16[16,128,2048]{2,1,0:T(8,128)(2,1)}, bf16[16,128,2048]{2,1,0:T(8,128)(2,1)}) fusion(bf16[16,128,4096]{2,1,0:T(8,128)(2,1)} %all-to-all-done), kind=kLoop, calls=%fused_computation.73 | loop fusion | bytes 33554432 | tf_op jit(solution)/shard_map/slice | solution.py:44
  370.2 7.6 %gather_fusion.2 = bf16[12,128,2048]{2,1,0:T(8,128)(2,1)} fusion(bf16[16,128,2048]{2,1,0:T(8,128)(2,1)} %get-tuple-element.9, s32[1024]{0:T(1024)S(1)} %pad_clamp_fusion), kind=kCustom, calls=%fused_computation.1.clone | custom fusion | bytes 12582960 | tf_op jit(solution)/shard_map/jit(_take)/gather | solution.py:47
  377.8 7.6 %gather_fusion.3 = bf16[12,128,2048]{2,1,0:T(8,128)(2,1)} fusion(bf16[16,128,2048]{2,1,0:T(8,128)(2,1)} %get-tuple-element.10, s32[1024]{0:T(1024)S(1)} %pad_clamp_fusion), kind=kCustom, calls=%fused_computation.3.clone | custom fusion | bytes 12582960 | tf_op jit(solution)/shard_map/jit(_take)/gather | solution.py:46
  385.4 5.5 broadcast_select_fusion.1
  390.9 4.9 copy.77
  395.8 5.0 copy.78
  400.8 9.4 %copy.63 = bf16[6,256,16,128]{1,3,2,0:T(8,128)(2,1)} copy(bf16[6,256,16,128]{3,2,1,0:T(8,128)(2,1)} %bitcast.98) | data formatting | bytes 12582912 | tf_op jit(solution)/shard_map/reshape | solution.py:46
  410.2 10.2 %fusion.20 = f32[6,16,256,128]{3,2,1,0:T(8,128)} fusion(bf16[6,256,16,128]{1,3,2,0:T(8,128)(2,1)} %copy.63, bf16[6,128,16,128]{3,2,1,0:T(8,128)(2,1)} %bitcast.108), kind=kOutput, calls=%fused_computation.39 | convolution fusion | flops 805306368 | bytes 22020096 | tf_op jit(solution)/shard_map/qrhd,qkhd->qhrk/dot_general | solution.py:49
  420.4 16.0 %fusion.54 = (f32[6,16,128]{2,1,0:T(8,128)S(1)}, f32[6,16,128,256]{2,3,1,0:T(8,128)}) fusion(f32[6,16,256,128]{3,2,1,0:T(8,128)} %fusion.20), kind=kOutput, calls=%fused_computation.74 | output fusion | flops 12583167 | bytes 25214976 | tf_op jit(solution)/shard_map/sub | solution.py:16
  436.4 12.9 %multiply_reduce_fusion = (f32[6,16,128]{2,1,0:T(8,128)S(1)}, bf16[6,16,128,128]{3,2,1,0:T(8,128)(2,1)}) fusion(f32[6,16,128,128]{2,3,1,0:T(8,128)} %copy.75, f32[6,16,128,256]{2,3,1,0:T(8,128)} %get-tuple-element.16, f32[6,16,128]{2,1,0:T(8,128)S(1)} %get-tuple-element.15, bf16[6,256,16,128]{3,2,1,0:T(8,128)(2,1)} %bitcast.99), kind=kOutput, calls=%fused_computation.16 | convolution fusion | flops 817876992 | bytes 28409856 | tf_op jit(solution)/shard_map/qhrk,qkhd->qrhd/dot_general | solution.py:53
  449.4 6.4 copy.66
  455.8 7.8 %reshape_reshape.3 = bf16[768,8,16,16]{0,3,2,1:T(8,128)(2,1)} reshape(bf16[6,128,16,128]{1,0,3,2:T(8,128)(2,1)} %copy.66) | data formatting | bytes 6291456 | tf_op jit(solution)/shard_map/reshape;reshape | solution.py:85
  466.5 9.2 %convolution_convert_fusion = bf16[2048,2048]{1,0:T(8,128)(2,1)} fusion(bf16[768,2048]{0,1:T(8,128)(2,1)S(1)} %bitcast.112, bf16[1,768,2048]{2,1,0:T(8,128)(2,1)S(1)} %copy-done.9), kind=kOutput, calls=%fused_computation.14 | convolution fusion | flops 6446645248 | bytes 14680064 | tf_op jit(solution)/shard_map/dot_general | solution.py:89
  475.7 9.1 %fusion.12 = f32[6,16,128,256]{2,3,1,0:T(8,128)} fusion(bf16[6,256,16,128]{3,2,1,0:T(8,128)(2,1)} %bitcast.100, bf16[6,128,16,128]{3,2,1,0:T(8,128)(2,1)S(1)} %bitcast.97), kind=kOutput, calls=%fused_computation.27 | convolution fusion | flops 805306368 | bytes 22020096 | tf_op jit(solution)/shard_map/qrhd,qkhd->qhrk/dot_general | solution.py:99
  484.8 96.4 %reduce-scatter.3.cloned.1.call-done = bf16[128,2048]{1,0:T(8,128)(2,1)} async-done(((bf16[2048,2048]{1,0:T(8,128)(2,1)}), bf16[128,2048]{1,0:T(8,128)(2,1)}) %reduce-scatter.3.cloned.1.call-update) | async-done | bytes 524304 | tf_op jit(solution)/shard_map/reduce_scatter | solution.py:92
  581.3 14.2 %fusion.14 = bf16[6,128,16,128]{1,3,2,0:T(8,128)(2,1)} fusion(bf16[6,256,16,128]{1,3,2,0:T(8,128)(2,1)} %copy.63, f32[6,16,128,256]{2,3,1,0:T(8,128)} %fusion.12, f32[6,16,128]{2,1,0:T(8,128)S(1)} %get-tuple-element.17, f32[6,16,128,256]{2,3,1,0:T(8,128)} %get-tuple-element.16, f32[6,16,128]{2,1,0:T(8,128)S(1)} %get-tuple-element.15), kind=kOutput, calls=%fused_computation.31 | convolution fusion | flops 821035008 | bytes 34701312 | tf_op jit(solution)/shard_map/qhrk,qkhd->qrhd/dot_general | solution.py:107
  598.7 3.8 copy.65
  605.9 10.9 %reduce-scatter.5.cloned.1.call-done = bf16[16,2048]{1,0:T(8,128)(2,1)} async-done(((bf16[128,2048]{1,0:T(8,128)(2,1)}), bf16[16,2048]{1,0:T(8,128)(2,1)}) %reduce-scatter.5.cloned.1.call-update) | async-done | bytes 65552 | tf_op jit(solution)/shard_map/reduce_scatter | solution.py:93
  616.9 6.7 fusion.39
  623.6 5.8 fusion.42
  631.3 36.9 %all-gather.6.cloned.1.call-done = bf16[256,2048]{1,0:T(8,128)(2,1)} async-done(((bf16[16,2048]{1,0:T(8,128)(2,1)}), bf16[256,2048]{1,0:T(8,128)(2,1)}) %all-gather.6.cloned.1.call-update) | async-done | bytes 1048592 | tf_op jit(solution)/shard_map/all_gather | solution.py:94
  (59 shorter events, 30.5 us)
Async XLA Ops:
  7.2 28.0 %copy-start = (bf16[1,768,2048]{2,1,0:T(8,128)(2,1)S(1)}, bf16[1,768,2048]{2,1,0:T(8,128)(2,1)}, u32[]{:S(2)}) copy-start(bf16[1,768,2048]{2,1,0:T(8,128)(2,1)} %param.12) | copy-start | bytes 9437188
  60.4 263.9 %copy-start.5 = (s32[1,6,2]{1,2,0:T(2,128)S(1)}, s32[1,6,2]{1,2,0:T(2,128)}, u32[]{:S(2)}) copy-start(s32[1,6,2]{1,2,0:T(2,128)} %param.15) | copy-start | bytes 148
  60.4 264.3 %copy-start.3 = (bf16[1,768,2048]{2,1,0:T(8,128)(2,1)S(1)}, bf16[1,768,2048]{2,1,0:T(8,128)(2,1)}, u32[]{:S(2)}) copy-start(bf16[1,768,2048]{2,1,0:T(8,128)(2,1)} %param.10) | copy-start | bytes 9437188
  60.4 297.9 %all-to-all-start = ((bf16[16,128,4096]{2,1,0:T(8,128)(2,1)}), bf16[16,128,4096]{2,1,0:T(8,128)(2,1)}, u32[]{:S(2)}, u32[]{:S(2)}) async-start(bf16[16,128,4096]{2,1,0:T(8,128)(2,1)} %pad_maximum_fusion), calls=%async_computation | async-start | bytes 33554432 | tf_op jit(solution)/shard_map/all_to_all | solution.py:41
  65.7 258.1 %all-gather.4.cloned.1.call-start = ((), (), s32[]{:S(2)}) async-start(), calls=%async_computation.3 | async-start | bytes 4718592 | tf_op jit(solution)/shard_map/all_gather | solution.py:64
  67.7 513.5 %reduce-scatter.3.cloned.1.call-start = ((), (), s32[]{:S(2)}) async-start(), calls=%async_computation.4 | async-start | bytes 8912896 | tf_op jit(solution)/shard_map/reduce_scatter | solution.py:92
  323.8 7.6 %collective-permute-start = (bf16[2048,1024]{1,0:T(8,128)(2,1)}, bf16[2048,1024]{1,0:T(8,128)(2,1)}, u32[]{:S(2)}, u32[]{:S(2)}) collective-permute-start(bf16[2048,1024]{1,0:T(8,128)(2,1)} %all-gather.4.cloned.1.call-done), channel_id=1, source_target_pairs={{0,1},{1,0},{2,3},{3,2},{4,5},{5,4},{6,7},{7,6},{8,9},{9,8},{10,11... | collective-permute-start | bytes 12582920 | tf_op jit(solution)/shard_map/ppermute | solution.py:67
  324.7 6.7 copy-start.6
  331.4 5.2 copy-start.8
  463.7 2.8 copy-start.9
  475.7 141.1 %reduce-scatter.5.cloned.1.call-start = ((), (), s32[]{:S(2)}) async-start(), calls=%async_computation.5 | async-start | bytes 589824 | tf_op jit(solution)/shard_map/reduce_scatter | solution.py:93
  581.2 87.0 %all-gather.6.cloned.1.call-start = ((), (), s32[]{:S(2)}) async-start(), calls=%async_computation.6 | async-start | bytes 1114112 | tf_op jit(solution)/shard_map/all_gather | solution.py:94
  581.3 14.2 %copy-start.2 = (bf16[6,16,128,128]{3,2,1,0:T(8,128)(2,1)S(1)}, bf16[6,16,128,128]{3,2,1,0:T(8,128)(2,1)}, u32[]{:S(2)}) copy-start(bf16[6,16,128,128]{3,2,1,0:T(8,128)(2,1)} %get-tuple-element.18) | copy-start | bytes 9437188
  616.9 6.8 copy-start.4
  616.9 6.8 copy-start.7
  623.6 47.4 %copy-start.1 = (bf16[1,768,2048]{2,1,0:T(8,128)(2,1)S(1)}, bf16[1,768,2048]{2,1,0:T(8,128)(2,1)}, u32[]{:S(2)}) copy-start(bf16[1,768,2048]{2,1,0:T(8,128)(2,1)} %param.12) | copy-start | bytes 9437188
Sparse Core Ops, SparseCore 0:
  68.8 254.9 all-gather.3
  475.8 105.3 reduce-scatter.2
  583.6 33.1 reduce-scatter.4
  619.1 49.0 all-gather.5

commit v3 on v2

--- a/solution.py
+++ b/solution.py
@@ -33,13 +33,15 @@
     every_table = lax.all_gather(table, "ctx", axis=0, tiled=True).reshape(ctx_count, blocks * KSEL)
     wanted = every_table // blocks == own_index
     send_index = jnp.sum(jnp.where(wanted, every_table % blocks, 0), axis=1)
-    send_flag = jnp.any(wanted, axis=1)
-    flag = send_flag[:, None, None]
-    empty = jnp.zeros((), jnp.bfloat16)
-    send_keys = jnp.where(flag, jnp.take(key_blocks, send_index, axis=0), empty)
-    send_values = jnp.where(flag, jnp.take(value_blocks, send_index, axis=0), empty)
     got = lax.all_to_all(
-        jnp.concatenate([send_keys, send_values], axis=-1), "ctx", split_axis=0, concat_axis=0, tiled=True
+        jnp.concatenate(
+            [jnp.take(key_blocks, send_index, axis=0), jnp.take(value_blocks, send_index, axis=0)],
+            axis=-1,
+        ),
+        "ctx",
+        split_axis=0,
+        concat_axis=0,
+        tiled=True,
     )
     got_keys, got_values = got[..., :width], got[..., width:]
     order = owner.reshape(-1)
@@ -61,9 +63,15 @@
     grad_flat = grad_out[0]
     half = out_weight.shape[1] // 2
     side = own_index % 2
-    mine = lax.all_gather(
-        lax.dynamic_slice_in_dim(out_weight, side * half, half, axis=1), "dp", axis=0, tiled=True
-    )
+    own_half = lax.dynamic_slice_in_dim(out_weight, side * half, half, axis=1)
+    own_half, attention_flat = lax.optimization_barrier((own_half, attention_flat))
+    mine = lax.all_to_all(
+        jnp.broadcast_to(own_half[None], (data_count,) + own_half.shape),
+        "dp",
+        split_axis=0,
+        concat_axis=0,
+        tiled=True,
+    ).reshape(data_count * own_half.shape[0], half)
     other = lax.ppermute(mine, "ctx", [(j, j ^ 1) for j in range(ctx_count)])
     first = jnp.where(side == 0, mine, other)
     second = jnp.where(side == 0, other, mine)
@@ -90,11 +98,11 @@
         columns, grad_flat, (((0,), (0,)), ((), ())), preferred_element_type=jnp.float32
     )
     stage = lax.psum_scatter(partial.astype(jnp.bfloat16), "ctx", scatter_dimension=0, tiled=True)
-    shard = lax.psum_scatter(stage.astype(jnp.float32), "dp", scatter_dimension=0, tiled=True)
-    weight_sum = lax.all_gather(shard.astype(jnp.bfloat16), "ctx", axis=0, tiled=True).astype(
+    stage = stage.astype(jnp.float32) * (1.0 / math.sqrt(rows * ctx_count * data_count))
+    shard = lax.psum_scatter(stage, "dp", scatter_dimension=0, tiled=True).reshape(split, width)
+    weight_grad = lax.all_gather(shard.astype(jnp.bfloat16), "ctx", axis=0, tiled=True).astype(
         jnp.float32
     )
-    weight_grad = weight_sum / math.sqrt(rows * ctx_count * data_count)
     back_rows = back.reshape(blocks, BLK, HEADS, DH)
     dprobs = jnp.einsum(
         "qrhd,qkhd->qhrk", back_rows, picked_values, preferred_element_type=jnp.float32

time: 687 us -> 623 us (0.907)
  waiting for transfers between devices: 404 us -> 285 us
  blocking collectives: 26.6 us -> 79.9 us
  other arithmetic: 43.6 us -> 52 us
    all_gather x1 -> x0, waiting for transfers between devices: 256 us -> none  [local(): lax.all_gather(lax.dynamic_slice_in_dim(out_weight, side * half, half, ax...]
    all_to_all x1, waiting for transfers between devices: 0.01 us -> 219 us  [local(): lax.all_to_all(jnp.concatenate([jnp.take(key_blocks, send_index, axis=0),...]
    reduce_scatter x1, waiting for transfers between devices: 96.4 us -> 11.6 us  [local(): lax.psum_scatter(partial.astype(jnp.bfloat16), 'ctx', scatter_dimension=0...]
    all_to_all x0 -> x1, blocking collectives: none -> 53.3 us  [local(): lax.all_to_all(jnp.broadcast_to(own_half[None], (data_count,) + own_half....]
    another operation x1 -> x0, local copies, waits for them, and re-layouts: 7.85 us -> none  [local(): attention_flat.reshape(rows, data_count, ctx_count, split)]
    unnamed x26 -> x29, local copies, waits for them, and re-layouts: 23.5 us -> 27.9 us
  transfers between devices with their start and end apart: 6 -> 5, of which waited for: 5 -> 5; matrix products, arithmetic and copies ran while one was open for 12% -> 14% of each run, Pallas kernels for 0% -> 0%
where the time goes in v3:
time: 623 us; the launch traced here: 615 us
  waiting for transfers between devices  285 us (46%)
  local copies, waits for them, and re-layouts  101 us (16%)
  blocking collectives  79.9 us (13%)
  matrix products  74.1 us (12%)
  other arithmetic  52 us (8%)
  between operations  14.5 us (2%)
  starting transfers between devices  8.55 us (1%)
    all_to_all x1, waiting for transfers between devices, local(): lax.all_to_all(jnp.concatenate([jnp.take(key_blocks, send_index, axis=0),...  219 us
    all_to_all x1, blocking collectives, local(): lax.all_to_all(jnp.broadcast_to(own_half[None], (data_count,) + own_half....  53.3 us
    all_gather x1, waiting for transfers between devices, local(): lax.all_gather(shard.astype(jnp.bfloat16), 'ctx', axis=0, tiled=True)  36.9 us
    unnamed x29, local copies, waits for them, and re-layouts  27.9 us
    all_gather x1, blocking collectives, local(): lax.all_gather(table, 'ctx', axis=0, tiled=True)  26.6 us
    sub x1, other arithmetic, softmax_rows(): weights = jnp.exp(scores - top)  16 us
    dot_general x1, matrix products, local(): jnp.einsum('qhrk,qkhd->qrhd', dscores, picked_keys, preferred_element_typ...  14.1 us
  transfers between devices with their start and end apart: 5, of which 5 were waited for; matrix products, arithmetic and copies ran while one was open for 14% of the time, Pallas kernels for 0%

profile of v3, /device:TPU:1, one launch (start us, length us, event | category | flops | bytes accessed | tf_op | source)
XLA Modules:
  0.0 615.4 jit_solution(1808132028703950878)
XLA Ops:
  8.1 26.6 %all-gather = s32[1,96,2]{2,0,1:T(1,128)S(1)} all-gather(s32[1,6,2]{2,0,1:T(1,128)S(1)} %copy.50), channel_id=2, replica_groups=mesh['dp'=8,'ctx'=16] {'ctx'}, dimensions={1}, use_global_device_ids=true | all-gather | bytes 816 | tf_op jit(solution)/shard_map/all_gather | solution.py:33
  39.8 6.7 %gather_fusion = bf16[16,128,2048]{2,1,0:T(8,128)(2,1)} fusion(bf16[6,128,2048]{2,1,0:T(8,128)(2,1)} %bitcast.82, s32[1024]{0:T(1024)S(1)} %pad_clamp_fusion.1), kind=kCustom, calls=%fused_computation.clone | custom fusion | bytes 16777280 | tf_op jit(solution)/shard_map/jit(_take)/gather | solution.py:38
  46.5 6.8 %broadcast_select_fusion.1 = (bf16[16,128,2048]{2,1,0:T(8,128)(2,1)S(1)}, bf16[16,128,2048]{2,1,0:T(8,128)(2,1)S(1)}) fusion(bf16[16,128,2048]{2,1,0:T(8,128)(2,1)} %gather_fusion, pred[16]{0:T(512)(128)(4,1)S(1)} %compare_and_fusion.1, bf16[16,128,2048]{2,1,0:T(8,128)(2,1)} %gather_fusion.1), kind=kLoop, calls=%fused_computation.13 | loop fusion | flops 8388608 | bytes 33554448 | tf_op jit(solution)/shard_map/jit(_take)/select_n | solution.py:38
  53.3 6.9 %pad_maximum_fusion = bf16[16,128,4096]{2,1,0:T(8,128)(2,1)} fusion(bf16[16,128,2048]{2,1,0:T(8,128)(2,1)S(1)} %get-tuple-element.16, bf16[16,128,2048]{2,1,0:T(8,128)(2,1)S(1)} %get-tuple-element.15), kind=kLoop, calls=%fused_computation.5 | loop fusion | flops 33554432 | bytes 33554432 | tf_op jit(solution)/shard_map/concatenate | solution.py:37
  60.1 5.2 all-to-all-start
  70.7 218.7 %all-to-all-done = bf16[16,128,4096]{2,1,0:T(8,128)(2,1)} async-done(((bf16[16,128,4096]{2,1,0:T(8,128)(2,1)}), bf16[16,128,4096]{2,1,0:T(8,128)(2,1)}, u32[]{:S(2)}, u32[]{:S(2)}) %all-to-all-start) | async-done | bytes 16777248 | tf_op jit(solution)/shard_map/all_to_all | solution.py:36
  289.4 11.9 %fusion.33 = (bf16[16,128,2048]{2,1,0:T(8,128)(2,1)}, bf16[16,128,2048]{2,1,0:T(8,128)(2,1)}) fusion(bf16[16,128,4096]{2,1,0:T(8,128)(2,1)} %all-to-all-done), kind=kLoop, calls=%fused_computation.65 | loop fusion | bytes 33554432 | tf_op jit(solution)/shard_map/slice | solution.py:46
  301.2 7.6 %gather_fusion.2 = bf16[12,128,2048]{2,1,0:T(8,128)(2,1)} fusion(bf16[16,128,2048]{2,1,0:T(8,128)(2,1)} %get-tuple-element.11, s32[1024]{0:T(1024)S(1)} %pad_clamp_fusion), kind=kCustom, calls=%fused_computation.1.clone | custom fusion | bytes 12582960 | tf_op jit(solution)/shard_map/jit(_take)/gather | solution.py:49
  308.8 7.6 %gather_fusion.3 = bf16[12,128,2048]{2,1,0:T(8,128)(2,1)} fusion(bf16[16,128,2048]{2,1,0:T(8,128)(2,1)} %get-tuple-element.12, s32[1024]{0:T(1024)S(1)} %pad_clamp_fusion), kind=kCustom, calls=%fused_computation.3.clone | custom fusion | bytes 12582960 | tf_op jit(solution)/shard_map/jit(_take)/gather | solution.py:48
  316.4 5.5 broadcast_select_fusion.3
  321.9 4.9 copy.77
  326.8 5.0 copy.78
  331.8 9.3 %copy.63 = bf16[6,256,16,128]{1,3,2,0:T(8,128)(2,1)} copy(bf16[6,256,16,128]{3,2,1,0:T(8,128)(2,1)} %bitcast.77) | data formatting | bytes 12582912 | tf_op jit(solution)/shard_map/reshape | solution.py:48
  341.1 9.3 %fusion.16 = f32[6,16,256,128]{3,2,1,0:T(8,128)} fusion(bf16[6,256,16,128]{1,3,2,0:T(8,128)(2,1)} %copy.63, bf16[6,128,16,128]{3,2,1,0:T(8,128)(2,1)S(1)} %bitcast.90), kind=kOutput, calls=%fused_computation.36 | convolution fusion | flops 805306368 | bytes 22020096 | tf_op jit(solution)/shard_map/qrhd,qkhd->qhrk/dot_general | solution.py:51
  350.3 16.0 %fusion.34 = (f32[6,16,128]{2,1,0:T(8,128)S(1)}, f32[6,16,128,256]{2,3,1,0:T(8,128)}) fusion(f32[6,16,256,128]{3,2,1,0:T(8,128)} %fusion.16), kind=kOutput, calls=%fused_computation.66 | output fusion | flops 12583167 | bytes 25214976 | tf_op jit(solution)/shard_map/sub | solution.py:16
  366.4 9.2 %fusion.19 = bf16[6,16,128,128]{3,2,1,0:T(8,128)(2,1)S(1)} fusion(f32[6,16,128,256]{2,3,1,0:T(8,128)} %get-tuple-element.18, f32[6,16,128]{2,1,0:T(8,128)S(1)} %get-tuple-element.17, bf16[6,256,16,128]{3,2,1,0:T(8,128)(2,1)} %bitcast.78), kind=kOutput, calls=%fused_computation.39 | convolution fusion | flops 813170688 | bytes 22069248 | tf_op jit(solution)/shard_map/qhrk,qkhd->qrhd/dot_general | solution.py:55
  388.4 9.4 %convolution_convert_fusion = bf16[2048,2048]{1,0:T(8,128)(2,1)} fusion(bf16[768,2048]{0,1:T(8,128)(2,1)S(1)} %bitcast.92, bf16[1,768,2048]{2,1,0:T(8,128)(2,1)S(1)} %copy-done.8), kind=kOutput, calls=%fused_computation.14 | convolution fusion | flops 6446645248 | bytes 14680064 | tf_op jit(solution)/shard_map/dot_general | solution.py:97
  399.4 53.3 %all_to_all.10 = bf16[8,256,1024]{2,1,0:T(8,128)(2,1)} all-to-all(bf16[8,256,1024]{2,1,0:T(8,128)(2,1)S(1)} %broadcast_in_dim.30), channel_id=1, replica_groups=mesh['dp'=8,'ctx'=16] {'dp'}, dimensions={0} | all-to-all | bytes 8388608 | tf_op jit(solution)/shard_map/all_to_all | solution.py:68
  455.7 7.1 %collective-permute-done = bf16[2048,1024]{1,0:T(8,128)(2,1)} collective-permute-done((bf16[2048,1024]{1,0:T(8,128)(2,1)}, bf16[2048,1024]{1,0:T(8,128)(2,1)}, u32[]{:S(2)}, u32[]{:S(2)}) %collective-permute-start) | collective-permute-done | bytes 4194336 | tf_op jit(solution)/shard_map/ppermute | solution.py:75
  462.8 5.5 fusion.24
  468.3 6.0 fusion.18
  483.3 6.6 %copy.75 = f32[6,16,128,128]{2,3,1,0:T(8,128)} copy(f32[6,16,128,128]{3,1,2,0:T(8,128)} %bitcast_convert_fusion) | data formatting | bytes 12582912
  489.9 5.0 multiply_reduce_fusion
  494.9 9.1 %fusion.12 = f32[6,16,128,256]{2,3,1,0:T(8,128)} fusion(bf16[6,256,16,128]{3,2,1,0:T(8,128)(2,1)} %bitcast.79, bf16[6,128,16,128]{3,2,1,0:T(8,128)(2,1)S(1)} %bitcast.76), kind=kOutput, calls=%fused_computation.27 | convolution fusion | flops 805306368 | bytes 22020096 | tf_op jit(solution)/shard_map/qrhd,qkhd->qhrk/dot_general | solution.py:107
  503.9 11.6 %reduce-scatter.3.cloned.1.call-done = bf16[128,2048]{1,0:T(8,128)(2,1)} async-done(((bf16[2048,2048]{1,0:T(8,128)(2,1)}), bf16[128,2048]{1,0:T(8,128)(2,1)}) %reduce-scatter.3.cloned.1.call-update) | async-done | bytes 524304 | tf_op jit(solution)/shard_map/reduce_scatter | solution.py:100
  518.0 14.1 %fusion.14 = bf16[6,128,16,128]{1,3,2,0:T(8,128)(2,1)} fusion(bf16[6,256,16,128]{1,3,2,0:T(8,128)(2,1)} %copy.63, f32[6,16,128,256]{2,3,1,0:T(8,128)} %fusion.12, f32[6,16,128]{2,1,0:T(8,128)S(1)} %multiply_reduce_fusion, f32[6,16,128,256]{2,3,1,0:T(8,128)} %get-tuple-element.18, f32[6,16,128]{2,1,0:T(8,128)S(1)} %get-tuple-element.17), kind=kOutput, calls=%fused_computation.31 | convolution fusion | flops 821035008 | bytes 34701312 | tf_op jit(solution)/shard_map/qhrk,qkhd->qrhd/dot_general | solution.py:115
  532.1 5.1 copy.65
  537.1 5.8 broadcast_in_dim_reshape.3
  542.9 10.6 %reduce-scatter.5.cloned.1.call-done = f32[16,2048]{1,0:T(8,128)} async-done(((f32[128,2048]{1,0:T(8,128)}), f32[16,2048]{1,0:T(8,128)}) %reduce-scatter.5.cloned.1.call-update) | async-done | bytes 131088 | tf_op jit(solution)/shard_map/reduce_scatter | solution.py:102
  555.1 5.8 fusion.28
  560.9 5.8 fusion.27
  568.7 36.9 %all-gather.3.cloned.1.call-done = bf16[256,2048]{1,0:T(8,128)(2,1)} async-done(((bf16[16,2048]{1,0:T(8,128)(2,1)}), bf16[256,2048]{1,0:T(8,128)(2,1)}) %all-gather.3.cloned.1.call-update) | async-done | bytes 1048592 | tf_op jit(solution)/shard_map/all_gather | solution.py:103
  (60 shorter events, 46.3 us)
Async XLA Ops:
  7.2 27.9 %copy-start = (bf16[1,768,2048]{2,1,0:T(8,128)(2,1)S(1)}, bf16[1,768,2048]{2,1,0:T(8,128)(2,1)}, u32[]{:S(2)}) copy-start(bf16[1,768,2048]{2,1,0:T(8,128)(2,1)} %param.12) | copy-start | bytes 9437188
  60.1 5.3 copy-start.7
  60.1 229.2 %all-to-all-start = ((bf16[16,128,4096]{2,1,0:T(8,128)(2,1)}), bf16[16,128,4096]{2,1,0:T(8,128)(2,1)}, u32[]{:S(2)}, u32[]{:S(2)}) async-start(bf16[16,128,4096]{2,1,0:T(8,128)(2,1)} %pad_maximum_fusion), calls=%async_computation | async-start | bytes 33554432 | tf_op jit(solution)/shard_map/all_to_all | solution.py:36
  65.4 450.1 %reduce-scatter.3.cloned.1.call-start = ((), (), s32[]{:S(2)}) async-start(), calls=%async_computation.4 | async-start | bytes 8912896 | tf_op jit(solution)/shard_map/reduce_scatter | solution.py:100
  375.6 3.5 copy-start.5
  382.2 5.7 copy-start.2
  385.6 2.8 copy-start.8
  397.8 1.0 copy-start.6
  397.8 155.7 %reduce-scatter.5.cloned.1.call-start = ((), (), s32[]{:S(2)}) async-start(), calls=%async_computation.5 | async-start | bytes 1179648 | tf_op jit(solution)/shard_map/reduce_scatter | solution.py:102
  399.4 63.4 %copy-start.9 = (bf16[1,768,2048]{2,1,0:T(8,128)(2,1)S(1)}, bf16[1,768,2048]{2,1,0:T(8,128)(2,1)}, u32[]{:S(2)}) copy-start(bf16[1,768,2048]{2,1,0:T(8,128)(2,1)} %param.13) | copy-start | bytes 9437188
  452.7 10.1 %collective-permute-start = (bf16[2048,1024]{1,0:T(8,128)(2,1)}, bf16[2048,1024]{1,0:T(8,128)(2,1)}, u32[]{:S(2)}, u32[]{:S(2)}) collective-permute-start(bf16[2048,1024]{1,0:T(8,128)(2,1)} %bitcast.9), channel_id=1, source_target_pairs={{0,1},{1,0},{2,3},{3,2},{4,5},{5,4},{6,7},{7,6},{8,9},{9,8},{10,11... | collective-permute-start | bytes 12582920 | tf_op jit(solution)/shard_map/ppermute | solution.py:75
  462.8 5.5 copy-start.10
  517.6 88.0 %all-gather.3.cloned.1.call-start = ((), (), s32[]{:S(2)}) async-start(), calls=%async_computation.6 | async-start | bytes 1114112 | tf_op jit(solution)/shard_map/all_gather | solution.py:103
  532.1 23.0 %copy-start.3 = (bf16[96,8,16,128]{3,1,2,0:T(8,128)(2,1)S(1)}, bf16[96,8,16,128]{3,1,2,0:T(8,128)(2,1)}, u32[]{:S(2)}) copy-start(bf16[96,8,16,128]{3,1,2,0:T(8,128)(2,1)} %copy-done.2) | copy-start | bytes 9437188
  555.1 5.8 copy-start.4
  560.9 47.5 %copy-start.1 = (bf16[1,768,2048]{2,1,0:T(8,128)(2,1)S(1)}, bf16[1,768,2048]{2,1,0:T(8,128)(2,1)}, u32[]{:S(2)}) copy-start(bf16[1,768,2048]{2,1,0:T(8,128)(2,1)} %param.12) | copy-start | bytes 9437188
Sparse Core Ops, SparseCore 0:
  397.9 117.5 reduce-scatter.2
  518.5 35.0 reduce-scatter.4
  556.5 49.0 all-gather.2

commit v4 on v3

--- a/solution.py
+++ b/solution.py
@@ -3,12 +3,62 @@
 import jax
 import jax.numpy as jnp
 from jax import lax
+from jax.experimental import pallas as pl
+from jax.experimental.pallas import tpu as pltpu
 from jax.sharding import PartitionSpec as P
 
 HEADS = 16
 DH = 128
 BLK = 128
 KSEL = 2
+
+
+def _fwd_kernel(table, q_ref, k0_ref, k1_ref, v0_ref, v1_ref, att_ref, probs_ref):
+    scale = 1.0 / math.sqrt(DH)
+    keys = jnp.concatenate([k0_ref[0], k1_ref[0]], axis=0)
+    scores = lax.dot_general(
+        q_ref[...], keys, (((1,), (1,)), ((), ())), preferred_element_type=jnp.float32
+    ) * scale
+    top = jnp.max(scores, axis=-1, keepdims=True)
+    weights = jnp.exp(scores - top)
+    probs = weights / jnp.sum(weights, axis=-1, keepdims=True)
+    vals = jnp.concatenate([v0_ref[0], v1_ref[0]], axis=0)
+    att = jnp.dot(probs.astype(jnp.bfloat16), vals, preferred_element_type=jnp.float32)
+    att_ref[...] = att.astype(att_ref.dtype)
+    probs_ref[0, 0] = probs
+
+def forward_attention(query_flat, got, order, interpret=False):
+    rows, width = query_flat.shape
+    blocks = rows // BLK
+    heads = width // DH
+    def kv(k, off):
+        return pl.BlockSpec((1, BLK, DH), lambda b, h, t: (t[KSEL * b + k], 0, off + h))
+    grid_spec = pltpu.PrefetchScalarGridSpec(
+        num_scalar_prefetch=1,
+        grid=(blocks, heads),
+        in_specs=[
+            pl.BlockSpec((BLK, DH), lambda b, h, t: (b, h)),
+            kv(0, 0), kv(1, 0), kv(0, heads), kv(1, heads),
+        ],
+        out_specs=[
+            pl.BlockSpec((BLK, DH), lambda b, h, t: (b, h)),
+            pl.BlockSpec((1, 1, BLK, KSEL * BLK), lambda b, h, t: (b, h, 0, 0)),
+        ],
+    )
+    flops = blocks * heads * 4 * BLK * KSEL * BLK * DH
+    return pl.pallas_call(
+        _fwd_kernel,
+        grid_spec=grid_spec,
+        out_shape=[
+            jax.ShapeDtypeStruct((rows, width), jnp.bfloat16),
+            jax.ShapeDtypeStruct((blocks, heads, BLK, KSEL * BLK), jnp.float32),
+        ],
+        cost_estimate=pl.CostEstimate(
+            flops=flops, transcendentals=blocks * heads * BLK * KSEL * BLK,
+            bytes_accessed=rows * width * 2 * 3 + blocks * heads * BLK * KSEL * BLK * 4,
+        ),
+        interpret=interpret,
+    )(order, query_flat, got, got, got, got)
 
 
 def softmax_rows(scores):
@@ -45,21 +95,10 @@
     )
     got_keys, got_values = got[..., :width], got[..., width:]
     order = owner.reshape(-1)
+    attention_flat, probs = forward_attention(queries[0], got, order)
+    attention = attention_flat.reshape(blocks, BLK, HEADS, DH)
     picked_keys = jnp.take(got_keys, order, axis=0).reshape(blocks, KSEL * BLK, HEADS, DH)
     picked_values = jnp.take(got_values, order, axis=0).reshape(blocks, KSEL * BLK, HEADS, DH)
-    scores = (
-        jnp.einsum("qrhd,qkhd->qhrk", query_rows, picked_keys, preferred_element_type=jnp.float32)
-        * scale
-    )
-    probs = softmax_rows(scores)
-    attention = jnp.einsum(
-        "qhrk,qkhd->qrhd",
-        probs.astype(jnp.bfloat16),
-        picked_values,
-        preferred_element_type=jnp.float32,
-    )
-    attention = attention.astype(jnp.bfloat16)
-    attention_flat = attention.reshape(rows, width)
     grad_flat = grad_out[0]
     half = out_weight.shape[1] // 2
     side = own_index % 2
@@ -97,8 +136,8 @@
     partial = lax.dot_general(
         columns, grad_flat, (((0,), (0,)), ((), ())), preferred_element_type=jnp.float32
     )
-    stage = lax.psum_scatter(partial.astype(jnp.bfloat16), "ctx", scatter_dimension=0, tiled=True)
-    stage = stage.astype(jnp.float32) * (1.0 / math.sqrt(rows * ctx_count * data_count))
+    stage = lax.psum_scatter(partial, "ctx", scatter_dimension=0, tiled=True)
+    stage = stage * (1.0 / math.sqrt(rows * ctx_count * data_count))
     shard = lax.psum_scatter(stage, "dp", scatter_dimension=0, tiled=True).reshape(split, width)
     weight_grad = lax.all_gather(shard.astype(jnp.bfloat16), "ctx", axis=0, tiled=True).astype(
         jnp.float32

time: 623 us -> 635 us (1.019)
  Pallas kernels: 0 us -> 66.4 us
  local copies, waits for them, and re-layouts: 101 us -> 76.6 us
  other arithmetic: 52 us -> 30.5 us
  matrix products: 74.1 us -> 54.2 us
  waiting for transfers between devices: 285 us -> 299 us
    pallas_call x0 -> x1, Pallas kernels: none -> 66.4 us  [forward_attention(): pl.pallas_call(_fwd_kernel, grid_spec=grid_spec, out_shape=[jax.ShapeDtyp...]
    reduce_scatter x1, waiting for transfers between devices: 11.6 us -> 36.3 us  [local(): stage = lax.psum_scatter(partial, 'ctx', scatter_dimension=0, tiled=True)]
    dot_general x2 -> x0, matrix products: 18.5 us -> none  [the longest x1 9.25 us: local(): jnp.einsum('qrhd,qkhd->qhrk', query_rows, picked_keys, preferred_element_...]
    sub x1 -> x0, other arithmetic: 16 us -> none  [softmax_rows(): weights = jnp.exp(scores - top)]
    reshape x1 -> x0, local copies, waits for them, and re-layouts: 9.25 us -> none  [local(): jnp.take(got_keys, order, axis=0).reshape(blocks, KSEL * BLK, HEADS, DH)]
    unnamed x29 -> x31, local copies, waits for them, and re-layouts: 27.9 us -> 19.3 us
    reduce_scatter x1, waiting for transfers between devices: 10.6 us -> 3.35 us  [local(): lax.psum_scatter(stage, 'dp', scatter_dimension=0, tiled=True)]
    ppermute x1, waiting for transfers between devices: 7.13 us -> 0.01 us  [local(): other = lax.ppermute(mine, 'ctx', [(j, j ^ 1) for j in range(ctx_count)])]
  transfers between devices with their start and end apart: 5 -> 5, of which waited for: 5 -> 4; matrix products, arithmetic and copies ran while one was open for 14% -> 18% of each run, Pallas kernels for 0% -> 0%
where the time goes in v4:
time: 635 us; the launch traced here: 627 us
  waiting for transfers between devices  299 us (47%)
  blocking collectives  79.7 us (13%)
  local copies, waits for them, and re-layouts  76.6 us (12%)
  Pallas kernels  66.4 us (10%)
  matrix products  54.2 us (9%)
  other arithmetic  30.5 us (5%)
  between operations  14 us (2%)
  starting transfers between devices  7.15 us (1%)
    all_to_all x1, waiting for transfers between devices, local(): lax.all_to_all(jnp.concatenate([jnp.take(key_blocks, send_index, axis=0),...  222 us
    pallas_call x1, Pallas kernels, forward_attention(): pl.pallas_call(_fwd_kernel, grid_spec=grid_spec, out_shape=[jax.ShapeDtyp...  66.4 us
    all_to_all x1, blocking collectives, local(): lax.all_to_all(jnp.broadcast_to(own_half[None], (data_count,) + own_half....  53.2 us
    all_gather x1, waiting for transfers between devices, local(): lax.all_gather(shard.astype(jnp.bfloat16), 'ctx', axis=0, tiled=True)  36.8 us
    reduce_scatter x1, waiting for transfers between devices, local(): stage = lax.psum_scatter(partial, 'ctx', scatter_dimension=0, tiled=True)  36.3 us
    all_gather x1, blocking collectives, local(): lax.all_gather(table, 'ctx', axis=0, tiled=True)  26.6 us
    unnamed x31, local copies, waits for them, and re-layouts  19.3 us
  transfers between devices with their start and end apart: 5, of which 4 were waited for; matrix products, arithmetic and copies ran while one was open for 18% of the time, Pallas kernels for 0%

profile of v4, /device:TPU:1, one launch (start us, length us, event | category | flops | bytes accessed | tf_op | source)
XLA Modules:
  0.0 627.4 jit_solution(10729206432600985170)
XLA Ops:
  8.1 26.6 %all-gather = s32[1,96,2]{2,0,1:T(1,128)S(1)} all-gather(s32[1,6,2]{2,0,1:T(1,128)S(1)} %copy.34), channel_id=2, replica_groups=mesh['dp'=8,'ctx'=16] {'ctx'}, dimensions={1}, use_global_device_ids=true | all-gather | bytes 816 | tf_op jit(solution)/shard_map/all_gather | solution.py:83
  35.0 4.7 gather_fusion.1
  39.7 6.6 %gather_fusion = bf16[16,128,2048]{2,1,0:T(8,128)(2,1)} fusion(bf16[6,128,2048]{2,1,0:T(8,128)(2,1)} %bitcast.67, s32[1024]{0:T(1024)S(1)} %pad_clamp_fusion.1), kind=kCustom, calls=%fused_computation.clone | custom fusion | bytes 16777280 | tf_op jit(solution)/shard_map/jit(_take)/gather | solution.py:88
  46.3 6.8 %broadcast_select_fusion.1 = (bf16[16,128,2048]{2,1,0:T(8,128)(2,1)S(1)}, bf16[16,128,2048]{2,1,0:T(8,128)(2,1)S(1)}) fusion(bf16[16,128,2048]{2,1,0:T(8,128)(2,1)} %gather_fusion, pred[16]{0:T(512)(128)(4,1)S(1)} %compare_and_fusion.1, bf16[16,128,2048]{2,1,0:T(8,128)(2,1)} %gather_fusion.1), kind=kLoop, calls=%fused_computation.7 | loop fusion | flops 8388608 | bytes 33554448 | tf_op jit(solution)/shard_map/jit(_take)/select_n | solution.py:88
  53.1 6.9 %pad_maximum_fusion = bf16[16,128,4096]{2,1,0:T(8,128)(2,1)} fusion(bf16[16,128,2048]{2,1,0:T(8,128)(2,1)S(1)} %get-tuple-element.20, bf16[16,128,2048]{2,1,0:T(8,128)(2,1)S(1)} %get-tuple-element.19), kind=kLoop, calls=%fused_computation.4 | loop fusion | flops 33554432 | bytes 33554432 | tf_op jit(solution)/shard_map/concatenate | solution.py:87
  60.0 5.2 all-to-all-start
  67.1 222.4 %all-to-all-done.k0_ref.k1_ref.v0_ref.v1_ref = bf16[16,128,4096]{2,1,0:T(8,128)(2,1)} async-done(((bf16[16,128,4096]{2,1,0:T(8,128)(2,1)}), bf16[16,128,4096]{2,1,0:T(8,128)(2,1)}, u32[]{:S(2)}, u32[]{:S(2)}) %all-to-all-start) | async-done | bytes 16777248 | tf_op jit(solution)/shard_map/all_to_all | solution.py:86
  289.4 66.4 %shard_map.85 = (bf16[768,2048]{1,0:T(8,128)(2,1)}, f32[6,16,128,256]{3,2,1,0:T(8,128)}) custom-call(s32[12]{0:T(128)} %get-tuple-element.14.table, bf16[768,2048]{1,0:T(8,128)(2,1)} %bitcast.73, bf16[16,128,4096]{2,1,0:T(8,128)(2,1)} %all-to-all-done.k0_ref.k1_ref.v0_ref.v1_ref, bf16[16,128,4096]{2,1,0:T(8,128)(2,1)} %all-to-all-done.k0_ref.k1_ref.v0_ref.v1_ref, ...), custom_call_target="tpu_custom_call" | custom-call | flops 1610612736 | bytes 22020096 | tf_op jit(solution)/shard_map/pallas_call | solution.py:49
  355.9 3.2 copy.43
  360.9 9.5 %fusion.18 = f32[2048,2048]{1,0:T(8,128)} fusion(bf16[768,2048]{0,1:T(8,128)(2,1)S(1)} %bitcast.72, bf16[1,768,2048]{2,1,0:T(8,128)(2,1)S(1)} %copy-done.11), kind=kOutput, calls=%fused_computation.49 | convolution fusion | flops 6442450944 | bytes 23068672 | tf_op jit(solution)/shard_map/dot_general | solution.py:136
  372.0 53.2 %all_to_all.10 = bf16[8,256,1024]{2,1,0:T(8,128)(2,1)} all-to-all(bf16[8,256,1024]{2,1,0:T(8,128)(2,1)S(1)} %broadcast_in_dim.28), channel_id=1, replica_groups=mesh['dp'=8,'ctx'=16] {'dp'}, dimensions={0} | all-to-all | bytes 8388608 | tf_op jit(solution)/shard_map/all_to_all | solution.py:107
  427.0 12.0 %fusion.20 = (bf16[16,128,2048]{2,1,0:T(8,128)(2,1)}, bf16[16,128,2048]{2,1,0:T(8,128)(2,1)}) fusion(bf16[16,128,4096]{2,1,0:T(8,128)(2,1)} %all-to-all-done.k0_ref.k1_ref.v0_ref.v1_ref), kind=kLoop, calls=%fused_computation.51 | loop fusion | bytes 33554432 | tf_op jit(solution)/shard_map/slice | solution.py:96
  439.0 7.8 %gather_fusion.2 = bf16[12,128,2048]{2,1,0:T(8,128)(2,1)} fusion(bf16[16,128,2048]{2,1,0:T(8,128)(2,1)} %get-tuple-element.15, s32[1024]{0:T(1024)S(1)} %pad_clamp_fusion), kind=kCustom, calls=%fused_computation.1.clone | custom fusion | bytes 12582960 | tf_op jit(solution)/shard_map/jit(_take)/gather | solution.py:100
  446.9 8.1 %gather_fusion.3 = bf16[12,128,2048]{2,1,0:T(8,128)(2,1)} fusion(bf16[16,128,2048]{2,1,0:T(8,128)(2,1)} %get-tuple-element.16, s32[1024]{0:T(1024)S(1)} %pad_clamp_fusion), kind=kCustom, calls=%fused_computation.3.clone | custom fusion | bytes 12582960 | tf_op jit(solution)/shard_map/jit(_take)/gather | solution.py:101
  454.9 5.7 broadcast_select_fusion.3
  460.6 5.0 copy.53
  465.6 5.0 copy.55
  470.6 2.7 copy.56
  473.3 5.3 fusion.11
  478.7 6.1 fusion.8
  484.8 2.9 copy.38
  487.7 3.1 copy.54
  493.3 36.3 %reduce-scatter.3.cloned.1.call-done = f32[128,2048]{1,0:T(8,128)} async-done(((f32[2048,2048]{1,0:T(8,128)}), f32[128,2048]{1,0:T(8,128)}) %reduce-scatter.3.cloned.1.call-update) | async-done | bytes 1048592 | tf_op jit(solution)/shard_map/reduce_scatter | solution.py:139
  532.1 9.1 %fusion.3 = f32[6,16,128,256]{3,2,1,0:T(8,128)} fusion(bf16[6,256,16,128]{3,2,1,0:T(8,128)(2,1)} %bitcast.61, bf16[6,128,16,128]{3,2,1,0:T(8,128)(2,1)S(1)} %bitcast.63), kind=kOutput, calls=%fused_computation.12 | convolution fusion | flops 805306368 | bytes 22020096 | tf_op jit(solution)/shard_map/qrhd,qkhd->qhrk/dot_general | solution.py:146
  541.2 12.5 %fusion.6 = bf16[6,128,16,128]{1,3,2,0:T(8,128)(2,1)S(1)} fusion(f32[6,16,128,256]{3,2,1,0:T(8,128)} %get-tuple-element.12, f32[6,16,128,256]{3,2,1,0:T(8,128)} %fusion.3, f32[6,16,128]{2,1,0:T(8,128)S(1)} %copy-done.8, bf16[6,256,16,128]{3,2,1,0:T(8,128)(2,1)} %bitcast.64), kind=kOutput, calls=%fused_computation.21 | convolution fusion | flops 817889280 | bytes 34652160 | tf_op jit(solution)/shard_map/qhrk,qkhd->qrhd/dot_general | solution.py:154
  553.7 3.2 copy.42
  556.8 5.9 broadcast_in_dim_reshape.3
  562.8 3.4 reduce-scatter.5.cloned.1.call-done
  567.7 5.8 fusion.15
  573.5 5.8 fusion.14
  581.3 36.8 %all-gather.3.cloned.1.call-done = bf16[256,2048]{1,0:T(8,128)(2,1)} async-done(((bf16[16,2048]{1,0:T(8,128)(2,1)}), bf16[256,2048]{1,0:T(8,128)(2,1)}) %all-gather.3.cloned.1.call-update) | async-done | bytes 1048592 | tf_op jit(solution)/shard_map/all_gather | solution.py:142
  618.1 2.8 convert_element_type.35
  (59 shorter events, 16.7 us)
Async XLA Ops:
  7.2 27.9 %copy-start = (bf16[1,768,2048]{2,1,0:T(8,128)(2,1)S(1)}, bf16[1,768,2048]{2,1,0:T(8,128)(2,1)}, u32[]{:S(2)}) copy-start(bf16[1,768,2048]{2,1,0:T(8,128)(2,1)} %param.12) | copy-start | bytes 9437188
  60.0 5.3 copy-start.9
  60.0 5.7 copy-start.7
  60.0 229.4 %all-to-all-start = ((bf16[16,128,4096]{2,1,0:T(8,128)(2,1)}), bf16[16,128,4096]{2,1,0:T(8,128)(2,1)}, u32[]{:S(2)}, u32[]{:S(2)}) async-start(bf16[16,128,4096]{2,1,0:T(8,128)(2,1)} %pad_maximum_fusion), calls=%async_computation | async-start | bytes 33554432 | tf_op jit(solution)/shard_map/all_to_all | solution.py:86
  65.3 464.4 %reduce-scatter.3.cloned.1.call-start = ((), (), s32[]{:S(2)}) async-start(), calls=%async_computation.4 | async-start | bytes 17825792 | tf_op jit(solution)/shard_map/reduce_scatter | solution.py:139
  359.0 1.9 copy-start.11
  370.5 1.0 copy-start.6
  370.5 195.6 %reduce-scatter.5.cloned.1.call-start = ((), (), s32[]{:S(2)}) async-start(), calls=%async_computation.5 | async-start | bytes 1179648 | tf_op jit(solution)/shard_map/reduce_scatter | solution.py:141
  372.0 55.0 %copy-start.10 = (s32[12]{0:T(128)S(1)}, s32[12]{0:T(128)}, u32[]{:S(2)}) copy-start(s32[12]{0:T(128)} %get-tuple-element.14.table) | copy-start | bytes 148
  425.2 48.1 %collective-permute-start = (bf16[2048,1024]{1,0:T(8,128)(2,1)}, bf16[2048,1024]{1,0:T(8,128)(2,1)}, u32[]{:S(2)}, u32[]{:S(2)}) collective-permute-start(bf16[2048,1024]{1,0:T(8,128)(2,1)} %bitcast.8), channel_id=1, source_target_pairs={{0,1},{1,0},{2,3},{3,2},{4,5},{5,4},{6,7},{7,6},{8,9},{9,8},{10,11... | collective-permute-start | bytes 12582920 | tf_op jit(solution)/shard_map/ppermute | solution.py:114
  465.6 5.0 copy-start.2
  470.6 2.7 copy-start.12
  487.7 3.1 copy-start.5
  532.0 86.1 %all-gather.3.cloned.1.call-start = ((), (), s32[]{:S(2)}) async-start(), calls=%async_computation.6 | async-start | bytes 1114112 | tf_op jit(solution)/shard_map/all_gather | solution.py:142
  532.0 9.1 %copy-start.8 = (f32[6,16,128]{2,1,0:T(8,128)S(1)}, f32[6,16,128]{2,1,0:T(8,128)}, u32[]{:S(2)}) copy-start(f32[6,16,128]{2,1,0:T(8,128)} %copy.51) | copy-start | bytes 147460
  556.8 10.9 %copy-start.3 = (bf16[768,2048]{1,0:T(8,128)(2,1)S(1)}, bf16[768,2048]{1,0:T(8,128)(2,1)}, u32[]{:S(2)}) copy-start(bf16[768,2048]{1,0:T(8,128)(2,1)} %get-tuple-element.10) | copy-start | bytes 9437188
  567.7 5.8 copy-start.4
  573.5 47.4 %copy-start.1 = (bf16[1,768,2048]{2,1,0:T(8,128)(2,1)S(1)}, bf16[1,768,2048]{2,1,0:T(8,128)(2,1)}, u32[]{:S(2)}) copy-start(bf16[1,768,2048]{2,1,0:T(8,128)(2,1)} %param.12) | copy-start | bytes 9437188
Sparse Core Ops, SparseCore 0:
  370.6 159.0 reduce-scatter.2
  532.6 33.4 reduce-scatter.4
  569.1 48.9 all-gather.2

commit v5 on v4

--- a/solution.py
+++ b/solution.py
@@ -15,34 +15,42 @@
 
 def _fwd_kernel(table, q_ref, k0_ref, k1_ref, v0_ref, v1_ref, att_ref, probs_ref):
     scale = 1.0 / math.sqrt(DH)
-    keys = jnp.concatenate([k0_ref[0], k1_ref[0]], axis=0)
-    scores = lax.dot_general(
-        q_ref[...], keys, (((1,), (1,)), ((), ())), preferred_element_type=jnp.float32
-    ) * scale
-    top = jnp.max(scores, axis=-1, keepdims=True)
-    weights = jnp.exp(scores - top)
-    probs = weights / jnp.sum(weights, axis=-1, keepdims=True)
-    vals = jnp.concatenate([v0_ref[0], v1_ref[0]], axis=0)
-    att = jnp.dot(probs.astype(jnp.bfloat16), vals, preferred_element_type=jnp.float32)
-    att_ref[...] = att.astype(att_ref.dtype)
-    probs_ref[0, 0] = probs
+    for h in range(HEADS):
+        lanes = slice(h * DH, (h + 1) * DH)
+        keys = jnp.concatenate([k0_ref[0, :, lanes], k1_ref[0, :, lanes]], axis=0)
+        scores = lax.dot_general(
+            q_ref[:, lanes], keys, (((1,), (1,)), ((), ())), preferred_element_type=jnp.float32
+        ) * scale
+        top = jnp.max(scores, axis=-1, keepdims=True)
+        weights = jnp.exp(scores - top)
+        probs = weights / jnp.sum(weights, axis=-1, keepdims=True)
+        vals = jnp.concatenate([v0_ref[0, :, lanes], v1_ref[0, :, lanes]], axis=0)
+        att = jnp.dot(probs.astype(jnp.bfloat16), vals, preferred_element_type=jnp.float32)
+        att_ref[:, lanes] = att.astype(att_ref.dtype)
+        probs_ref[0, h] = probs
 
-def forward_attention(query_flat, got, order, interpret=False):
+
+def forward_attention(query_flat, got, order):
     rows, width = query_flat.shape
     blocks = rows // BLK
     heads = width // DH
+
     def kv(k, off):
-        return pl.BlockSpec((1, BLK, DH), lambda b, h, t: (t[KSEL * b + k], 0, off + h))
+        return pl.BlockSpec((1, BLK, width), lambda b, t: (t[KSEL * b + k], 0, off))
+
     grid_spec = pltpu.PrefetchScalarGridSpec(
         num_scalar_prefetch=1,
-        grid=(blocks, heads),
+        grid=(blocks,),
         in_specs=[
-            pl.BlockSpec((BLK, DH), lambda b, h, t: (b, h)),
-            kv(0, 0), kv(1, 0), kv(0, heads), kv(1, heads),
+            pl.BlockSpec((BLK, width), lambda b, t: (b, 0)),
+            kv(0, 0),
+            kv(1, 0),
+            kv(0, 1),
+            kv(1, 1),
         ],
         out_specs=[
-            pl.BlockSpec((BLK, DH), lambda b, h, t: (b, h)),
-            pl.BlockSpec((1, 1, BLK, KSEL * BLK), lambda b, h, t: (b, h, 0, 0)),
+            pl.BlockSpec((BLK, width), lambda b, t: (b, 0)),
+            pl.BlockSpec((1, heads, BLK, KSEL * BLK), lambda b, t: (b, 0, 0, 0)),
         ],
     )
     flops = blocks * heads * 4 * BLK * KSEL * BLK * DH
@@ -54,10 +62,10 @@
             jax.ShapeDtypeStruct((blocks, heads, BLK, KSEL * BLK), jnp.float32),
         ],
         cost_estimate=pl.CostEstimate(
-            flops=flops, transcendentals=blocks * heads * BLK * KSEL * BLK,
-            bytes_accessed=rows * width * 2 * 3 + blocks * heads * BLK * KSEL * BLK * 4,
+            flops=flops,
+            transcendentals=blocks * heads * BLK * KSEL * BLK,
+            bytes_accessed=rows * width * 2 * 6 + blocks * heads * BLK * KSEL * BLK * 4,
         ),
-        interpret=interpret,
     )(order, query_flat, got, got, got, got)
 
 
@@ -138,10 +146,20 @@
     )
     stage = lax.psum_scatter(partial, "ctx", scatter_dimension=0, tiled=True)
     stage = stage * (1.0 / math.sqrt(rows * ctx_count * data_count))
-    shard = lax.psum_scatter(stage, "dp", scatter_dimension=0, tiled=True).reshape(split, width)
-    weight_grad = lax.all_gather(shard.astype(jnp.bfloat16), "ctx", axis=0, tiled=True).astype(
-        jnp.float32
+    shard = jnp.sum(
+        lax.all_to_all(
+            stage.reshape(data_count, split, width), "dp", split_axis=0, concat_axis=0, tiled=True
+        ),
+        axis=0,
     )
+    piece = shard.astype(jnp.bfloat16)
+    weight_grad = lax.all_to_all(
+        jnp.broadcast_to(piece[None], (ctx_count,) + piece.shape),
+        "ctx",
+        split_axis=0,
+        concat_axis=0,
+        tiled=True,
+    ).reshape(ctx_count * split, width).astype(jnp.float32)
     back_rows = back.reshape(blocks, BLK, HEADS, DH)
     dprobs = jnp.einsum(
         "qrhd,qkhd->qhrk", back_rows, picked_values, preferred_element_type=jnp.float32

time: 635 us -> 537 us (0.85)
  waiting for transfers between devices: 299 us -> 244 us
  Pallas kernels: 66.4 us -> 15.7 us
  starting transfers between devices: 7.15 us -> 17.4 us
    pallas_call x1, Pallas kernels: 66.4 us -> 15.7 us  [forward_attention(): pl.pallas_call(_fwd_kernel, grid_spec=grid_spec, out_shape=[jax.ShapeDtyp...]
    all_gather x1 -> x0, waiting for transfers between devices: 36.8 us -> none  [local(): lax.all_gather(shard.astype(jnp.bfloat16), 'ctx', axis=0, tiled=True)]
    reduce_scatter x1, waiting for transfers between devices: 36.3 us -> 5.33 us  [local(): stage = lax.psum_scatter(partial, 'ctx', scatter_dimension=0, tiled=True)]
    all_to_all x0 -> x2, waiting for transfers between devices: none -> 16.6 us  [the longest x1 8.76 us: local(): lax.all_to_all(jnp.broadcast_to(piece[None], (ctx_count,) + piece.shape),...]
    all_to_all x0 -> x2, starting transfers between devices: none -> 10.3 us  [the longest x1 6.07 us: local(): lax.all_to_all(jnp.broadcast_to(piece[None], (ctx_count,) + piece.shape),...]
  transfers between devices with their start and end apart: 5 -> 5, of which waited for: 4 -> 4; matrix products, arithmetic and copies ran while one was open for 18% -> 22% of each run, Pallas kernels for 0% -> 0%
where the time goes in v5:
time: 537 us; the launch traced here: 536 us
  waiting for transfers between devices  244 us (45%)
  blocking collectives  79.7 us (15%)
  local copies, waits for them, and re-layouts  77.7 us (14%)
  matrix products  56.7 us (11%)
  other arithmetic  30.2 us (6%)
  starting transfers between devices  17.4 us (3%)
  Pallas kernels  15.7 us (3%)
  between operations  14.3 us (3%)
    all_to_all x1, waiting for transfers between devices, local(): lax.all_to_all(jnp.concatenate([jnp.take(key_blocks, send_index, axis=0),...  222 us
    all_to_all x1, blocking collectives, local(): lax.all_to_all(jnp.broadcast_to(own_half[None], (data_count,) + own_half....  53.2 us
    all_gather x1, blocking collectives, local(): lax.all_gather(table, 'ctx', axis=0, tiled=True)  26.6 us
    unnamed x31, local copies, waits for them, and re-layouts  19.2 us
    pallas_call x1, Pallas kernels, forward_attention(): pl.pallas_call(_fwd_kernel, grid_spec=grid_spec, out_shape=[jax.ShapeDtyp...  15.7 us
    dot_general x1, matrix products, local(): jnp.einsum('qhrk,qkhd->qrhd', dscores, picked_keys, preferred_element_typ...  13.1 us
    slice x1, local copies, waits for them, and re-layouts, local(): got_keys, got_values = (got[..., :width], got[..., width:])  12 us
  transfers between devices with their start and end apart: 5, of which 4 were waited for; matrix products, arithmetic and copies ran while one was open for 22% of the time, Pallas kernels for 0%

profile of v5, /device:TPU:1, one launch (start us, length us, event | category | flops | bytes accessed | tf_op | source)
XLA Modules:
  0.0 535.7 jit_solution(16724544198797965716)
XLA Ops:
  8.1 26.6 %all-gather = s32[1,96,2]{2,0,1:T(1,128)S(1)} all-gather(s32[1,6,2]{2,0,1:T(1,128)S(1)} %copy.34), channel_id=2, replica_groups=mesh['dp'=8,'ctx'=16] {'ctx'}, dimensions={1}, use_global_device_ids=true | all-gather | bytes 816 | tf_op jit(solution)/shard_map/all_gather | solution.py:91
  35.0 4.7 gather_fusion.1
  39.8 6.6 %gather_fusion = bf16[16,128,2048]{2,1,0:T(8,128)(2,1)} fusion(bf16[6,128,2048]{2,1,0:T(8,128)(2,1)} %bitcast.71, s32[1024]{0:T(1024)S(1)} %pad_clamp_fusion.1), kind=kCustom, calls=%fused_computation.clone | custom fusion | bytes 16777280 | tf_op jit(solution)/shard_map/jit(_take)/gather | solution.py:96
  46.4 6.8 %broadcast_select_fusion.1 = (bf16[16,128,2048]{2,1,0:T(8,128)(2,1)S(1)}, bf16[16,128,2048]{2,1,0:T(8,128)(2,1)S(1)}) fusion(bf16[16,128,2048]{2,1,0:T(8,128)(2,1)} %gather_fusion, pred[16]{0:T(512)(128)(4,1)S(1)} %compare_and_fusion.1, bf16[16,128,2048]{2,1,0:T(8,128)(2,1)} %gather_fusion.1), kind=kLoop, calls=%fused_computation.7 | loop fusion | flops 8388608 | bytes 33554448 | tf_op jit(solution)/shard_map/jit(_take)/select_n | solution.py:96
  53.2 6.8 %pad_maximum_fusion = bf16[16,128,4096]{2,1,0:T(8,128)(2,1)} fusion(bf16[16,128,2048]{2,1,0:T(8,128)(2,1)S(1)} %get-tuple-element.20, bf16[16,128,2048]{2,1,0:T(8,128)(2,1)S(1)} %get-tuple-element.19), kind=kLoop, calls=%fused_computation.4 | loop fusion | flops 33554432 | bytes 33554432 | tf_op jit(solution)/shard_map/concatenate | solution.py:95
  60.1 5.2 all-to-all-start
  67.1 222.2 %all-to-all-done.k0_ref.k1_ref.v0_ref.v1_ref = bf16[16,128,4096]{2,1,0:T(8,128)(2,1)} async-done(((bf16[16,128,4096]{2,1,0:T(8,128)(2,1)}), bf16[16,128,4096]{2,1,0:T(8,128)(2,1)}, u32[]{:S(2)}, u32[]{:S(2)}) %all-to-all-start) | async-done | bytes 16777248 | tf_op jit(solution)/shard_map/all_to_all | solution.py:94
  289.3 15.7 %shard_map.85 = (bf16[768,2048]{1,0:T(8,128)(2,1)}, f32[6,16,128,256]{3,2,1,0:T(8,128)}) custom-call(s32[12]{0:T(128)} %get-tuple-element.14.table, bf16[768,2048]{1,0:T(8,128)(2,1)} %bitcast.78, bf16[16,128,4096]{2,1,0:T(8,128)(2,1)} %all-to-all-done.k0_ref.k1_ref.v0_ref.v1_ref, bf16[16,128,4096]{2,1,0:T(8,128)(2,1)} %all-to-all-done.k0_ref.k1_ref.v0_ref.v1_ref, ...), custom_call_target="tpu_custom_call" | custom-call | flops 1610612736 | bytes 31457280 | tf_op jit(solution)/shard_map/pallas_call | solution.py:57
  304.9 3.2 copy.43
  310.0 9.5 %fusion.18 = f32[2048,2048]{1,0:T(8,128)} fusion(bf16[768,2048]{0,1:T(8,128)(2,1)S(1)} %bitcast.77, bf16[1,768,2048]{2,1,0:T(8,128)(2,1)S(1)} %copy-done.11), kind=kOutput, calls=%fused_computation.50 | convolution fusion | flops 6442450944 | bytes 23068672 | tf_op jit(solution)/shard_map/dot_general | solution.py:144
  321.1 53.2 %all_to_all.20 = bf16[8,256,1024]{2,1,0:T(8,128)(2,1)} all-to-all(bf16[8,256,1024]{2,1,0:T(8,128)(2,1)S(1)} %broadcast_in_dim.34), channel_id=1, replica_groups=mesh['dp'=8,'ctx'=16] {'dp'}, dimensions={0} | all-to-all | bytes 8388608 | tf_op jit(solution)/shard_map/all_to_all | solution.py:115
  376.1 12.0 %fusion.20 = (bf16[16,128,2048]{2,1,0:T(8,128)(2,1)}, bf16[16,128,2048]{2,1,0:T(8,128)(2,1)}) fusion(bf16[16,128,4096]{2,1,0:T(8,128)(2,1)} %all-to-all-done.k0_ref.k1_ref.v0_ref.v1_ref), kind=kLoop, calls=%fused_computation.52 | loop fusion | bytes 33554432 | tf_op jit(solution)/shard_map/slice | solution.py:104
  388.1 7.8 %gather_fusion.2 = bf16[12,128,2048]{2,1,0:T(8,128)(2,1)} fusion(bf16[16,128,2048]{2,1,0:T(8,128)(2,1)} %get-tuple-element.15, s32[1024]{0:T(1024)S(1)} %pad_clamp_fusion), kind=kCustom, calls=%fused_computation.1.clone | custom fusion | bytes 12582960 | tf_op jit(solution)/shard_map/jit(_take)/gather | solution.py:108
  395.9 8.0 %gather_fusion.3 = bf16[12,128,2048]{2,1,0:T(8,128)(2,1)} fusion(bf16[16,128,2048]{2,1,0:T(8,128)(2,1)} %get-tuple-element.16, s32[1024]{0:T(1024)S(1)} %pad_clamp_fusion), kind=kCustom, calls=%fused_computation.3.clone | custom fusion | bytes 12582960 | tf_op jit(solution)/shard_map/jit(_take)/gather | solution.py:109
  404.0 5.7 %broadcast_select_fusion.3 = (bf16[12,128,2048]{2,1,0:T(8,128)(2,1)S(1)}, bf16[12,128,2048]{2,1,0:T(8,128)(2,1)S(1)}) fusion(bf16[12,128,2048]{2,1,0:T(8,128)(2,1)} %gather_fusion.2, pred[12]{0:T(512)(128)(4,1)S(1)} %get-tuple-element.13, bf16[12,128,2048]{2,1,0:T(8,128)(2,1)} %gather_fusion.3), kind=kLoop, calls=%fused_computation.18 | loop fusion | flops 6291456 | bytes 25165836 | tf_op jit(solution)/shard_map/jit(_take)/select_n | solution.py:108
  409.7 4.9 copy.53
  414.6 4.9 copy.55
  422.3 5.3 fusion.11
  427.6 6.2 %fusion.8 = bf16[768,2048]{0,1:T(8,128)(2,1)S(1)} fusion(f32[2048,768]{1,0:T(8,128)S(1)} %fusion.11, bf16[2048,1024]{1,0:T(8,128)(2,1)} %bitcast.8, bf16[2048,1024]{1,0:T(8,128)(2,1)} %collective-permute-done, pred[]{:T(512)S(6)} %eq.17, bf16[768,2048]{1,0:T(8,128)(2,1)S(1)} %bitcast.80), kind=kOutput, calls=%fused_computation.25 | convolution fusion | flops 3226468352 | bytes 19398656 | tf_op jit(solution)/shard_map/dot_general | solution.py:133
  433.8 2.9 copy.38
  436.6 3.1 copy.54
  442.3 9.1 %fusion.3 = f32[6,16,128,256]{3,2,1,0:T(8,128)} fusion(bf16[6,256,16,128]{3,2,1,0:T(8,128)(2,1)} %bitcast.65, bf16[6,128,16,128]{3,2,1,0:T(8,128)(2,1)S(1)} %bitcast.67), kind=kOutput, calls=%fused_computation.12 | convolution fusion | flops 805306368 | bytes 22020096 | tf_op jit(solution)/shard_map/qrhd,qkhd->qhrk/dot_general | solution.py:164
  451.4 13.1 %fusion.6 = bf16[6,128,16,128]{1,3,2,0:T(8,128)(2,1)S(1)} fusion(f32[6,16,128,256]{3,2,1,0:T(8,128)} %get-tuple-element.12, f32[6,16,128,256]{3,2,1,0:T(8,128)} %fusion.3, f32[6,16,128]{2,1,0:T(8,128)S(1)} %copy-done.8, bf16[6,256,16,128]{3,2,1,0:T(8,128)(2,1)} %bitcast.68), kind=kOutput, calls=%fused_computation.21 | convolution fusion | flops 817889280 | bytes 34652160 | tf_op jit(solution)/shard_map/qhrk,qkhd->qrhd/dot_general | solution.py:172
  464.5 3.2 copy.42
  467.8 6.0 %broadcast_in_dim_reshape.3 = bf16[1,768,2048]{2,1,0:T(8,128)(2,1)} reshape(bf16[6,128,16,128]{3,2,1,0:T(8,128)(2,1)} %copy.42) | data formatting | bytes 6291456 | tf_op jit(solution)/shard_map/broadcast_in_dim;reshape | solution.py:176
  473.8 5.3 reduce-scatter.2.cloned.1.call-done
  481.4 4.2 all-to-all-start.2
  485.6 6.7 %fusion.15 = bf16[1,768,1024]{2,1,0:T(8,128)(2,1)} fusion(bf16[768,2048]{1,0:T(8,128)(2,1)S(1)} %copy-done.3, bf16[2048,1024]{1,0:T(8,128)(2,1)} %collective-permute-done, bf16[2048,1024]{1,0:T(8,128)(2,1)} %bitcast.8, pred[]{:T(512)S(6)} %eq.17), kind=kOutput, calls=%fused_computation.32 | convolution fusion | flops 3224109056 | bytes 13107201 | tf_op jit(solution)/shard_map/dot_general | solution.py:128
  492.4 7.8 %all-to-all-done.2 = f32[8,16,2048]{2,1,0:T(8,128)} async-done(((f32[8,16,2048]{2,1,0:T(8,128)}), f32[8,16,2048]{2,1,0:T(8,128)}, u32[]{:S(2)}, u32[]{:S(2)}) %all-to-all-start.2) | async-done | bytes 1048608 | tf_op jit(solution)/shard_map/all_to_all | solution.py:150
  502.6 6.1 %all-to-all-start.3 = ((bf16[16,16,2048]{2,1,0:T(8,128)(2,1)}), bf16[16,16,2048]{2,1,0:T(8,128)(2,1)}, u32[]{:S(2)}, u32[]{:S(2)}) async-start(bf16[16,16,2048]{2,1,0:T(8,128)(2,1)} %broadcast_in_dim.35), calls=%async_computation.4 | async-start | bytes 2097152 | tf_op jit(solution)/shard_map/all_to_all | solution.py:156
  508.7 6.7 %fusion.14 = bf16[1,768,1024]{2,1,0:T(8,128)(2,1)S(1)} fusion(bf16[768,2048]{1,0:T(8,128)(2,1)} %get-tuple-element.10, bf16[2048,1024]{1,0:T(8,128)(2,1)} %bitcast.8, bf16[2048,1024]{1,0:T(8,128)(2,1)} %collective-permute-done, pred[]{:T(512)S(6)} %eq.17), kind=kOutput, calls=%fused_computation.31 | convolution fusion | flops 3224109056 | bytes 13107201 | tf_op jit(solution)/shard_map/dot_general | solution.py:127
  517.3 8.8 %all-to-all-done.3 = bf16[16,16,2048]{2,1,0:T(8,128)(2,1)} async-done(((bf16[16,16,2048]{2,1,0:T(8,128)(2,1)}), bf16[16,16,2048]{2,1,0:T(8,128)(2,1)}, u32[]{:S(2)}, u32[]{:S(2)}) %all-to-all-start.3) | async-done | bytes 1048608 | tf_op jit(solution)/shard_map/all_to_all | solution.py:156
  (58 shorter events, 23.0 us)
Async XLA Ops:
  7.2 27.9 %copy-start = (bf16[1,768,2048]{2,1,0:T(8,128)(2,1)S(1)}, bf16[1,768,2048]{2,1,0:T(8,128)(2,1)}, u32[]{:S(2)}) copy-start(bf16[1,768,2048]{2,1,0:T(8,128)(2,1)} %param.12) | copy-start | bytes 9437188
  60.1 5.3 copy-start.9
  60.1 5.7 %copy-start.7 = (bf16[256,2048]{1,0:T(8,128)(2,1)S(1)}, bf16[256,2048]{1,0:T(8,128)(2,1)}, u32[]{:S(2)}) copy-start(bf16[256,2048]{1,0:T(8,128)(2,1)} %param.14) | copy-start | bytes 3145732
  60.1 229.2 %all-to-all-start = ((bf16[16,128,4096]{2,1,0:T(8,128)(2,1)}), bf16[16,128,4096]{2,1,0:T(8,128)(2,1)}, u32[]{:S(2)}, u32[]{:S(2)}) async-start(bf16[16,128,4096]{2,1,0:T(8,128)(2,1)} %pad_maximum_fusion), calls=%async_computation | async-start | bytes 33554432 | tf_op jit(solution)/shard_map/all_to_all | solution.py:94
  65.3 413.8 %reduce-scatter.2.cloned.1.call-start = ((), (), s32[]{:S(2)}) async-start(), calls=%async_computation.5 | async-start | bytes 17825792 | tf_op jit(solution)/shard_map/reduce_scatter | solution.py:147
  308.1 1.9 copy-start.11
  319.5 1.0 copy-start.5
  321.1 55.0 %copy-start.10 = (s32[12]{0:T(128)S(1)}, s32[12]{0:T(128)}, u32[]{:S(2)}) copy-start(s32[12]{0:T(128)} %get-tuple-element.14.table) | copy-start | bytes 148
  374.3 47.9 %collective-permute-start = (bf16[2048,1024]{1,0:T(8,128)(2,1)}, bf16[2048,1024]{1,0:T(8,128)(2,1)}, u32[]{:S(2)}, u32[]{:S(2)}) collective-permute-start(bf16[2048,1024]{1,0:T(8,128)(2,1)} %bitcast.8), channel_id=1, source_target_pairs={{0,1},{1,0},{2,3},{3,2},{4,5},{5,4},{6,7},{7,6},{8,9},{9,8},{10,11... | collective-permute-start | bytes 12582920 | tf_op jit(solution)/shard_map/ppermute | solution.py:122
  414.6 4.9 copy-start.2
  419.6 2.7 copy-start.12
  436.6 3.1 copy-start.4
  442.3 9.1 %copy-start.8 = (f32[6,16,128]{2,1,0:T(8,128)S(1)}, f32[6,16,128]{2,1,0:T(8,128)}, u32[]{:S(2)}) copy-start(f32[6,16,128]{2,1,0:T(8,128)} %copy.51) | copy-start | bytes 147460
  467.8 17.9 %copy-start.3 = (bf16[768,2048]{1,0:T(8,128)(2,1)S(1)}, bf16[768,2048]{1,0:T(8,128)(2,1)}, u32[]{:S(2)}) copy-start(bf16[768,2048]{1,0:T(8,128)(2,1)} %get-tuple-element.10) | copy-start | bytes 9437188
  481.4 18.8 %all-to-all-start.2 = ((f32[8,16,2048]{2,1,0:T(8,128)}), f32[8,16,2048]{2,1,0:T(8,128)}, u32[]{:S(2)}, u32[]{:S(2)}) async-start(f32[8,16,2048]{2,1,0:T(8,128)} %bitcast.76), calls=%async_computation.3 | async-start | bytes 2097152 | tf_op jit(solution)/shard_map/all_to_all | solution.py:150
  502.6 23.5 %all-to-all-start.3 = ((bf16[16,16,2048]{2,1,0:T(8,128)(2,1)}), bf16[16,16,2048]{2,1,0:T(8,128)(2,1)}, u32[]{:S(2)}, u32[]{:S(2)}) async-start(bf16[16,16,2048]{2,1,0:T(8,128)(2,1)} %broadcast_in_dim.35), calls=%async_computation.4 | async-start | bytes 2097152 | tf_op jit(solution)/shard_map/all_to_all | solution.py:156
  508.6 6.7 %copy-start.6 = (bf16[1,768,1024]{2,1,0:T(8,128)(2,1)S(1)}, bf16[1,768,1024]{2,1,0:T(8,128)(2,1)}, u32[]{:S(2)}) copy-start(bf16[1,768,1024]{2,1,0:T(8,128)(2,1)} %fusion.15) | copy-start | bytes 4718596
  508.6 20.3 %copy-start.1 = (bf16[1,768,2048]{2,1,0:T(8,128)(2,1)S(1)}, bf16[1,768,2048]{2,1,0:T(8,128)(2,1)}, u32[]{:S(2)}) copy-start(bf16[1,768,2048]{2,1,0:T(8,128)(2,1)} %param.12) | copy-start | bytes 9437188
Sparse Core Ops, SparseCore 0:
  319.7 159.3 reduce-scatter.1

commit v6 on v5

--- a/solution.py
+++ b/solution.py
@@ -69,6 +69,32 @@
     )(order, query_flat, got, got, got, got)
 
 
+def _send_kernel(index, k_ref, v_ref, o_ref):
+    width = k_ref.shape[-1]
+    o_ref[0, :, :width] = k_ref[0]
+    o_ref[0, :, width:] = v_ref[0]
+
+
+def send_buffer(key_blocks, value_blocks, send_index):
+    count = send_index.shape[0]
+    _, blk, width = key_blocks.shape
+    grid_spec = pltpu.PrefetchScalarGridSpec(
+        num_scalar_prefetch=1,
+        grid=(count,),
+        in_specs=[
+            pl.BlockSpec((1, blk, width), lambda d, t: (t[d], 0, 0)),
+            pl.BlockSpec((1, blk, width), lambda d, t: (t[d], 0, 0)),
+        ],
+        out_specs=pl.BlockSpec((1, blk, 2 * width), lambda d, t: (d, 0, 0)),
+    )
+    return pl.pallas_call(
+        _send_kernel,
+        grid_spec=grid_spec,
+        out_shape=jax.ShapeDtypeStruct((count, blk, 2 * width), key_blocks.dtype),
+        cost_estimate=pl.CostEstimate(flops=0, transcendentals=0, bytes_accessed=count * blk * width * 8),
+    )(send_index, key_blocks, value_blocks)
+
+
 def softmax_rows(scores):
     top = jnp.max(scores, axis=-1, keepdims=True)
     weights = jnp.exp(scores - top)
@@ -88,14 +114,18 @@
     value_blocks = values[0].reshape(blocks, BLK, width)
     table = pattern[0]
     owner = table // blocks
-    every_table = lax.all_gather(table, "ctx", axis=0, tiled=True).reshape(ctx_count, blocks * KSEL)
+    flat_table = table.reshape(1, blocks * KSEL)
+    every_table = lax.all_to_all(
+        jnp.broadcast_to(flat_table, (ctx_count, blocks * KSEL)),
+        "ctx",
+        split_axis=0,
+        concat_axis=0,
+        tiled=True,
+    )
     wanted = every_table // blocks == own_index
     send_index = jnp.sum(jnp.where(wanted, every_table % blocks, 0), axis=1)
     got = lax.all_to_all(
-        jnp.concatenate(
-            [jnp.take(key_blocks, send_index, axis=0), jnp.take(value_blocks, send_index, axis=0)],
-            axis=-1,
-        ),
+        send_buffer(key_blocks, value_blocks, send_index),
         "ctx",
         split_axis=0,
         concat_axis=0,

time: 537 us -> 527 us (0.981)
  blocking collectives: 79.7 us -> 54 us
  Pallas kernels: 15.7 us -> 32.5 us
  other arithmetic: 30.2 us -> 15.2 us
  starting transfers between devices: 17.4 us -> 28.8 us
  local copies, waits for them, and re-layouts: 77.7 us -> 71.5 us
    all_gather x1 -> x0, blocking collectives: 26.6 us -> none  [local(): lax.all_gather(table, 'ctx', axis=0, tiled=True)]
    pallas_call x0 -> x1, Pallas kernels: none -> 16.8 us  [send_buffer(): pl.pallas_call(_send_kernel, grid_spec=grid_spec, out_shape=jax.ShapeDtyp...]
    gather x2 -> x0, local copies, waits for them, and re-layouts: 11.4 us -> none  [the longest x1 6.62 us: local(): jnp.take(key_blocks, send_index, axis=0)]
    all_to_all x1 -> x2, starting transfers between devices: 5.19 us -> 14.7 us  [the longest x1 9.12 us: local(): lax.all_to_all(jnp.broadcast_to(flat_table, (ctx_count, blocks * KSEL)),...]
    all_to_all x1 -> x2, waiting for transfers between devices: 222 us -> 230 us  [the longest x1 224 us: local(): lax.all_to_all(send_buffer(key_blocks, value_blocks, send_index), 'ctx',...]
    concatenate x1 -> x0, other arithmetic: 6.85 us -> none  [local(): jnp.concatenate([jnp.take(key_blocks, send_index, axis=0), jnp.take(value...]
    select_n x2 -> x0, other arithmetic: 6.82 us -> none  [local(): jnp.take(key_blocks, send_index, axis=0)]
    unnamed x31 -> x23, local copies, waits for them, and re-layouts: 19.2 us -> 18.6 us
  transfers between devices with their start and end apart: 5 -> 6, of which waited for: 4 -> 4; matrix products, arithmetic and copies ran while one was open for 22% -> 23% of each run, Pallas kernels for 0% -> 0%
where the time goes in v6:
time: 527 us; the launch traced here: 526 us
  waiting for transfers between devices  248 us (47%)
  local copies, waits for them, and re-layouts  71.5 us (14%)
  matrix products  61.5 us (12%)
  blocking collectives  54 us (10%)
  Pallas kernels  32.5 us (6%)
  starting transfers between devices  28.8 us (5%)
  other arithmetic  15.2 us (3%)
  between operations  14.2 us (3%)
    all_to_all x1, waiting for transfers between devices, local(): lax.all_to_all(send_buffer(key_blocks, value_blocks, send_index), 'ctx',...  224 us
    all_to_all x1, blocking collectives, local(): lax.all_to_all(jnp.broadcast_to(own_half[None], (data_count,) + own_half....  54 us
    unnamed x23, local copies, waits for them, and re-layouts  18.6 us
    pallas_call x1, Pallas kernels, send_buffer(): pl.pallas_call(_send_kernel, grid_spec=grid_spec, out_shape=jax.ShapeDtyp...  16.8 us
    pallas_call x1, Pallas kernels, forward_attention(): pl.pallas_call(_fwd_kernel, grid_spec=grid_spec, out_shape=[jax.ShapeDtyp...  15.7 us
    dot_general x1, matrix products, local(): jnp.einsum('qhrk,qkhd->qrhd', dscores, picked_keys, preferred_element_typ...  14.2 us
    slice x1, local copies, waits for them, and re-layouts, local(): got_keys, got_values = (got[..., :width], got[..., width:])  12 us
  transfers between devices with their start and end apart: 6, of which 4 were waited for; matrix products, arithmetic and copies ran while one was open for 23% of the time, Pallas kernels for 0%

profile of v6, /device:TPU:1, one launch (start us, length us, event | category | flops | bytes accessed | tf_op | source)
XLA Modules:
  0.0 525.5 jit_solution(3770855006281168168)
XLA Ops:
  8.7 9.1 %all-to-all-start = ((s32[16,1,12]{2,1,0:T(1,128)}), s32[16,1,12]{2,1,0:T(1,128)S(1)}, u32[]{:S(2)}, u32[]{:S(2)}) async-start(s32[16,1,12]{2,1,0:T(1,128)} %broadcast_in_dim.17), calls=%async_computation | async-start | bytes 16384 | tf_op jit(solution)/shard_map/all_to_all | solution.py:118
  17.8 6.9 %all-to-all-done = s32[16,1,12]{2,1,0:T(1,128)S(1)} async-done(((s32[16,1,12]{2,1,0:T(1,128)}), s32[16,1,12]{2,1,0:T(1,128)S(1)}, u32[]{:S(2)}, u32[]{:S(2)}) %all-to-all-start) | async-done | bytes 800 | tf_op jit(solution)/shard_map/all_to_all | solution.py:118
  26.1 16.8 %shard_map.85 = bf16[16,128,4096]{2,1,0:T(8,128)(2,1)} custom-call(s32[16]{0:T(128)} %fusion.18.index, bf16[6,128,2048]{2,1,0:T(8,128)(2,1)} %bitcast.86, bf16[6,128,2048]{2,1,0:T(8,128)(2,1)} %bitcast.87), custom_call_target="tpu_custom_call" | custom-call | bytes 33554432 | tf_op jit(solution)/shard_map/pallas_call | solution.py:90
  42.9 5.6 %all-to-all-start.1 = ((bf16[16,128,4096]{2,1,0:T(8,128)(2,1)}), bf16[16,128,4096]{2,1,0:T(8,128)(2,1)}, u32[]{:S(2)}, u32[]{:S(2)}) async-start(bf16[16,128,4096]{2,1,0:T(8,128)(2,1)} %shard_map.85), calls=%async_computation.1 | async-start | bytes 33554432 | tf_op jit(solution)/shard_map/all_to_all | solution.py:127
  49.1 223.5 %all-to-all-done.1.k0_ref.k1_ref.v0_ref.v1_ref = bf16[16,128,4096]{2,1,0:T(8,128)(2,1)} async-done(((bf16[16,128,4096]{2,1,0:T(8,128)(2,1)}), bf16[16,128,4096]{2,1,0:T(8,128)(2,1)}, u32[]{:S(2)}, u32[]{:S(2)}) %all-to-all-start.1) | async-done | bytes 16777248 | tf_op jit(solution)/shard_map/all_to_all | solution.py:127
  272.7 15.7 %shard_map.86 = (bf16[768,2048]{1,0:T(8,128)(2,1)}, f32[6,16,128,256]{3,2,1,0:T(8,128)}) custom-call(s32[12]{0:T(128)} %get-tuple-element.13.table, bf16[768,2048]{1,0:T(8,128)(2,1)} %bitcast.89, bf16[16,128,4096]{2,1,0:T(8,128)(2,1)} %all-to-all-done.1.k0_ref.k1_ref.v0_ref.v1_ref, bf16[16,128,4096]{2,1,0:T(8,128)(2,1)} %all-to-all-done.1.k0_ref.k1_ref.v0_ref.v1_ref, ...), custom_call_target="tpu_custom_call" | custom-call | flops 1610612736 | bytes 31457280 | tf_op jit(solution)/shard_map/pallas_call | solution.py:57
  288.3 4.6 copy.40
  293.0 2.4 copy.41
  295.8 9.5 %fusion.22 = f32[2048,2048]{1,0:T(8,128)} fusion(bf16[768,2048]{0,1:T(8,128)(2,1)S(1)} %bitcast.88, bf16[1,768,2048]{2,1,0:T(8,128)(2,1)S(1)} %copy-done.7), kind=kOutput, calls=%fused_computation.46 | convolution fusion | flops 6442450944 | bytes 23068672 | tf_op jit(solution)/shard_map/dot_general | solution.py:174
  305.9 54.0 %all_to_all.26 = bf16[8,256,1024]{2,1,0:T(8,128)(2,1)} all-to-all(bf16[8,256,1024]{2,1,0:T(8,128)(2,1)S(1)} %broadcast_in_dim.18), channel_id=1, replica_groups=mesh['dp'=8,'ctx'=16] {'dp'}, dimensions={0} | all-to-all | bytes 8388608 | tf_op jit(solution)/shard_map/all_to_all | solution.py:145
  361.7 12.0 %fusion.24 = (bf16[16,128,2048]{2,1,0:T(8,128)(2,1)}, bf16[16,128,2048]{2,1,0:T(8,128)(2,1)}) fusion(bf16[16,128,4096]{2,1,0:T(8,128)(2,1)} %all-to-all-done.1.k0_ref.k1_ref.v0_ref.v1_ref), kind=kLoop, calls=%fused_computation.48 | loop fusion | bytes 33554432 | tf_op jit(solution)/shard_map/slice | solution.py:134
  373.7 7.9 %gather_fusion = bf16[12,128,2048]{2,1,0:T(8,128)(2,1)} fusion(bf16[16,128,2048]{2,1,0:T(8,128)(2,1)} %get-tuple-element.14, s32[1024]{0:T(1024)S(1)} %pad_clamp_fusion), kind=kCustom, calls=%fused_computation.clone | custom fusion | bytes 12582960 | tf_op jit(solution)/shard_map/jit(_take)/gather | solution.py:138
  381.5 8.1 %gather_fusion.1 = bf16[12,128,2048]{2,1,0:T(8,128)(2,1)} fusion(bf16[16,128,2048]{2,1,0:T(8,128)(2,1)} %get-tuple-element.15, s32[1024]{0:T(1024)S(1)} %pad_clamp_fusion), kind=kCustom, calls=%fused_computation.1.clone | custom fusion | bytes 12582960 | tf_op jit(solution)/shard_map/jit(_take)/gather | solution.py:139
  389.6 5.7 %broadcast_select_fusion.1 = (bf16[12,128,2048]{2,1,0:T(8,128)(2,1)S(1)}, bf16[12,128,2048]{2,1,0:T(8,128)(2,1)S(1)}) fusion(bf16[12,128,2048]{2,1,0:T(8,128)(2,1)} %gather_fusion, pred[12]{0:T(512)(128)(4,1)S(1)} %get-tuple-element.12, bf16[12,128,2048]{2,1,0:T(8,128)(2,1)} %gather_fusion.1), kind=kLoop, calls=%fused_computation.13 | loop fusion | flops 6291456 | bytes 25165836 | tf_op jit(solution)/shard_map/jit(_take)/select_n | solution.py:138
  395.3 4.9 copy.50
  400.2 4.9 copy.52
  405.2 2.7 copy.53
  407.9 5.3 %fusion.11 = f32[2048,768]{1,0:T(8,128)S(1)} fusion(bf16[2048,1024]{1,0:T(8,128)(2,1)} %collective-permute-done, bf16[2048,1024]{1,0:T(8,128)(2,1)} %bitcast.11, pred[]{:T(512)S(6)} %eq.16, bf16[768,2048]{1,0:T(8,128)(2,1)S(1)} %bitcast.93), kind=kOutput, calls=%fused_computation.23 | convolution fusion | flops 3223322624 | bytes 16252929 | tf_op jit(solution)/shard_map/dot_general | solution.py:165
  413.2 7.8 %fusion.8 = bf16[768,2048]{0,1:T(8,128)(2,1)} fusion(f32[2048,768]{1,0:T(8,128)S(1)} %fusion.11, bf16[2048,1024]{1,0:T(8,128)(2,1)} %bitcast.11, bf16[2048,1024]{1,0:T(8,128)(2,1)} %collective-permute-done, pred[]{:T(512)S(6)} %eq.16, bf16[768,2048]{1,0:T(8,128)(2,1)S(1)} %bitcast.94), kind=kOutput, calls=%fused_computation.20 | convolution fusion | flops 3226468352 | bytes 19398656 | tf_op jit(solution)/shard_map/dot_general | solution.py:163
  421.0 4.8 copy.35
  425.8 3.0 copy.51
  432.4 10.4 %fusion.3 = f32[6,16,128,256]{3,2,1,0:T(8,128)} fusion(bf16[6,256,16,128]{3,2,1,0:T(8,128)(2,1)} %bitcast.76, bf16[6,128,16,128]{3,2,1,0:T(8,128)(2,1)} %bitcast.78), kind=kOutput, calls=%fused_computation.7 | convolution fusion | flops 805306368 | bytes 22020096 | tf_op jit(solution)/shard_map/qrhd,qkhd->qhrk/dot_general | solution.py:194
  442.7 14.2 %fusion.6 = bf16[6,128,16,128]{1,3,2,0:T(8,128)(2,1)} fusion(f32[6,16,128,256]{3,2,1,0:T(8,128)} %get-tuple-element.11, f32[6,16,128,256]{3,2,1,0:T(8,128)} %fusion.3, f32[6,16,128]{2,1,0:T(8,128)S(1)} %copy.48, bf16[6,256,16,128]{3,2,1,0:T(8,128)(2,1)} %bitcast.79), kind=kOutput, calls=%fused_computation.16 | convolution fusion | flops 817889280 | bytes 34652160 | tf_op jit(solution)/shard_map/qhrk,qkhd->qrhd/dot_general | solution.py:202
  456.9 4.9 copy.39
  461.8 5.8 %broadcast_in_dim_reshape.3 = bf16[1,768,2048]{2,1,0:T(8,128)(2,1)} reshape(bf16[6,128,16,128]{3,2,1,0:T(8,128)(2,1)} %copy.39) | data formatting | bytes 6291456 | tf_op jit(solution)/shard_map/broadcast_in_dim;reshape | solution.py:206
  467.6 2.3 broadcast_multiply_fusion
  469.9 4.4 all-to-all-start.3
  474.3 7.7 %fusion.15 = bf16[1,768,1024]{2,1,0:T(8,128)(2,1)} fusion(bf16[768,2048]{1,0:T(8,128)(2,1)} %get-tuple-element.9, bf16[2048,1024]{1,0:T(8,128)(2,1)} %collective-permute-done, bf16[2048,1024]{1,0:T(8,128)(2,1)} %bitcast.11, pred[]{:T(512)S(6)} %eq.16), kind=kOutput, calls=%fused_computation.27 | convolution fusion | flops 3224109056 | bytes 13107201 | tf_op jit(solution)/shard_map/dot_general | solution.py:158
  482.0 8.7 %all-to-all-done.3 = f32[8,16,2048]{2,1,0:T(8,128)S(1)} async-done(((f32[8,16,2048]{2,1,0:T(8,128)}), f32[8,16,2048]{2,1,0:T(8,128)S(1)}, u32[]{:S(2)}, u32[]{:S(2)}) %all-to-all-start.3) | async-done | bytes 1048608 | tf_op jit(solution)/shard_map/all_to_all | solution.py:180
  491.9 7.8 %all-to-all-start.4 = ((bf16[16,16,2048]{2,1,0:T(8,128)(2,1)}), bf16[16,16,2048]{2,1,0:T(8,128)(2,1)S(1)}, u32[]{:S(2)}, u32[]{:S(2)}) async-start(bf16[16,16,2048]{2,1,0:T(8,128)(2,1)} %broadcast_in_dim.19), calls=%async_computation.5 | async-start | bytes 2097152 | tf_op jit(solution)/shard_map/all_to_all | solution.py:186
  499.8 6.7 %fusion.14 = bf16[1,768,1024]{2,1,0:T(8,128)(2,1)S(1)} fusion(bf16[768,2048]{1,0:T(8,128)(2,1)} %get-tuple-element.9, bf16[2048,1024]{1,0:T(8,128)(2,1)} %bitcast.11, bf16[2048,1024]{1,0:T(8,128)(2,1)} %collective-permute-done, pred[]{:T(512)S(6)} %eq.16), kind=kOutput, calls=%fused_computation.26 | convolution fusion | flops 3224109056 | bytes 13107201 | tf_op jit(solution)/shard_map/dot_general | solution.py:157
  508.5 8.6 %all-to-all-done.4 = bf16[16,16,2048]{2,1,0:T(8,128)(2,1)S(1)} async-done(((bf16[16,16,2048]{2,1,0:T(8,128)(2,1)}), bf16[16,16,2048]{2,1,0:T(8,128)(2,1)S(1)}, u32[]{:S(2)}, u32[]{:S(2)}) %all-to-all-start.4) | async-done | bytes 1048608 | tf_op jit(solution)/shard_map/all_to_all | solution.py:186
  (40 shorter events, 14.6 us)
Async XLA Ops:
  7.2 41.4 %copy-start = (bf16[256,2048]{1,0:T(8,128)(2,1)S(1)}, bf16[256,2048]{1,0:T(8,128)(2,1)}, u32[]{:S(2)}) copy-start(bf16[256,2048]{1,0:T(8,128)(2,1)} %param.12) | copy-start | bytes 3145732
  8.7 16.1 %all-to-all-start = ((s32[16,1,12]{2,1,0:T(1,128)}), s32[16,1,12]{2,1,0:T(1,128)S(1)}, u32[]{:S(2)}, u32[]{:S(2)}) async-start(s32[16,1,12]{2,1,0:T(1,128)} %broadcast_in_dim.17), calls=%async_computation | async-start | bytes 16384 | tf_op jit(solution)/shard_map/all_to_all | solution.py:118
  42.9 229.8 %all-to-all-start.1 = ((bf16[16,128,4096]{2,1,0:T(8,128)(2,1)}), bf16[16,128,4096]{2,1,0:T(8,128)(2,1)}, u32[]{:S(2)}, u32[]{:S(2)}) async-start(bf16[16,128,4096]{2,1,0:T(8,128)(2,1)} %shard_map.85), calls=%async_computation.1 | async-start | bytes 33554432 | tf_op jit(solution)/shard_map/all_to_all | solution.py:127
  48.5 419.1 %reduce-scatter.2.cloned.1.call-start = ((), (), s32[]{:S(2)}) async-start(), calls=%async_computation.6 | async-start | bytes 17825792 | tf_op jit(solution)/shard_map/reduce_scatter | solution.py:177
  293.0 2.8 copy-start.7
  305.9 55.8 %copy-start.6 = (s32[12]{0:T(128)S(1)}, s32[12]{0:T(128)}, u32[]{:S(2)}) copy-start(s32[12]{0:T(128)} %get-tuple-element.13.table) | copy-start | bytes 148
  359.8 48.0 %collective-permute-start = (bf16[2048,1024]{1,0:T(8,128)(2,1)}, bf16[2048,1024]{1,0:T(8,128)(2,1)}, u32[]{:S(2)}, u32[]{:S(2)}) collective-permute-start(bf16[2048,1024]{1,0:T(8,128)(2,1)} %bitcast.11), channel_id=1, source_target_pairs={{0,1},{1,0},{2,3},{3,2},{4,5},{5,4},{6,7},{7,6},{8,9},{9,8},{10,11... | collective-permute-start | bytes 12582920 | tf_op jit(solution)/shard_map/ppermute | solution.py:152
  400.2 4.9 copy-start.3
  405.2 2.7 copy-start.8
  425.8 4.7 copy-start.4
  428.8 1.7 copy-start.2
  469.9 20.9 %all-to-all-start.3 = ((f32[8,16,2048]{2,1,0:T(8,128)}), f32[8,16,2048]{2,1,0:T(8,128)S(1)}, u32[]{:S(2)}, u32[]{:S(2)}) async-start(f32[8,16,2048]{2,1,0:T(8,128)} %bitcast.20), calls=%async_computation.4 | async-start | bytes 2097152 | tf_op jit(solution)/shard_map/all_to_all | solution.py:180
  491.9 25.1 %all-to-all-start.4 = ((bf16[16,16,2048]{2,1,0:T(8,128)(2,1)}), bf16[16,16,2048]{2,1,0:T(8,128)(2,1)S(1)}, u32[]{:S(2)}, u32[]{:S(2)}) async-start(bf16[16,16,2048]{2,1,0:T(8,128)(2,1)} %broadcast_in_dim.19), calls=%async_computation.5 | async-start | bytes 2097152 | tf_op jit(solution)/shard_map/all_to_all | solution.py:186
  499.8 6.7 %copy-start.5 = (bf16[1,768,1024]{2,1,0:T(8,128)(2,1)S(1)}, bf16[1,768,1024]{2,1,0:T(8,128)(2,1)}, u32[]{:S(2)}) copy-start(bf16[1,768,1024]{2,1,0:T(8,128)(2,1)} %fusion.15) | copy-start | bytes 4718596
  499.8 18.9 %copy-start.1 = (bf16[256,2048]{1,0:T(8,128)(2,1)S(1)}, bf16[256,2048]{1,0:T(8,128)(2,1)}, u32[]{:S(2)}) copy-start(bf16[256,2048]{1,0:T(8,128)(2,1)} %param.12) | copy-start | bytes 3145732
Sparse Core Ops, SparseCore 0:
  305.5 159.1 reduce-scatter.1

commit v7 on v6

--- a/solution.py
+++ b/solution.py
@@ -69,6 +69,59 @@
     )(order, query_flat, got, got, got, got)
 
 
+def _bwd_kernel(table, back_ref, att_ref, probs_ref, k0_ref, k1_ref, v0_ref, v1_ref, out_ref):
+    scale = 1.0 / math.sqrt(DH)
+    for h in range(HEADS):
+        lanes = slice(h * DH, (h + 1) * DH)
+        back = back_ref[:, lanes]
+        vals = jnp.concatenate([v0_ref[0, :, lanes], v1_ref[0, :, lanes]], axis=0)
+        dprobs = lax.dot_general(
+            back, vals, (((1,), (1,)), ((), ())), preferred_element_type=jnp.float32
+        )
+        delta = jnp.sum(
+            back.astype(jnp.float32) * att_ref[:, lanes].astype(jnp.float32), axis=-1, keepdims=True
+        )
+        dscores = (probs_ref[0, h] * (dprobs - delta)).astype(jnp.bfloat16)
+        keys = jnp.concatenate([k0_ref[0, :, lanes], k1_ref[0, :, lanes]], axis=0)
+        grad = jnp.dot(dscores, keys, preferred_element_type=jnp.float32) * scale
+        out_ref[:, lanes] = grad.astype(out_ref.dtype)
+
+
+def backward_attention(back_flat, attention_flat, probs, got, order):
+    rows, width = back_flat.shape
+    blocks = rows // BLK
+    heads = width // DH
+
+    def kv(k, off):
+        return pl.BlockSpec((1, BLK, width), lambda b, t: (t[KSEL * b + k], 0, off))
+
+    grid_spec = pltpu.PrefetchScalarGridSpec(
+        num_scalar_prefetch=1,
+        grid=(blocks,),
+        in_specs=[
+            pl.BlockSpec((BLK, width), lambda b, t: (b, 0)),
+            pl.BlockSpec((BLK, width), lambda b, t: (b, 0)),
+            pl.BlockSpec((1, heads, BLK, KSEL * BLK), lambda b, t: (b, 0, 0, 0)),
+            kv(0, 0),
+            kv(1, 0),
+            kv(0, 1),
+            kv(1, 1),
+        ],
+        out_specs=pl.BlockSpec((BLK, width), lambda b, t: (b, 0)),
+    )
+    flops = blocks * heads * 4 * BLK * KSEL * BLK * DH
+    return pl.pallas_call(
+        _bwd_kernel,
+        grid_spec=grid_spec,
+        out_shape=jax.ShapeDtypeStruct((rows, width), jnp.bfloat16),
+        cost_estimate=pl.CostEstimate(
+            flops=flops,
+            transcendentals=0,
+            bytes_accessed=rows * width * 2 * 7 + blocks * heads * BLK * KSEL * BLK * 4,
+        ),
+    )(order, back_flat, attention_flat, probs, got, got, got, got)
+
+
 def _send_kernel(index, k_ref, v_ref, o_ref):
     width = k_ref.shape[-1]
     o_ref[0, :, :width] = k_ref[0]
@@ -109,7 +162,6 @@
     blocks = rows // BLK
     width = HEADS * DH
     scale = 1.0 / math.sqrt(DH)
-    query_rows = queries[0].reshape(blocks, BLK, HEADS, DH)
     key_blocks = keys[0].reshape(blocks, BLK, width)
     value_blocks = values[0].reshape(blocks, BLK, width)
     table = pattern[0]
@@ -131,12 +183,8 @@
         concat_axis=0,
         tiled=True,
     )
-    got_keys, got_values = got[..., :width], got[..., width:]
     order = owner.reshape(-1)
     attention_flat, probs = forward_attention(queries[0], got, order)
-    attention = attention_flat.reshape(blocks, BLK, HEADS, DH)
-    picked_keys = jnp.take(got_keys, order, axis=0).reshape(blocks, KSEL * BLK, HEADS, DH)
-    picked_values = jnp.take(got_values, order, axis=0).reshape(blocks, KSEL * BLK, HEADS, DH)
     grad_flat = grad_out[0]
     half = out_weight.shape[1] // 2
     side = own_index % 2
@@ -190,19 +238,7 @@
         concat_axis=0,
         tiled=True,
     ).reshape(ctx_count * split, width).astype(jnp.float32)
-    back_rows = back.reshape(blocks, BLK, HEADS, DH)
-    dprobs = jnp.einsum(
-        "qrhd,qkhd->qhrk", back_rows, picked_values, preferred_element_type=jnp.float32
-    )
-    delta = jnp.einsum("qrhd,qrhd->qhr", back_rows, attention, preferred_element_type=jnp.float32)[
-        ..., None
-    ]
-    dscores = (probs * (dprobs - delta)).astype(jnp.bfloat16)
-    query_sum = (
-        jnp.einsum("qhrk,qkhd->qrhd", dscores, picked_keys, preferred_element_type=jnp.float32)
-        * scale
-    )
-    query_grad = query_sum.astype(jnp.bfloat16).reshape(rows, width)
+    query_grad = backward_attention(back, attention_flat, probs, got, order)
     return (mixed[None], query_grad[None], weight_grad)
 
 

time: 527 us -> 519 us (0.985)
  waiting for transfers between devices: 248 us -> 320 us
  local copies, waits for them, and re-layouts: 71.5 us -> 10.7 us
  matrix products: 61.5 us -> 37.2 us
  Pallas kernels: 32.5 us -> 47.7 us
  other arithmetic: 15.2 us -> 7.79 us
    reduce_scatter x1, waiting for transfers between devices: 0.01 us -> 67.2 us  [local(): stage = lax.psum_scatter(partial, 'ctx', scatter_dimension=0, tiled=True)]
    dot_general x2 -> x0, matrix products: 24.5 us -> none  [the longest x1 14.2 us: local(): jnp.einsum('qhrk,qkhd->qrhd', dscores, picked_keys, preferred_element_typ...]
    unnamed x23 -> x11, local copies, waits for them, and re-layouts: 18.6 us -> 1.33 us
    gather x2 -> x0, local copies, waits for them, and re-layouts: 15.9 us -> none  [the longest x1 8.08 us: local(): jnp.take(got_values, order, axis=0).reshape(blocks, KSEL * BLK, HEADS, DH)]
    pallas_call x0 -> x1, Pallas kernels: none -> 15 us  [backward_attention(): pl.pallas_call(_bwd_kernel, grid_spec=grid_spec, out_shape=jax.ShapeDtype...]
    slice x1 -> x0, local copies, waits for them, and re-layouts: 12 us -> none  [local(): got_keys, got_values = (got[..., :width], got[..., width:])]
    convert_element_type x2 -> x0, local copies, waits for them, and re-layouts: 9.73 us -> none  [the longest x1 4.94 us: local(): query_grad = query_sum.astype(jnp.bfloat16).reshape(rows, width)]
    ppermute x1, waiting for transfers between devices: 0.01 us -> 7.13 us  [local(): other = lax.ppermute(mine, 'ctx', [(j, j ^ 1) for j in range(ctx_count)])]
  transfers between devices with their start and end apart: 6 -> 6, of which waited for: 4 -> 6; matrix products, arithmetic and copies ran while one was open for 23% -> 6% of each run, Pallas kernels for 0% -> 3%
where the time goes in v7:
time: 519 us
  waiting for transfers between devices  320 us (62%)
  blocking collectives  54.1 us (10%)
  Pallas kernels  47.7 us (9%)
  matrix products  37.2 us (7%)
  starting transfers between devices  26.7 us (5%)
  between operations  14.1 us (3%)
  local copies, waits for them, and re-layouts  10.7 us (2%)
  other arithmetic  7.79 us (2%)
    all_to_all x1, waiting for transfers between devices, local(): lax.all_to_all(send_buffer(key_blocks, value_blocks, send_index), 'ctx',...  224 us
    reduce_scatter x1, waiting for transfers between devices, local(): stage = lax.psum_scatter(partial, 'ctx', scatter_dimension=0, tiled=True)  67.2 us
    all_to_all x1, blocking collectives, local(): lax.all_to_all(jnp.broadcast_to(own_half[None], (data_count,) + own_half....  54.1 us
    pallas_call x1, Pallas kernels, send_buffer(): pl.pallas_call(_send_kernel, grid_spec=grid_spec, out_shape=jax.ShapeDtyp...  17 us
    pallas_call x1, Pallas kernels, forward_attention(): pl.pallas_call(_fwd_kernel, grid_spec=grid_spec, out_shape=[jax.ShapeDtyp...  15.7 us
    pallas_call x1, Pallas kernels, backward_attention(): pl.pallas_call(_bwd_kernel, grid_spec=grid_spec, out_shape=jax.ShapeDtype...  15 us
  transfers between devices with their start and end apart: 6, of which 6 were waited for; matrix products, arithmetic and copies ran while one was open for 6% of the time, Pallas kernels for 3%

profile of v7, /device:TPU:1, one launch (start us, length us, event | category | flops | bytes accessed | tf_op | source)
XLA Modules:
  0.0 518.5 jit_solution(5620542858446177126)
XLA Ops:
  7.2 0.9 copy.28
  8.1 0.6 broadcast_in_dim.10
  8.7 9.1 %all-to-all-start = ((s32[16,1,12]{2,1,0:T(1,128)}), s32[16,1,12]{2,1,0:T(1,128)S(1)}, u32[]{:S(2)}, u32[]{:S(2)}) async-start(s32[16,1,12]{2,1,0:T(1,128)} %broadcast_in_dim.10), calls=%async_computation | async-start | bytes 16384 | tf_op jit(solution)/shard_map/all_to_all | solution.py:170
  17.8 6.9 %all-to-all-done = s32[16,1,12]{2,1,0:T(1,128)S(1)} async-done(((s32[16,1,12]{2,1,0:T(1,128)}), s32[16,1,12]{2,1,0:T(1,128)S(1)}, u32[]{:S(2)}, u32[]{:S(2)}) %all-to-all-start) | async-done | bytes 800 | tf_op jit(solution)/shard_map/all_to_all | solution.py:170
  24.8 0.7 div.17
  25.5 0.6 fusion.8.index
  26.1 17.0 %shard_map.85 = bf16[16,128,4096]{2,1,0:T(8,128)(2,1)} custom-call(s32[16]{0:T(128)} %fusion.8.index, bf16[6,128,2048]{2,1,0:T(8,128)(2,1)} %bitcast.49, bf16[6,128,2048]{2,1,0:T(8,128)(2,1)} %bitcast.50), custom_call_target="tpu_custom_call" | custom-call | bytes 33554432 | tf_op jit(solution)/shard_map/pallas_call | solution.py:143
  43.1 5.6 %all-to-all-start.1 = ((bf16[16,128,4096]{2,1,0:T(8,128)(2,1)}), bf16[16,128,4096]{2,1,0:T(8,128)(2,1)}, u32[]{:S(2)}, u32[]{:S(2)}) async-start(bf16[16,128,4096]{2,1,0:T(8,128)(2,1)} %shard_map.85), calls=%async_computation.1 | async-start | bytes 33554432 | tf_op jit(solution)/shard_map/all_to_all | solution.py:179
  48.8 0.5 and_select_fusion.table
  49.3 223.5 %all-to-all-done.1.k0_ref.k1_ref.v0_ref.v1_ref = bf16[16,128,4096]{2,1,0:T(8,128)(2,1)} async-done(((bf16[16,128,4096]{2,1,0:T(8,128)(2,1)}), bf16[16,128,4096]{2,1,0:T(8,128)(2,1)}, u32[]{:S(2)}, u32[]{:S(2)}) %all-to-all-start.1) | async-done | bytes 16777248 | tf_op jit(solution)/shard_map/all_to_all | solution.py:179
  272.9 15.7 %shard_map.86 = (bf16[768,2048]{1,0:T(8,128)(2,1)}, f32[6,16,128,256]{3,2,1,0:T(8,128)}) custom-call(s32[12]{0:T(128)} %and_select_fusion.table, bf16[768,2048]{1,0:T(8,128)(2,1)} %bitcast.52, bf16[16,128,4096]{2,1,0:T(8,128)(2,1)} %all-to-all-done.1.k0_ref.k1_ref.v0_ref.v1_ref, bf16[16,128,4096]{2,1,0:T(8,128)(2,1)} %all-to-all-done.1.k0_ref.k1_ref.v0_ref.v1_ref, ...), custom_call_target="tpu_custom_call" | custom-call | flops 1610612736 | bytes 31457280 | tf_op jit(solution)/shard_map/pallas_call | solution.py:57
  288.6 4.6 copy.34
  293.2 2.4 copy.35
  296.0 9.5 %fusion.12 = f32[2048,2048]{1,0:T(8,128)} fusion(bf16[768,2048]{0,1:T(8,128)(2,1)S(1)} %bitcast.51, bf16[1,768,2048]{2,1,0:T(8,128)(2,1)S(1)} %copy-done.3), kind=kOutput, calls=%fused_computation.27 | convolution fusion | flops 6442450944 | bytes 23068672 | tf_op jit(solution)/shard_map/dot_general | solution.py:222
  305.6 0.5 broadcast_in_dim.11
  306.1 54.1 %all_to_all.26 = bf16[8,256,1024]{2,1,0:T(8,128)(2,1)} all-to-all(bf16[8,256,1024]{2,1,0:T(8,128)(2,1)S(1)} %broadcast_in_dim.11), channel_id=1, replica_groups=mesh['dp'=8,'ctx'=16] {'dp'}, dimensions={0} | all-to-all | bytes 8388608 | tf_op jit(solution)/shard_map/all_to_all | solution.py:193
  360.2 1.8 collective-permute-start
  362.0 7.1 %collective-permute-done = bf16[2048,1024]{1,0:T(8,128)(2,1)} collective-permute-done((bf16[2048,1024]{1,0:T(8,128)(2,1)}, bf16[2048,1024]{1,0:T(8,128)(2,1)}, u32[]{:S(2)}, u32[]{:S(2)}) %collective-permute-start) | collective-permute-done | bytes 4194336 | tf_op jit(solution)/shard_map/ppermute | solution.py:200
  369.2 5.9 %fusion.1 = f32[2048,768]{0,1:T(8,128)S(1)} fusion(bf16[2048,1024]{1,0:T(8,128)(2,1)} %collective-permute-done, bf16[2048,1024]{1,0:T(8,128)(2,1)} %bitcast.9, pred[]{:T(512)S(6)} %eq.16, bf16[768,2048]{1,0:T(8,128)(2,1)} %bitcast.56), kind=kOutput, calls=%fused_computation.7 | convolution fusion | flops 3223322624 | bytes 16252929 | tf_op jit(solution)/shard_map/dot_general | solution.py:213
  375.1 7.3 %fusion.back_ref = bf16[768,2048]{1,0:T(8,128)(2,1)} fusion(f32[2048,768]{0,1:T(8,128)S(1)} %fusion.1, bf16[2048,1024]{1,0:T(8,128)(2,1)} %bitcast.9, bf16[2048,1024]{1,0:T(8,128)(2,1)} %collective-permute-done, pred[]{:T(512)S(6)} %eq.16, bf16[768,2048]{1,0:T(8,128)(2,1)S(1)} %bitcast.57), kind=kOutput, calls=%fused_computation.4 | convolution fusion | flops 3226468352 | bytes 19398656 | tf_op jit(solution)/shard_map/dot_general | solution.py:211
  382.4 15.0 %shard_map.87 = bf16[768,2048]{1,0:T(8,128)(2,1)} custom-call(s32[12]{0:T(128)} %and_select_fusion.table, bf16[768,2048]{1,0:T(8,128)(2,1)} %fusion.back_ref, bf16[768,2048]{1,0:T(8,128)(2,1)} %get-tuple-element.8.att_ref, f32[6,16,128,256]{3,2,1,0:T(8,128)} %get-tuple-element.10.probs_ref, ...), custom_call_target="tpu_custom_call" | custom-call | flops 1610612736 | bytes 34603008 | tf_op jit(solution)/shard_map/pallas_call | solution.py:113
  397.4 67.2 %reduce-scatter.2.cloned.1.call-done = f32[128,2048]{1,0:T(8,128)} async-done(((f32[2048,2048]{1,0:T(8,128)}), f32[128,2048]{1,0:T(8,128)}) %reduce-scatter.2.cloned.1.call-update) | async-done | bytes 1048592 | tf_op jit(solution)/shard_map/reduce_scatter | solution.py:225
  464.6 2.3 broadcast_multiply_fusion
  467.0 4.1 all-to-all-start.3
  471.1 7.7 %fusion.4 = bf16[1,768,1024]{2,1,0:T(8,128)(2,1)} fusion(bf16[768,2048]{1,0:T(8,128)(2,1)} %get-tuple-element.8.att_ref, bf16[2048,1024]{1,0:T(8,128)(2,1)} %bitcast.9, bf16[2048,1024]{1,0:T(8,128)(2,1)} %collective-permute-done, pred[]{:T(512)S(6)} %eq.16), kind=kOutput, calls=%fused_computation.10 | convolution fusion | flops 3224109056 | bytes 13107201 | tf_op jit(solution)/shard_map/dot_general | solution.py:205
  478.8 6.8 %all-to-all-done.3 = f32[8,16,2048]{2,1,0:T(8,128)S(1)} async-done(((f32[8,16,2048]{2,1,0:T(8,128)}), f32[8,16,2048]{2,1,0:T(8,128)S(1)}, u32[]{:S(2)}, u32[]{:S(2)}) %all-to-all-start.3) | async-done | bytes 1048608 | tf_op jit(solution)/shard_map/all_to_all | solution.py:228
  485.6 1.1 broadcast_in_dim.13
  486.7 6.1 %all-to-all-start.4 = ((bf16[16,16,2048]{2,1,0:T(8,128)(2,1)}), bf16[16,16,2048]{2,1,0:T(8,128)(2,1)S(1)}, u32[]{:S(2)}, u32[]{:S(2)}) async-start(bf16[16,16,2048]{2,1,0:T(8,128)(2,1)} %broadcast_in_dim.13), calls=%async_computation.5 | async-start | bytes 2097152 | tf_op jit(solution)/shard_map/all_to_all | solution.py:234
  492.8 6.7 %fusion.5 = bf16[1,768,1024]{2,1,0:T(8,128)(2,1)S(1)} fusion(bf16[768,2048]{1,0:T(8,128)(2,1)} %get-tuple-element.8.att_ref, bf16[2048,1024]{1,0:T(8,128)(2,1)} %collective-permute-done, bf16[2048,1024]{1,0:T(8,128)(2,1)} %bitcast.9, pred[]{:T(512)S(6)} %eq.16), kind=kOutput, calls=%fused_computation.11 | convolution fusion | flops 3224109056 | bytes 13107201 | tf_op jit(solution)/shard_map/dot_general | solution.py:206
  499.5 2.0 pad_maximum_fusion
  501.4 8.6 %all-to-all-done.4 = bf16[16,16,2048]{2,1,0:T(8,128)(2,1)S(1)} async-done(((bf16[16,16,2048]{2,1,0:T(8,128)(2,1)}), bf16[16,16,2048]{2,1,0:T(8,128)(2,1)S(1)}, u32[]{:S(2)}, u32[]{:S(2)}) %all-to-all-start.4) | async-done | bytes 1048608 | tf_op jit(solution)/shard_map/all_to_all | solution.py:234
  510.0 1.6 bitcast_convert_fusion
  (16 shorter events, 0.7 us)
Async XLA Ops:
  7.2 41.6 %copy-start = (bf16[256,2048]{1,0:T(8,128)(2,1)S(1)}, bf16[256,2048]{1,0:T(8,128)(2,1)}, u32[]{:S(2)}) copy-start(bf16[256,2048]{1,0:T(8,128)(2,1)} %param.10) | copy-start | bytes 3145732
  8.7 16.1 %all-to-all-start = ((s32[16,1,12]{2,1,0:T(1,128)}), s32[16,1,12]{2,1,0:T(1,128)S(1)}, u32[]{:S(2)}, u32[]{:S(2)}) async-start(s32[16,1,12]{2,1,0:T(1,128)} %broadcast_in_dim.10), calls=%async_computation | async-start | bytes 16384 | tf_op jit(solution)/shard_map/all_to_all | solution.py:170
  43.1 229.8 %all-to-all-start.1 = ((bf16[16,128,4096]{2,1,0:T(8,128)(2,1)}), bf16[16,128,4096]{2,1,0:T(8,128)(2,1)}, u32[]{:S(2)}, u32[]{:S(2)}) async-start(bf16[16,128,4096]{2,1,0:T(8,128)(2,1)} %shard_map.85), calls=%async_computation.1 | async-start | bytes 33554432 | tf_op jit(solution)/shard_map/all_to_all | solution.py:179
  48.7 416.0 %reduce-scatter.2.cloned.1.call-start = ((), (), s32[]{:S(2)}) async-start(), calls=%async_computation.6 | async-start | bytes 17825792 | tf_op jit(solution)/shard_map/reduce_scatter | solution.py:225
  293.2 2.8 copy-start.3
  360.2 9.0 %collective-permute-start = (bf16[2048,1024]{1,0:T(8,128)(2,1)}, bf16[2048,1024]{1,0:T(8,128)(2,1)}, u32[]{:S(2)}, u32[]{:S(2)}) collective-permute-start(bf16[2048,1024]{1,0:T(8,128)(2,1)} %bitcast.9), channel_id=1, source_target_pairs={{0,1},{1,0},{2,3},{3,2},{4,5},{5,4},{6,7},{7,6},{8,9},{9,8},{10,11... | collective-permute-start | bytes 12582920 | tf_op jit(solution)/shard_map/ppermute | solution.py:200
  369.2 5.9 %copy-start.4 = (bf16[1,768,2048]{2,1,0:T(8,128)(2,1)S(1)}, bf16[1,768,2048]{2,1,0:T(8,128)(2,1)}, u32[]{:S(2)}) copy-start(bf16[1,768,2048]{2,1,0:T(8,128)(2,1)} %param.9) | copy-start | bytes 9437188
  467.0 18.6 %all-to-all-start.3 = ((f32[8,16,2048]{2,1,0:T(8,128)}), f32[8,16,2048]{2,1,0:T(8,128)S(1)}, u32[]{:S(2)}, u32[]{:S(2)}) async-start(f32[8,16,2048]{2,1,0:T(8,128)} %bitcast.18), calls=%async_computation.4 | async-start | bytes 2097152 | tf_op jit(solution)/shard_map/all_to_all | solution.py:228
  486.7 23.3 %all-to-all-start.4 = ((bf16[16,16,2048]{2,1,0:T(8,128)(2,1)}), bf16[16,16,2048]{2,1,0:T(8,128)(2,1)S(1)}, u32[]{:S(2)}, u32[]{:S(2)}) async-start(bf16[16,16,2048]{2,1,0:T(8,128)(2,1)} %broadcast_in_dim.13), calls=%async_computation.5 | async-start | bytes 2097152 | tf_op jit(solution)/shard_map/all_to_all | solution.py:234
  492.8 6.7 %copy-start.2 = (bf16[1,768,1024]{2,1,0:T(8,128)(2,1)S(1)}, bf16[1,768,1024]{2,1,0:T(8,128)(2,1)}, u32[]{:S(2)}) copy-start(bf16[1,768,1024]{2,1,0:T(8,128)(2,1)} %fusion.4) | copy-start | bytes 4718596
  499.5 12.2 %copy-start.1 = (bf16[256,2048]{1,0:T(8,128)(2,1)S(1)}, bf16[256,2048]{1,0:T(8,128)(2,1)}, u32[]{:S(2)}) copy-start(bf16[256,2048]{1,0:T(8,128)(2,1)} %param.10) | copy-start | bytes 3145732
Sparse Core Ops, SparseCore 0:
  305.7 158.9 reduce-scatter.1

commit v8 on v7

--- a/solution.py
+++ b/solution.py
@@ -223,6 +223,8 @@
         columns, grad_flat, (((0,), (0,)), ((), ())), preferred_element_type=jnp.float32
     )
     stage = lax.psum_scatter(partial, "ctx", scatter_dimension=0, tiled=True)
+    query_grad = backward_attention(back, attention_flat, probs, got, order)
+    stage, mixed, query_grad = lax.optimization_barrier((stage, mixed, query_grad))
     stage = stage * (1.0 / math.sqrt(rows * ctx_count * data_count))
     shard = jnp.sum(
         lax.all_to_all(
@@ -238,7 +240,6 @@
         concat_axis=0,
         tiled=True,
     ).reshape(ctx_count * split, width).astype(jnp.float32)
-    query_grad = backward_attention(back, attention_flat, probs, got, order)
     return (mixed[None], query_grad[None], weight_grad)
 
 

time: 519 us -> 517 us (level)
  blocking collectives: 54.1 us -> 94.6 us
  waiting for transfers between devices: 320 us -> 290 us
  starting transfers between devices: 26.7 us -> 16.1 us
    all_to_all x0 -> x2, blocking collectives: none -> 40.8 us  [the longest x1 23.2 us: local(): lax.all_to_all(jnp.broadcast_to(piece[None], (ctx_count,) + piece.shape),...]
    all_to_all x2 -> x0, waiting for transfers between devices: 15.4 us -> none  [the longest x1 8.6 us: local(): lax.all_to_all(jnp.broadcast_to(piece[None], (ctx_count,) + piece.shape),...]
    reduce_scatter x1, waiting for transfers between devices: 67.2 us -> 53 us  [local(): stage = lax.psum_scatter(partial, 'ctx', scatter_dimension=0, tiled=True)]
    all_to_all x2 -> x0, starting transfers between devices: 10.2 us -> none  [the longest x1 6.07 us: local(): lax.all_to_all(jnp.broadcast_to(piece[None], (ctx_count,) + piece.shape),...]
  transfers between devices with their start and end apart: 6 -> 4, of which waited for: 6 -> 4; matrix products, arithmetic and copies ran while one was open for 6% -> 6% of each run, Pallas kernels for 3% -> 3%
where the time goes in v8:
time: 517 us; the launch traced here: 516 us
  waiting for transfers between devices  290 us (56%)
  blocking collectives  94.6 us (18%)
  Pallas kernels  48.5 us (9%)
  matrix products  35.4 us (7%)
  starting transfers between devices  16.1 us (3%)
  between operations  14.2 us (3%)
  local copies, waits for them, and re-layouts  9.7 us (2%)
  other arithmetic  6.8 us (1%)
    all_to_all x1, waiting for transfers between devices, local(): lax.all_to_all(send_buffer(key_blocks, value_blocks, send_index), 'ctx',...  223 us
    all_to_all x1, blocking collectives, local(): lax.all_to_all(jnp.broadcast_to(own_half[None], (data_count,) + own_half....  53.8 us
    reduce_scatter x1, waiting for transfers between devices, local(): stage = lax.psum_scatter(partial, 'ctx', scatter_dimension=0, tiled=True)  53 us
    all_to_all x1, blocking collectives, local(): lax.all_to_all(jnp.broadcast_to(piece[None], (ctx_count,) + piece.shape),...  23.2 us
    pallas_call x1, Pallas kernels, send_buffer(): pl.pallas_call(_send_kernel, grid_spec=grid_spec, out_shape=jax.ShapeDtyp...  17.8 us
    all_to_all x1, blocking collectives, local(): lax.all_to_all(stage.reshape(data_count, split, width), 'dp', split_axis=...  17.6 us
    pallas_call x1, Pallas kernels, forward_attention(): pl.pallas_call(_fwd_kernel, grid_spec=grid_spec, out_shape=[jax.ShapeDtyp...  15.7 us
    pallas_call x1, Pallas kernels, backward_attention(): pl.pallas_call(_bwd_kernel, grid_spec=grid_spec, out_shape=jax.ShapeDtype...  15 us
  transfers between devices with their start and end apart: 4, of which 4 were waited for; matrix products, arithmetic and copies ran while one was open for 6% of the time, Pallas kernels for 3%

profile of v8, /device:TPU:1, one launch (start us, length us, event | category | flops | bytes accessed | tf_op | source)
XLA Modules:
  0.0 515.6 jit_solution(6196599454581521227)
XLA Ops:
  7.2 0.9 copy.28
  8.0 0.1 squeeze.9
  8.1 0.6 broadcast_in_dim.12
  8.7 9.1 %all-to-all-start = ((s32[16,1,12]{2,1,0:T(1,128)}), s32[16,1,12]{2,1,0:T(1,128)S(1)}, u32[]{:S(2)}, u32[]{:S(2)}) async-start(s32[16,1,12]{2,1,0:T(1,128)} %broadcast_in_dim.12), calls=%async_computation | async-start | bytes 16384 | tf_op jit(solution)/shard_map/all_to_all | solution.py:170
  17.8 6.9 %all-to-all-done = s32[16,1,12]{2,1,0:T(1,128)S(1)} async-done(((s32[16,1,12]{2,1,0:T(1,128)}), s32[16,1,12]{2,1,0:T(1,128)S(1)}, u32[]{:S(2)}, u32[]{:S(2)}) %all-to-all-start) | async-done | bytes 800 | tf_op jit(solution)/shard_map/all_to_all | solution.py:170
  24.8 0.7 div.17
  25.5 0.6 fusion.6.index
  26.1 17.8 %shard_map.85 = bf16[16,128,4096]{2,1,0:T(8,128)(2,1)} custom-call(s32[16]{0:T(128)} %fusion.6.index, bf16[6,128,2048]{2,1,0:T(8,128)(2,1)} %bitcast.47, bf16[6,128,2048]{2,1,0:T(8,128)(2,1)} %bitcast.48), custom_call_target="tpu_custom_call" | custom-call | bytes 33554432 | tf_op jit(solution)/shard_map/pallas_call | solution.py:143
  43.9 5.1 all-to-all-start.1
  49.1 0.5 and_select_fusion.table
  49.7 223.3 %all-to-all-done.1.k0_ref.k1_ref.v0_ref.v1_ref = bf16[16,128,4096]{2,1,0:T(8,128)(2,1)} async-done(((bf16[16,128,4096]{2,1,0:T(8,128)(2,1)}), bf16[16,128,4096]{2,1,0:T(8,128)(2,1)}, u32[]{:S(2)}, u32[]{:S(2)}) %all-to-all-start.1) | async-done | bytes 16777248 | tf_op jit(solution)/shard_map/all_to_all | solution.py:179
  273.0 15.7 %shard_map.86 = (bf16[768,2048]{1,0:T(8,128)(2,1)}, f32[6,16,128,256]{3,2,1,0:T(8,128)}) custom-call(s32[12]{0:T(128)} %and_select_fusion.table, bf16[768,2048]{1,0:T(8,128)(2,1)} %bitcast.51, bf16[16,128,4096]{2,1,0:T(8,128)(2,1)} %all-to-all-done.1.k0_ref.k1_ref.v0_ref.v1_ref, bf16[16,128,4096]{2,1,0:T(8,128)(2,1)} %all-to-all-done.1.k0_ref.k1_ref.v0_ref.v1_ref, ...), custom_call_target="tpu_custom_call" | custom-call | flops 1610612736 | bytes 31457280 | tf_op jit(solution)/shard_map/pallas_call | solution.py:57
  288.7 4.6 copy.32
  293.3 2.4 copy.33
  295.7 0.4 copy-done.3
  296.1 9.5 %fusion.10 = f32[2048,2048]{1,0:T(8,128)} fusion(bf16[768,2048]{0,1:T(8,128)(2,1)S(1)} %bitcast.50, bf16[1,768,2048]{2,1,0:T(8,128)(2,1)S(1)} %copy-done.3), kind=kOutput, calls=%fused_computation.25 | convolution fusion | flops 6442450944 | bytes 23068672 | tf_op jit(solution)/shard_map/dot_general | solution.py:222
  305.7 0.5 broadcast_in_dim.13
  306.2 53.8 %all_to_all.26 = bf16[8,256,1024]{2,1,0:T(8,128)(2,1)} all-to-all(bf16[8,256,1024]{2,1,0:T(8,128)(2,1)S(1)} %broadcast_in_dim.13), channel_id=1, replica_groups=mesh['dp'=8,'ctx'=16] {'dp'}, dimensions={0} | all-to-all | bytes 8388608 | tf_op jit(solution)/shard_map/all_to_all | solution.py:193
  360.0 1.8 collective-permute-start
  361.8 7.1 %collective-permute-done = bf16[2048,1024]{1,0:T(8,128)(2,1)} collective-permute-done((bf16[2048,1024]{1,0:T(8,128)(2,1)}, bf16[2048,1024]{1,0:T(8,128)(2,1)}, u32[]{:S(2)}, u32[]{:S(2)}) %collective-permute-start) | collective-permute-done | bytes 4194336 | tf_op jit(solution)/shard_map/ppermute | solution.py:200
  369.0 5.9 %fusion.1 = f32[2048,768]{0,1:T(8,128)S(1)} fusion(bf16[2048,1024]{1,0:T(8,128)(2,1)} %collective-permute-done, bf16[2048,1024]{1,0:T(8,128)(2,1)} %bitcast.13, pred[]{:T(512)S(6)} %eq.16, bf16[768,2048]{1,0:T(8,128)(2,1)} %bitcast.55), kind=kOutput, calls=%fused_computation.7 | convolution fusion | flops 3223322624 | bytes 16252929 | tf_op jit(solution)/shard_map/dot_general | solution.py:213
  374.9 7.3 %fusion.back_ref = bf16[768,2048]{1,0:T(8,128)(2,1)} fusion(f32[2048,768]{0,1:T(8,128)S(1)} %fusion.1, bf16[2048,1024]{1,0:T(8,128)(2,1)} %bitcast.13, bf16[2048,1024]{1,0:T(8,128)(2,1)} %collective-permute-done, pred[]{:T(512)S(6)} %eq.16, bf16[768,2048]{1,0:T(8,128)(2,1)S(1)} %bitcast.56), kind=kOutput, calls=%fused_computation.4 | convolution fusion | flops 3226468352 | bytes 19398656 | tf_op jit(solution)/shard_map/dot_general | solution.py:211
  382.2 15.0 %shard_map.87 = bf16[768,2048]{1,0:T(8,128)(2,1)} custom-call(s32[12]{0:T(128)} %and_select_fusion.table, bf16[768,2048]{1,0:T(8,128)(2,1)} %fusion.back_ref, bf16[768,2048]{1,0:T(8,128)(2,1)} %get-tuple-element.11.att_ref, f32[6,16,128,256]{3,2,1,0:T(8,128)} %get-tuple-element.13.probs_ref, ...), custom_call_target="tpu_custom_call" | custom-call | flops 1610612736 | bytes 34603008 | tf_op jit(solution)/shard_map/pallas_call | solution.py:113
  397.2 6.9 %convolution_convert_fusion.1 = bf16[768,1024]{1,0:T(8,128)(2,1)S(1)} fusion(bf16[768,2048]{1,0:T(8,128)(2,1)} %get-tuple-element.11.att_ref, bf16[2048,1024]{1,0:T(8,128)(2,1)} %bitcast.13, bf16[2048,1024]{1,0:T(8,128)(2,1)} %collective-permute-done, pred[]{:T(512)S(6)} %eq.16), kind=kOutput, calls=%fused_computation.6 | convolution fusion | flops 3224109056 | bytes 13107201 | tf_op jit(solution)/shard_map/dot_general | solution.py:205
  404.1 5.7 %convolution_convert_fusion = bf16[768,1024]{1,0:T(8,128)(2,1)S(1)} fusion(bf16[768,2048]{1,0:T(8,128)(2,1)S(1)} %copy-done.2, bf16[2048,1024]{1,0:T(8,128)(2,1)} %collective-permute-done, bf16[2048,1024]{1,0:T(8,128)(2,1)} %bitcast.13, pred[]{:T(512)S(6)} %eq.16), kind=kOutput, calls=%fused_computation.5 | convolution fusion | flops 3224109056 | bytes 13107201 | tf_op jit(solution)/shard_map/dot_general | solution.py:206
  409.8 2.0 pad_maximum_fusion
  411.8 53.0 %reduce-scatter.2.cloned.1.call-done = f32[128,2048]{1,0:T(8,128)} async-done(((f32[2048,2048]{1,0:T(8,128)}), f32[128,2048]{1,0:T(8,128)}) %reduce-scatter.2.cloned.1.call-update) | async-done | bytes 1048592 | tf_op jit(solution)/shard_map/reduce_scatter | solution.py:225
  464.8 1.3 broadcast_multiply_fusion
  466.1 17.6 %all_to_all.27 = f32[8,16,2048]{2,1,0:T(8,128)S(1)} all-to-all(f32[8,16,2048]{2,1,0:T(8,128)S(1)} %bitcast.45), channel_id=1, replica_groups=mesh['dp'=8,'ctx'=16] {'dp'}, dimensions={0} | all-to-all | bytes 2097152 | tf_op jit(solution)/shard_map/all_to_all | solution.py:230
  483.8 0.1 broadcast_in_dim.29
  483.9 23.2 %all_to_all.28 = bf16[16,16,2048]{2,1,0:T(8,128)(2,1)S(1)} all-to-all(bf16[16,16,2048]{2,1,0:T(8,128)(2,1)S(1)} %broadcast_in_dim.29), channel_id=1, replica_groups=mesh['dp'=8,'ctx'=16] {'ctx'}, dimensions={0} | all-to-all | bytes 2097152 | tf_op jit(solution)/shard_map/all_to_all | solution.py:236
  507.1 1.6 bitcast_convert_fusion
  (14 shorter events, 0.2 us)
Async XLA Ops:
  7.2 41.9 %copy-start = (bf16[256,2048]{1,0:T(8,128)(2,1)S(1)}, bf16[256,2048]{1,0:T(8,128)(2,1)}, u32[]{:S(2)}) copy-start(bf16[256,2048]{1,0:T(8,128)(2,1)} %param.10) | copy-start | bytes 3145732
  8.7 16.1 %all-to-all-start = ((s32[16,1,12]{2,1,0:T(1,128)}), s32[16,1,12]{2,1,0:T(1,128)S(1)}, u32[]{:S(2)}, u32[]{:S(2)}) async-start(s32[16,1,12]{2,1,0:T(1,128)} %broadcast_in_dim.12), calls=%async_computation | async-start | bytes 16384 | tf_op jit(solution)/shard_map/all_to_all | solution.py:170
  43.9 229.1 %all-to-all-start.1 = ((bf16[16,128,4096]{2,1,0:T(8,128)(2,1)}), bf16[16,128,4096]{2,1,0:T(8,128)(2,1)}, u32[]{:S(2)}, u32[]{:S(2)}) async-start(bf16[16,128,4096]{2,1,0:T(8,128)(2,1)} %shard_map.85), calls=%async_computation.1 | async-start | bytes 33554432 | tf_op jit(solution)/shard_map/all_to_all | solution.py:179
  49.0 415.7 %reduce-scatter.2.cloned.1.call-start = ((), (), s32[]{:S(2)}) async-start(), calls=%async_computation.6 | async-start | bytes 17825792 | tf_op jit(solution)/shard_map/reduce_scatter | solution.py:225
  293.3 2.8 copy-start.3
  360.0 9.0 %collective-permute-start = (bf16[2048,1024]{1,0:T(8,128)(2,1)}, bf16[2048,1024]{1,0:T(8,128)(2,1)}, u32[]{:S(2)}, u32[]{:S(2)}) collective-permute-start(bf16[2048,1024]{1,0:T(8,128)(2,1)} %bitcast.13), channel_id=1, source_target_pairs={{0,1},{1,0},{2,3},{3,2},{4,5},{5,4},{6,7},{7,6},{8,9},{9,8},{10,11... | collective-permute-start | bytes 12582920 | tf_op jit(solution)/shard_map/ppermute | solution.py:200
  369.0 5.9 %copy-start.4 = (bf16[1,768,2048]{2,1,0:T(8,128)(2,1)S(1)}, bf16[1,768,2048]{2,1,0:T(8,128)(2,1)}, u32[]{:S(2)}) copy-start(bf16[1,768,2048]{2,1,0:T(8,128)(2,1)} %param.9) | copy-start | bytes 9437188
  397.2 6.9 %copy-start.2 = (bf16[768,2048]{1,0:T(8,128)(2,1)S(1)}, bf16[768,2048]{1,0:T(8,128)(2,1)}, u32[]{:S(2)}) copy-start(bf16[768,2048]{1,0:T(8,128)(2,1)} %get-tuple-element.11.att_ref) | copy-start | bytes 9437188
  483.7 25.0 %copy-start.1 = (bf16[256,2048]{1,0:T(8,128)(2,1)S(1)}, bf16[256,2048]{1,0:T(8,128)(2,1)}, u32[]{:S(2)}) copy-start(bf16[256,2048]{1,0:T(8,128)(2,1)} %param.10) | copy-start | bytes 3145732
Sparse Core Ops, SparseCore 0:
  305.8 158.9 reduce-scatter.1

commit v9 on v8

--- a/solution.py
+++ b/solution.py
@@ -122,30 +122,33 @@
     )(order, back_flat, attention_flat, probs, got, got, got, got)
 
 
-def _send_kernel(index, k_ref, v_ref, o_ref):
-    width = k_ref.shape[-1]
-    o_ref[0, :, :width] = k_ref[0]
-    o_ref[0, :, width:] = v_ref[0]
+def _send_kernel(index, k0_ref, k1_ref, v0_ref, v1_ref, o_ref):
+    width = k0_ref.shape[-1]
+    o_ref[0, :, :width] = k0_ref[0]
+    o_ref[0, :, width:] = v0_ref[0]
+    o_ref[1, :, :width] = k1_ref[0]
+    o_ref[1, :, width:] = v1_ref[0]
 
 
 def send_buffer(key_blocks, value_blocks, send_index):
     count = send_index.shape[0]
     _, blk, width = key_blocks.shape
+
+    def pick(k):
+        return pl.BlockSpec((1, blk, width), lambda d, t: (t[2 * d + k], 0, 0))
+
     grid_spec = pltpu.PrefetchScalarGridSpec(
         num_scalar_prefetch=1,
-        grid=(count,),
-        in_specs=[
-            pl.BlockSpec((1, blk, width), lambda d, t: (t[d], 0, 0)),
-            pl.BlockSpec((1, blk, width), lambda d, t: (t[d], 0, 0)),
-        ],
-        out_specs=pl.BlockSpec((1, blk, 2 * width), lambda d, t: (d, 0, 0)),
+        grid=(count // 2,),
+        in_specs=[pick(0), pick(1), pick(0), pick(1)],
+        out_specs=pl.BlockSpec((2, blk, 2 * width), lambda d, t: (d, 0, 0)),
     )
     return pl.pallas_call(
         _send_kernel,
         grid_spec=grid_spec,
         out_shape=jax.ShapeDtypeStruct((count, blk, 2 * width), key_blocks.dtype),
         cost_estimate=pl.CostEstimate(flops=0, transcendentals=0, bytes_accessed=count * blk * width * 8),
-    )(send_index, key_blocks, value_blocks)
+    )(send_index, key_blocks, key_blocks, value_blocks, value_blocks)
 
 
 def softmax_rows(scores):

time: 517 us -> 513 us (level)
  Pallas kernels: 48.5 us -> 42.9 us
    pallas_call x1, Pallas kernels: 17.8 us -> 12.3 us  [send_buffer(): pl.pallas_call(_send_kernel, grid_spec=grid_spec, out_shape=jax.ShapeDtyp...]
where the time goes in v9:
time: 513 us; the launch traced here: 512 us
  waiting for transfers between devices  291 us (57%)
  blocking collectives  94.7 us (18%)
  Pallas kernels  42.9 us (8%)
  matrix products  35.3 us (7%)
  starting transfers between devices  17.6 us (3%)
  between operations  14.2 us (3%)
  local copies, waits for them, and re-layouts  9.7 us (2%)
  other arithmetic  6.8 us (1%)
    all_to_all x1, waiting for transfers between devices, local(): lax.all_to_all(send_buffer(key_blocks, value_blocks, send_index), 'ctx',...  224 us
    all_to_all x1, blocking collectives, local(): lax.all_to_all(jnp.broadcast_to(own_half[None], (data_count,) + own_half....  53.9 us
    reduce_scatter x1, waiting for transfers between devices, local(): stage = lax.psum_scatter(partial, 'ctx', scatter_dimension=0, tiled=True)  53 us
    all_to_all x1, blocking collectives, local(): lax.all_to_all(jnp.broadcast_to(piece[None], (ctx_count,) + piece.shape),...  23.3 us
    all_to_all x1, blocking collectives, local(): lax.all_to_all(stage.reshape(data_count, split, width), 'dp', split_axis=...  17.5 us
    pallas_call x1, Pallas kernels, forward_attention(): pl.pallas_call(_fwd_kernel, grid_spec=grid_spec, out_shape=[jax.ShapeDtyp...  15.7 us
    pallas_call x1, Pallas kernels, backward_attention(): pl.pallas_call(_bwd_kernel, grid_spec=grid_spec, out_shape=jax.ShapeDtype...  15 us
    pallas_call x1, Pallas kernels, send_buffer(): pl.pallas_call(_send_kernel, grid_spec=grid_spec, out_shape=jax.ShapeDtyp...  12.3 us
  transfers between devices with their start and end apart: 4, of which 4 were waited for; matrix products, arithmetic and copies ran while one was open for 6% of the time, Pallas kernels for 3%

profile of v9, /device:TPU:1, one launch (start us, length us, event | category | flops | bytes accessed | tf_op | source)
XLA Modules:
  0.0 511.8 jit_solution(14035620039435642942)
XLA Ops:
  7.2 0.9 copy.28
  8.0 0.1 squeeze.9
  8.1 0.6 broadcast_in_dim.12
  8.7 9.1 %all-to-all-start = ((s32[16,1,12]{2,1,0:T(1,128)}), s32[16,1,12]{2,1,0:T(1,128)S(1)}, u32[]{:S(2)}, u32[]{:S(2)}) async-start(s32[16,1,12]{2,1,0:T(1,128)} %broadcast_in_dim.12), calls=%async_computation | async-start | bytes 16384 | tf_op jit(solution)/shard_map/all_to_all | solution.py:173
  17.8 6.9 %all-to-all-done = s32[16,1,12]{2,1,0:T(1,128)S(1)} async-done(((s32[16,1,12]{2,1,0:T(1,128)}), s32[16,1,12]{2,1,0:T(1,128)S(1)}, u32[]{:S(2)}, u32[]{:S(2)}) %all-to-all-start) | async-done | bytes 800 | tf_op jit(solution)/shard_map/all_to_all | solution.py:173
  24.8 0.7 div.17
  25.5 0.6 fusion.6.index
  26.1 12.3 %shard_map.85 = bf16[16,128,4096]{2,1,0:T(8,128)(2,1)} custom-call(s32[16]{0:T(128)} %fusion.6.index, bf16[6,128,2048]{2,1,0:T(8,128)(2,1)} %bitcast.45, bf16[6,128,2048]{2,1,0:T(8,128)(2,1)} %bitcast.46, bf16[6,128,2048]{2,1,0:T(8,128)(2,1)} %bitcast.47, bf16[6,128,2048]{2,1,0:T(8,128)(2,1)} %bitcast.48), custom_call_target="tpu_custom_call" | custom-call | bytes 33554432 | tf_op jit(solution)/shard_map/pallas_call | solution.py:146
  38.4 6.6 %all-to-all-start.1 = ((bf16[16,128,4096]{2,1,0:T(8,128)(2,1)}), bf16[16,128,4096]{2,1,0:T(8,128)(2,1)}, u32[]{:S(2)}, u32[]{:S(2)}) async-start(bf16[16,128,4096]{2,1,0:T(8,128)(2,1)} %shard_map.85), calls=%async_computation.1 | async-start | bytes 33554432 | tf_op jit(solution)/shard_map/all_to_all | solution.py:182
  45.1 0.5 and_select_fusion.table
  45.6 223.5 %all-to-all-done.1.k0_ref.k1_ref.v0_ref.v1_ref = bf16[16,128,4096]{2,1,0:T(8,128)(2,1)} async-done(((bf16[16,128,4096]{2,1,0:T(8,128)(2,1)}), bf16[16,128,4096]{2,1,0:T(8,128)(2,1)}, u32[]{:S(2)}, u32[]{:S(2)}) %all-to-all-start.1) | async-done | bytes 16777248 | tf_op jit(solution)/shard_map/all_to_all | solution.py:182
  269.2 15.7 %shard_map.86 = (bf16[768,2048]{1,0:T(8,128)(2,1)}, f32[6,16,128,256]{3,2,1,0:T(8,128)}) custom-call(s32[12]{0:T(128)} %and_select_fusion.table, bf16[768,2048]{1,0:T(8,128)(2,1)} %bitcast.53, bf16[16,128,4096]{2,1,0:T(8,128)(2,1)} %all-to-all-done.1.k0_ref.k1_ref.v0_ref.v1_ref, bf16[16,128,4096]{2,1,0:T(8,128)(2,1)} %all-to-all-done.1.k0_ref.k1_ref.v0_ref.v1_ref, ...), custom_call_target="tpu_custom_call" | custom-call | flops 1610612736 | bytes 31457280 | tf_op jit(solution)/shard_map/pallas_call | solution.py:57
  284.8 4.6 copy.32
  289.5 2.4 copy.33
  291.9 0.4 copy-done.3
  292.3 9.5 %fusion.10 = f32[2048,2048]{1,0:T(8,128)} fusion(bf16[768,2048]{0,1:T(8,128)(2,1)S(1)} %bitcast.52, bf16[1,768,2048]{2,1,0:T(8,128)(2,1)S(1)} %copy-done.3), kind=kOutput, calls=%fused_computation.25 | convolution fusion | flops 6442450944 | bytes 23068672 | tf_op jit(solution)/shard_map/dot_general | solution.py:225
  301.8 0.5 broadcast_in_dim.13
  302.4 53.9 %all_to_all.26 = bf16[8,256,1024]{2,1,0:T(8,128)(2,1)} all-to-all(bf16[8,256,1024]{2,1,0:T(8,128)(2,1)S(1)} %broadcast_in_dim.13), channel_id=1, replica_groups=mesh['dp'=8,'ctx'=16] {'dp'}, dimensions={0} | all-to-all | bytes 8388608 | tf_op jit(solution)/shard_map/all_to_all | solution.py:196
  356.3 1.8 collective-permute-start
  358.1 7.1 %collective-permute-done = bf16[2048,1024]{1,0:T(8,128)(2,1)} collective-permute-done((bf16[2048,1024]{1,0:T(8,128)(2,1)}, bf16[2048,1024]{1,0:T(8,128)(2,1)}, u32[]{:S(2)}, u32[]{:S(2)}) %collective-permute-start) | collective-permute-done | bytes 4194336 | tf_op jit(solution)/shard_map/ppermute | solution.py:203
  365.2 5.9 %fusion.1 = f32[2048,768]{0,1:T(8,128)S(1)} fusion(bf16[2048,1024]{1,0:T(8,128)(2,1)} %collective-permute-done, bf16[2048,1024]{1,0:T(8,128)(2,1)} %bitcast.13, pred[]{:T(512)S(6)} %eq.16, bf16[768,2048]{1,0:T(8,128)(2,1)} %bitcast.57), kind=kOutput, calls=%fused_computation.7 | convolution fusion | flops 3223322624 | bytes 16252929 | tf_op jit(solution)/shard_map/dot_general | solution.py:216
  371.2 7.3 %fusion.back_ref = bf16[768,2048]{1,0:T(8,128)(2,1)} fusion(f32[2048,768]{0,1:T(8,128)S(1)} %fusion.1, bf16[2048,1024]{1,0:T(8,128)(2,1)} %bitcast.13, bf16[2048,1024]{1,0:T(8,128)(2,1)} %collective-permute-done, pred[]{:T(512)S(6)} %eq.16, bf16[768,2048]{1,0:T(8,128)(2,1)S(1)} %bitcast.58), kind=kOutput, calls=%fused_computation.4 | convolution fusion | flops 3226468352 | bytes 19398656 | tf_op jit(solution)/shard_map/dot_general | solution.py:214
  378.5 15.0 %shard_map.87 = bf16[768,2048]{1,0:T(8,128)(2,1)} custom-call(s32[12]{0:T(128)} %and_select_fusion.table, bf16[768,2048]{1,0:T(8,128)(2,1)} %fusion.back_ref, bf16[768,2048]{1,0:T(8,128)(2,1)} %get-tuple-element.11.att_ref, f32[6,16,128,256]{3,2,1,0:T(8,128)} %get-tuple-element.13.probs_ref, ...), custom_call_target="tpu_custom_call" | custom-call | flops 1610612736 | bytes 34603008 | tf_op jit(solution)/shard_map/pallas_call | solution.py:113
  393.4 6.9 %convolution_convert_fusion.1 = bf16[768,1024]{1,0:T(8,128)(2,1)S(1)} fusion(bf16[768,2048]{1,0:T(8,128)(2,1)} %get-tuple-element.11.att_ref, bf16[2048,1024]{1,0:T(8,128)(2,1)} %bitcast.13, bf16[2048,1024]{1,0:T(8,128)(2,1)} %collective-permute-done, pred[]{:T(512)S(6)} %eq.16), kind=kOutput, calls=%fused_computation.6 | convolution fusion | flops 3224109056 | bytes 13107201 | tf_op jit(solution)/shard_map/dot_general | solution.py:208
  400.4 5.7 %convolution_convert_fusion = bf16[768,1024]{1,0:T(8,128)(2,1)S(1)} fusion(bf16[768,2048]{1,0:T(8,128)(2,1)S(1)} %copy-done.2, bf16[2048,1024]{1,0:T(8,128)(2,1)} %collective-permute-done, bf16[2048,1024]{1,0:T(8,128)(2,1)} %bitcast.13, pred[]{:T(512)S(6)} %eq.16), kind=kOutput, calls=%fused_computation.5 | convolution fusion | flops 3224109056 | bytes 13107201 | tf_op jit(solution)/shard_map/dot_general | solution.py:209
  406.1 2.0 pad_maximum_fusion
  408.0 53.0 %reduce-scatter.2.cloned.1.call-done = f32[128,2048]{1,0:T(8,128)} async-done(((f32[2048,2048]{1,0:T(8,128)}), f32[128,2048]{1,0:T(8,128)}) %reduce-scatter.2.cloned.1.call-update) | async-done | bytes 1048592 | tf_op jit(solution)/shard_map/reduce_scatter | solution.py:228
  461.0 1.3 broadcast_multiply_fusion
  462.4 17.5 %all_to_all.27 = f32[8,16,2048]{2,1,0:T(8,128)S(1)} all-to-all(f32[8,16,2048]{2,1,0:T(8,128)S(1)} %bitcast.49), channel_id=1, replica_groups=mesh['dp'=8,'ctx'=16] {'dp'}, dimensions={0} | all-to-all | bytes 2097152 | tf_op jit(solution)/shard_map/all_to_all | solution.py:233
  479.9 0.1 broadcast_in_dim.29
  480.0 23.3 %all_to_all.28 = bf16[16,16,2048]{2,1,0:T(8,128)(2,1)S(1)} all-to-all(bf16[16,16,2048]{2,1,0:T(8,128)(2,1)S(1)} %broadcast_in_dim.29), channel_id=1, replica_groups=mesh['dp'=8,'ctx'=16] {'ctx'}, dimensions={0} | all-to-all | bytes 2097152 | tf_op jit(solution)/shard_map/all_to_all | solution.py:239
  503.3 1.6 bitcast_convert_fusion
  (14 shorter events, 0.2 us)
Async XLA Ops:
  7.2 37.9 %copy-start = (bf16[256,2048]{1,0:T(8,128)(2,1)S(1)}, bf16[256,2048]{1,0:T(8,128)(2,1)}, u32[]{:S(2)}) copy-start(bf16[256,2048]{1,0:T(8,128)(2,1)} %param.10) | copy-start | bytes 3145732
  8.7 16.1 %all-to-all-start = ((s32[16,1,12]{2,1,0:T(1,128)}), s32[16,1,12]{2,1,0:T(1,128)S(1)}, u32[]{:S(2)}, u32[]{:S(2)}) async-start(s32[16,1,12]{2,1,0:T(1,128)} %broadcast_in_dim.12), calls=%async_computation | async-start | bytes 16384 | tf_op jit(solution)/shard_map/all_to_all | solution.py:173
  38.4 230.8 %all-to-all-start.1 = ((bf16[16,128,4096]{2,1,0:T(8,128)(2,1)}), bf16[16,128,4096]{2,1,0:T(8,128)(2,1)}, u32[]{:S(2)}, u32[]{:S(2)}) async-start(bf16[16,128,4096]{2,1,0:T(8,128)(2,1)} %shard_map.85), calls=%async_computation.1 | async-start | bytes 33554432 | tf_op jit(solution)/shard_map/all_to_all | solution.py:182
  45.0 416.1 %reduce-scatter.2.cloned.1.call-start = ((), (), s32[]{:S(2)}) async-start(), calls=%async_computation.6 | async-start | bytes 17825792 | tf_op jit(solution)/shard_map/reduce_scatter | solution.py:228
  289.5 2.8 copy-start.3
  356.3 9.0 %collective-permute-start = (bf16[2048,1024]{1,0:T(8,128)(2,1)}, bf16[2048,1024]{1,0:T(8,128)(2,1)}, u32[]{:S(2)}, u32[]{:S(2)}) collective-permute-start(bf16[2048,1024]{1,0:T(8,128)(2,1)} %bitcast.13), channel_id=1, source_target_pairs={{0,1},{1,0},{2,3},{3,2},{4,5},{5,4},{6,7},{7,6},{8,9},{9,8},{10,11... | collective-permute-start | bytes 12582920 | tf_op jit(solution)/shard_map/ppermute | solution.py:203
  365.2 5.9 %copy-start.4 = (bf16[1,768,2048]{2,1,0:T(8,128)(2,1)S(1)}, bf16[1,768,2048]{2,1,0:T(8,128)(2,1)}, u32[]{:S(2)}) copy-start(bf16[1,768,2048]{2,1,0:T(8,128)(2,1)} %param.9) | copy-start | bytes 9437188
  393.4 6.9 %copy-start.2 = (bf16[768,2048]{1,0:T(8,128)(2,1)S(1)}, bf16[768,2048]{1,0:T(8,128)(2,1)}, u32[]{:S(2)}) copy-start(bf16[768,2048]{1,0:T(8,128)(2,1)} %get-tuple-element.11.att_ref) | copy-start | bytes 9437188
  479.8 25.1 %copy-start.1 = (bf16[256,2048]{1,0:T(8,128)(2,1)S(1)}, bf16[256,2048]{1,0:T(8,128)(2,1)}, u32[]{:S(2)}) copy-start(bf16[256,2048]{1,0:T(8,128)(2,1)} %param.10) | copy-start | bytes 3145732
Sparse Core Ops, SparseCore 0:
  302.0 159.0 reduce-scatter.1

commit v10 on v9

--- a/solution.py
+++ b/solution.py
@@ -13,21 +13,24 @@
 KSEL = 2
 
 
-def _fwd_kernel(table, q_ref, k0_ref, k1_ref, v0_ref, v1_ref, att_ref, probs_ref):
+def _head_probs(q_ref, k0_ref, k1_ref, lanes):
     scale = 1.0 / math.sqrt(DH)
+    keys = jnp.concatenate([k0_ref[0, :, lanes], k1_ref[0, :, lanes]], axis=0)
+    scores = lax.dot_general(
+        q_ref[:, lanes], keys, (((1,), (1,)), ((), ())), preferred_element_type=jnp.float32
+    ) * scale
+    top = jnp.max(scores, axis=-1, keepdims=True)
+    weights = jnp.exp(scores - top)
+    return weights / jnp.sum(weights, axis=-1, keepdims=True), keys
+
+
+def _fwd_kernel(table, q_ref, k0_ref, k1_ref, v0_ref, v1_ref, att_ref):
     for h in range(HEADS):
         lanes = slice(h * DH, (h + 1) * DH)
-        keys = jnp.concatenate([k0_ref[0, :, lanes], k1_ref[0, :, lanes]], axis=0)
-        scores = lax.dot_general(
-            q_ref[:, lanes], keys, (((1,), (1,)), ((), ())), preferred_element_type=jnp.float32
-        ) * scale
-        top = jnp.max(scores, axis=-1, keepdims=True)
-        weights = jnp.exp(scores - top)
-        probs = weights / jnp.sum(weights, axis=-1, keepdims=True)
+        probs, _ = _head_probs(q_ref, k0_ref, k1_ref, lanes)
         vals = jnp.concatenate([v0_ref[0, :, lanes], v1_ref[0, :, lanes]], axis=0)
         att = jnp.dot(probs.astype(jnp.bfloat16), vals, preferred_element_type=jnp.float32)
         att_ref[:, lanes] = att.astype(att_ref.dtype)
-        probs_ref[0, h] = probs
 
 
 def forward_attention(query_flat, got, order):
@@ -48,31 +51,26 @@
             kv(0, 1),
             kv(1, 1),
         ],
-        out_specs=[
-            pl.BlockSpec((BLK, width), lambda b, t: (b, 0)),
-            pl.BlockSpec((1, heads, BLK, KSEL * BLK), lambda b, t: (b, 0, 0, 0)),
-        ],
+        out_specs=pl.BlockSpec((BLK, width), lambda b, t: (b, 0)),
     )
     flops = blocks * heads * 4 * BLK * KSEL * BLK * DH
     return pl.pallas_call(
         _fwd_kernel,
         grid_spec=grid_spec,
-        out_shape=[
-            jax.ShapeDtypeStruct((rows, width), jnp.bfloat16),
-            jax.ShapeDtypeStruct((blocks, heads, BLK, KSEL * BLK), jnp.float32),
-        ],
+        out_shape=jax.ShapeDtypeStruct((rows, width), jnp.bfloat16),
         cost_estimate=pl.CostEstimate(
             flops=flops,
             transcendentals=blocks * heads * BLK * KSEL * BLK,
-            bytes_accessed=rows * width * 2 * 6 + blocks * heads * BLK * KSEL * BLK * 4,
+            bytes_accessed=rows * width * 2 * 6,
         ),
     )(order, query_flat, got, got, got, got)
 
 
-def _bwd_kernel(table, back_ref, att_ref, probs_ref, k0_ref, k1_ref, v0_ref, v1_ref, out_ref):
+def _bwd_kernel(table, q_ref, back_ref, att_ref, k0_ref, k1_ref, v0_ref, v1_ref, out_ref):
     scale = 1.0 / math.sqrt(DH)
     for h in range(HEADS):
         lanes = slice(h * DH, (h + 1) * DH)
+        probs, keys = _head_probs(q_ref, k0_ref, k1_ref, lanes)
         back = back_ref[:, lanes]
         vals = jnp.concatenate([v0_ref[0, :, lanes], v1_ref[0, :, lanes]], axis=0)
         dprobs = lax.dot_general(
@@ -81,13 +79,12 @@
         delta = jnp.sum(
             back.astype(jnp.float32) * att_ref[:, lanes].astype(jnp.float32), axis=-1, keepdims=True
         )
-        dscores = (probs_ref[0, h] * (dprobs - delta)).astype(jnp.bfloat16)
-        keys = jnp.concatenate([k0_ref[0, :, lanes], k1_ref[0, :, lanes]], axis=0)
+        dscores = (probs * (dprobs - delta)).astype(jnp.bfloat16)
         grad = jnp.dot(dscores, keys, preferred_element_type=jnp.float32) * scale
         out_ref[:, lanes] = grad.astype(out_ref.dtype)
 
 
-def backward_attention(back_flat, attention_flat, probs, got, order):
+def backward_attention(query_flat, back_flat, attention_flat, got, order):
     rows, width = back_flat.shape
     blocks = rows // BLK
     heads = width // DH
@@ -101,7 +98,7 @@
         in_specs=[
             pl.BlockSpec((BLK, width), lambda b, t: (b, 0)),
             pl.BlockSpec((BLK, width), lambda b, t: (b, 0)),
-            pl.BlockSpec((1, heads, BLK, KSEL * BLK), lambda b, t: (b, 0, 0, 0)),
+            pl.BlockSpec((BLK, width), lambda b, t: (b, 0)),
             kv(0, 0),
             kv(1, 0),
             kv(0, 1),
@@ -116,10 +113,10 @@
         out_shape=jax.ShapeDtypeStruct((rows, width), jnp.bfloat16),
         cost_estimate=pl.CostEstimate(
             flops=flops,
-            transcendentals=0,
-            bytes_accessed=rows * width * 2 * 7 + blocks * heads * BLK * KSEL * BLK * 4,
-        ),
-    )(order, back_flat, attention_flat, probs, got, got, got, got)
+            transcendentals=blocks * heads * BLK * KSEL * BLK,
+            bytes_accessed=rows * width * 2 * 8,
+        ),
+    )(order, query_flat, back_flat, attention_flat, got, got, got, got)
 
 
 def _send_kernel(index, k0_ref, k1_ref, v0_ref, v1_ref, o_ref):
@@ -187,7 +184,7 @@
         tiled=True,
     )
     order = owner.reshape(-1)
-    attention_flat, probs = forward_attention(queries[0], got, order)
+    attention_flat = forward_attention(queries[0], got, order)
     grad_flat = grad_out[0]
     half = out_weight.shape[1] // 2
     side = own_index % 2
@@ -226,7 +223,7 @@
         columns, grad_flat, (((0,), (0,)), ((), ())), preferred_element_type=jnp.float32
     )
     stage = lax.psum_scatter(partial, "ctx", scatter_dimension=0, tiled=True)
-    query_grad = backward_attention(back, attention_flat, probs, got, order)
+    query_grad = backward_attention(queries[0], back, attention_flat, got, order)
     stage, mixed, query_grad = lax.optimization_barrier((stage, mixed, query_grad))
     stage = stage * (1.0 / math.sqrt(rows * ctx_count * data_count))
     shard = jnp.sum(

time: 513 us -> 510 us (level)
  waiting for transfers between devices: 291 us -> 282 us
  Pallas kernels: 42.9 us -> 50.7 us
    pallas_call x1, Pallas kernels: 15 us -> 23.3 us  [backward_attention(): pl.pallas_call(_bwd_kernel, grid_spec=grid_spec, out_shape=jax.ShapeDtype...]
    reduce_scatter x1, waiting for transfers between devices: 53 us -> 44.8 us  [local(): stage = lax.psum_scatter(partial, 'ctx', scatter_dimension=0, tiled=True)]
  transfers between devices with their start and end apart: 4 -> 4, of which waited for: 4 -> 4; matrix products, arithmetic and copies ran while one was open for 6% -> 6% of each run, Pallas kernels for 3% -> 5%
where the time goes in v10:
time: 510 us
  waiting for transfers between devices  282 us (55%)
  blocking collectives  93.9 us (18%)
  Pallas kernels  50.7 us (10%)
  matrix products  35.3 us (7%)
  starting transfers between devices  16.6 us (3%)
  between operations  14.2 us (3%)
  local copies, waits for them, and re-layouts  9.7 us (2%)
  other arithmetic  6.8 us (1%)
    all_to_all x1, waiting for transfers between devices, local(): lax.all_to_all(send_buffer(key_blocks, value_blocks, send_index), 'ctx',...  224 us
    all_to_all x1, blocking collectives, local(): lax.all_to_all(jnp.broadcast_to(own_half[None], (data_count,) + own_half....  53.1 us
    reduce_scatter x1, waiting for transfers between devices, local(): stage = lax.psum_scatter(partial, 'ctx', scatter_dimension=0, tiled=True)  44.8 us
    pallas_call x1, Pallas kernels, backward_attention(): pl.pallas_call(_bwd_kernel, grid_spec=grid_spec, out_shape=jax.ShapeDtype...  23.3 us
    all_to_all x1, blocking collectives, local(): lax.all_to_all(jnp.broadcast_to(piece[None], (ctx_count,) + piece.shape),...  23.2 us
    all_to_all x1, blocking collectives, local(): lax.all_to_all(stage.reshape(data_count, split, width), 'dp', split_axis=...  17.6 us
    pallas_call x1, Pallas kernels, send_buffer(): pl.pallas_call(_send_kernel, grid_spec=grid_spec, out_shape=jax.ShapeDtyp...  14 us
    pallas_call x1, Pallas kernels, forward_attention(): pl.pallas_call(_fwd_kernel, grid_spec=grid_spec, out_shape=jax.ShapeDtype...  13.4 us
  transfers between devices with their start and end apart: 4, of which 4 were waited for; matrix products, arithmetic and copies ran while one was open for 6% of the time, Pallas kernels for 5%

profile of v10, /device:TPU:1, one launch (start us, length us, event | category | flops | bytes accessed | tf_op | source)
XLA Modules:
  0.0 509.5 jit_solution(13375733186769831773)
XLA Ops:
  7.2 0.9 copy.28
  8.0 0.1 squeeze.10
  8.1 0.6 broadcast_in_dim.12
  8.7 9.1 %all-to-all-start = ((s32[16,1,12]{2,1,0:T(1,128)}), s32[16,1,12]{2,1,0:T(1,128)S(1)}, u32[]{:S(2)}, u32[]{:S(2)}) async-start(s32[16,1,12]{2,1,0:T(1,128)} %broadcast_in_dim.12), calls=%async_computation | async-start | bytes 16384 | tf_op jit(solution)/shard_map/all_to_all | solution.py:170
  17.8 6.9 %all-to-all-done = s32[16,1,12]{2,1,0:T(1,128)S(1)} async-done(((s32[16,1,12]{2,1,0:T(1,128)}), s32[16,1,12]{2,1,0:T(1,128)S(1)}, u32[]{:S(2)}, u32[]{:S(2)}) %all-to-all-start) | async-done | bytes 800 | tf_op jit(solution)/shard_map/all_to_all | solution.py:170
  24.8 0.7 div.17
  25.5 0.6 fusion.6.index
  26.1 14.0 %shard_map.85 = bf16[16,128,4096]{2,1,0:T(8,128)(2,1)} custom-call(s32[16]{0:T(128)} %fusion.6.index, bf16[6,128,2048]{2,1,0:T(8,128)(2,1)} %bitcast.47, bf16[6,128,2048]{2,1,0:T(8,128)(2,1)} %bitcast.48, bf16[6,128,2048]{2,1,0:T(8,128)(2,1)} %bitcast.49, bf16[6,128,2048]{2,1,0:T(8,128)(2,1)} %bitcast.50), custom_call_target="tpu_custom_call" | custom-call | bytes 33554432 | tf_op jit(solution)/shard_map/pallas_call | solution.py:143
  40.0 5.6 %all-to-all-start.1 = ((bf16[16,128,4096]{2,1,0:T(8,128)(2,1)}), bf16[16,128,4096]{2,1,0:T(8,128)(2,1)}, u32[]{:S(2)}, u32[]{:S(2)}) async-start(bf16[16,128,4096]{2,1,0:T(8,128)(2,1)} %shard_map.85), calls=%async_computation.1 | async-start | bytes 33554432 | tf_op jit(solution)/shard_map/all_to_all | solution.py:179
  45.8 0.5 and_select_fusion.table
  46.3 223.5 %all-to-all-done.1.k0_ref.k1_ref.v0_ref.v1_ref = bf16[16,128,4096]{2,1,0:T(8,128)(2,1)} async-done(((bf16[16,128,4096]{2,1,0:T(8,128)(2,1)}), bf16[16,128,4096]{2,1,0:T(8,128)(2,1)}, u32[]{:S(2)}, u32[]{:S(2)}) %all-to-all-start.1) | async-done | bytes 16777248 | tf_op jit(solution)/shard_map/all_to_all | solution.py:179
  269.9 13.4 %shard_map.86.att_ref = bf16[768,2048]{1,0:T(8,128)(2,1)} custom-call(s32[12]{0:T(128)} %and_select_fusion.table, bf16[768,2048]{1,0:T(8,128)(2,1)} %bitcast.44, bf16[16,128,4096]{2,1,0:T(8,128)(2,1)} %all-to-all-done.1.k0_ref.k1_ref.v0_ref.v1_ref, bf16[16,128,4096]{2,1,0:T(8,128)(2,1)} %all-to-all-done.1.k0_ref.k1_ref.v0_ref.v1_ref, ...), custom_call_target="tpu_custom_call" | custom-call | flops 1610612736 | bytes 18874368 | tf_op jit(solution)/shard_map/pallas_call | solution.py:57
  283.3 4.6 copy.32
  287.9 2.4 copy.33
  290.3 0.4 copy-done.3
  290.8 9.5 %fusion.10 = f32[2048,2048]{1,0:T(8,128)} fusion(bf16[768,2048]{0,1:T(8,128)(2,1)S(1)} %bitcast.54, bf16[1,768,2048]{2,1,0:T(8,128)(2,1)S(1)} %copy-done.3), kind=kOutput, calls=%fused_computation.25 | convolution fusion | flops 6442450944 | bytes 23068672 | tf_op jit(solution)/shard_map/dot_general | solution.py:222
  300.3 0.5 broadcast_in_dim.13
  300.8 53.1 %all_to_all.26 = bf16[8,256,1024]{2,1,0:T(8,128)(2,1)} all-to-all(bf16[8,256,1024]{2,1,0:T(8,128)(2,1)S(1)} %broadcast_in_dim.13), channel_id=1, replica_groups=mesh['dp'=8,'ctx'=16] {'dp'}, dimensions={0} | all-to-all | bytes 8388608 | tf_op jit(solution)/shard_map/all_to_all | solution.py:193
  353.9 1.8 collective-permute-start
  355.8 7.1 %collective-permute-done = bf16[2048,1024]{1,0:T(8,128)(2,1)} collective-permute-done((bf16[2048,1024]{1,0:T(8,128)(2,1)}, bf16[2048,1024]{1,0:T(8,128)(2,1)}, u32[]{:S(2)}, u32[]{:S(2)}) %collective-permute-start) | collective-permute-done | bytes 4194336 | tf_op jit(solution)/shard_map/ppermute | solution.py:200
  362.9 5.9 %fusion.1 = f32[2048,768]{0,1:T(8,128)S(1)} fusion(bf16[2048,1024]{1,0:T(8,128)(2,1)} %collective-permute-done, bf16[2048,1024]{1,0:T(8,128)(2,1)} %bitcast.13, pred[]{:T(512)S(6)} %eq.16, bf16[768,2048]{1,0:T(8,128)(2,1)} %bitcast.58), kind=kOutput, calls=%fused_computation.7 | convolution fusion | flops 3223322624 | bytes 16252929 | tf_op jit(solution)/shard_map/dot_general | solution.py:213
  368.8 7.3 %fusion.back_ref = bf16[768,2048]{1,0:T(8,128)(2,1)} fusion(f32[2048,768]{0,1:T(8,128)S(1)} %fusion.1, bf16[2048,1024]{1,0:T(8,128)(2,1)} %bitcast.13, bf16[2048,1024]{1,0:T(8,128)(2,1)} %collective-permute-done, pred[]{:T(512)S(6)} %eq.16, bf16[768,2048]{1,0:T(8,128)(2,1)S(1)} %bitcast.59), kind=kOutput, calls=%fused_computation.4 | convolution fusion | flops 3226468352 | bytes 19398656 | tf_op jit(solution)/shard_map/dot_general | solution.py:211
  376.2 23.3 %shard_map.87 = bf16[768,2048]{1,0:T(8,128)(2,1)} custom-call(s32[12]{0:T(128)} %and_select_fusion.table, bf16[768,2048]{1,0:T(8,128)(2,1)} %bitcast.45, bf16[768,2048]{1,0:T(8,128)(2,1)} %fusion.back_ref, bf16[768,2048]{1,0:T(8,128)(2,1)} %shard_map.86.att_ref, bf16[16,128,4096]{2,1,0:T(8,128)(2,1)} %all-to-all-done.1.k0_ref.k1_ref.v0_ref.v1_ref, ...), custom_call_target="tpu_custom_call" | custom-call | flops 1610612736 | bytes 25165824 | tf_op jit(solution)/shard_map/pallas_call | solution.py:110
  399.5 6.7 %convolution_convert_fusion.1 = bf16[768,1024]{1,0:T(8,128)(2,1)S(1)} fusion(bf16[768,2048]{1,0:T(8,128)(2,1)} %shard_map.86.att_ref, bf16[2048,1024]{1,0:T(8,128)(2,1)} %bitcast.13, bf16[2048,1024]{1,0:T(8,128)(2,1)} %collective-permute-done, pred[]{:T(512)S(6)} %eq.16), kind=kOutput, calls=%fused_computation.6 | convolution fusion | flops 3224109056 | bytes 13107201 | tf_op jit(solution)/shard_map/dot_general | solution.py:205
  406.2 5.9 %convolution_convert_fusion = bf16[768,1024]{1,0:T(8,128)(2,1)S(1)} fusion(bf16[768,2048]{1,0:T(8,128)(2,1)S(1)} %copy-done.2, bf16[2048,1024]{1,0:T(8,128)(2,1)} %collective-permute-done, bf16[2048,1024]{1,0:T(8,128)(2,1)} %bitcast.13, pred[]{:T(512)S(6)} %eq.16), kind=kOutput, calls=%fused_computation.5 | convolution fusion | flops 3224109056 | bytes 13107201 | tf_op jit(solution)/shard_map/dot_general | solution.py:206
  412.0 2.0 pad_maximum_fusion
  414.0 44.8 %reduce-scatter.2.cloned.1.call-done = f32[128,2048]{1,0:T(8,128)} async-done(((f32[2048,2048]{1,0:T(8,128)}), f32[128,2048]{1,0:T(8,128)}) %reduce-scatter.2.cloned.1.call-update) | async-done | bytes 1048592 | tf_op jit(solution)/shard_map/reduce_scatter | solution.py:225
  458.8 1.3 broadcast_multiply_fusion
  460.1 17.6 %all_to_all.27 = f32[8,16,2048]{2,1,0:T(8,128)S(1)} all-to-all(f32[8,16,2048]{2,1,0:T(8,128)S(1)} %bitcast.51), channel_id=1, replica_groups=mesh['dp'=8,'ctx'=16] {'dp'}, dimensions={0} | all-to-all | bytes 2097152 | tf_op jit(solution)/shard_map/all_to_all | solution.py:230
  477.7 0.1 broadcast_in_dim.29
  477.8 23.2 %all_to_all.28 = bf16[16,16,2048]{2,1,0:T(8,128)(2,1)S(1)} all-to-all(bf16[16,16,2048]{2,1,0:T(8,128)(2,1)S(1)} %broadcast_in_dim.29), channel_id=1, replica_groups=mesh['dp'=8,'ctx'=16] {'ctx'}, dimensions={0} | all-to-all | bytes 2097152 | tf_op jit(solution)/shard_map/all_to_all | solution.py:236
  501.0 1.6 bitcast_convert_fusion
  (14 shorter events, 0.2 us)
Async XLA Ops:
  7.2 38.6 %copy-start = (bf16[256,2048]{1,0:T(8,128)(2,1)S(1)}, bf16[256,2048]{1,0:T(8,128)(2,1)}, u32[]{:S(2)}) copy-start(bf16[256,2048]{1,0:T(8,128)(2,1)} %param.10) | copy-start | bytes 3145732
  8.7 16.1 %all-to-all-start = ((s32[16,1,12]{2,1,0:T(1,128)}), s32[16,1,12]{2,1,0:T(1,128)S(1)}, u32[]{:S(2)}, u32[]{:S(2)}) async-start(s32[16,1,12]{2,1,0:T(1,128)} %broadcast_in_dim.12), calls=%async_computation | async-start | bytes 16384 | tf_op jit(solution)/shard_map/all_to_all | solution.py:170
  40.0 229.8 %all-to-all-start.1 = ((bf16[16,128,4096]{2,1,0:T(8,128)(2,1)}), bf16[16,128,4096]{2,1,0:T(8,128)(2,1)}, u32[]{:S(2)}, u32[]{:S(2)}) async-start(bf16[16,128,4096]{2,1,0:T(8,128)(2,1)} %shard_map.85), calls=%async_computation.1 | async-start | bytes 33554432 | tf_op jit(solution)/shard_map/all_to_all | solution.py:179
  45.7 413.1 %reduce-scatter.2.cloned.1.call-start = ((), (), s32[]{:S(2)}) async-start(), calls=%async_computation.6 | async-start | bytes 17825792 | tf_op jit(solution)/shard_map/reduce_scatter | solution.py:225
  287.9 2.8 copy-start.3
  353.9 9.0 %collective-permute-start = (bf16[2048,1024]{1,0:T(8,128)(2,1)}, bf16[2048,1024]{1,0:T(8,128)(2,1)}, u32[]{:S(2)}, u32[]{:S(2)}) collective-permute-start(bf16[2048,1024]{1,0:T(8,128)(2,1)} %bitcast.13), channel_id=1, source_target_pairs={{0,1},{1,0},{2,3},{3,2},{4,5},{5,4},{6,7},{7,6},{8,9},{9,8},{10,11... | collective-permute-start | bytes 12582920 | tf_op jit(solution)/shard_map/ppermute | solution.py:200
  362.9 5.9 %copy-start.4 = (bf16[1,768,2048]{2,1,0:T(8,128)(2,1)S(1)}, bf16[1,768,2048]{2,1,0:T(8,128)(2,1)}, u32[]{:S(2)}) copy-start(bf16[1,768,2048]{2,1,0:T(8,128)(2,1)} %param.9) | copy-start | bytes 9437188
  399.5 6.7 %copy-start.2 = (bf16[768,2048]{1,0:T(8,128)(2,1)S(1)}, bf16[768,2048]{1,0:T(8,128)(2,1)}, u32[]{:S(2)}) copy-start(bf16[768,2048]{1,0:T(8,128)(2,1)} %shard_map.86.att_ref) | copy-start | bytes 9437188
  477.7 25.0 %copy-start.1 = (bf16[256,2048]{1,0:T(8,128)(2,1)S(1)}, bf16[256,2048]{1,0:T(8,128)(2,1)}, u32[]{:S(2)}) copy-start(bf16[256,2048]{1,0:T(8,128)(2,1)} %param.10) | copy-start | bytes 3145732
Sparse Core Ops, SparseCore 0:
  300.4 158.2 reduce-scatter.1

commit v11 on v10

--- a/solution.py
+++ b/solution.py
@@ -119,33 +119,34 @@
     )(order, query_flat, back_flat, attention_flat, got, got, got, got)
 
 
-def _send_kernel(index, k0_ref, k1_ref, v0_ref, v1_ref, o_ref):
-    width = k0_ref.shape[-1]
-    o_ref[0, :, :width] = k0_ref[0]
-    o_ref[0, :, width:] = v0_ref[0]
-    o_ref[1, :, :width] = k1_ref[0]
-    o_ref[1, :, width:] = v1_ref[0]
-
-
-def send_buffer(key_blocks, value_blocks, send_index):
+def _send_kernel(index, *refs):
+    o_ref = refs[-1]
+    slots = (len(refs) - 1) // 2
+    width = refs[0].shape[-1]
+    for s in range(slots):
+        o_ref[s, :, :width] = refs[s][0]
+        o_ref[s, :, width:] = refs[slots + s][0]
+
+
+def send_buffer(key_blocks, value_blocks, send_index, slots=4):
     count = send_index.shape[0]
     _, blk, width = key_blocks.shape
 
     def pick(k):
-        return pl.BlockSpec((1, blk, width), lambda d, t: (t[2 * d + k], 0, 0))
+        return pl.BlockSpec((1, blk, width), lambda d, t: (t[slots * d + k], 0, 0))
 
     grid_spec = pltpu.PrefetchScalarGridSpec(
         num_scalar_prefetch=1,
-        grid=(count // 2,),
-        in_specs=[pick(0), pick(1), pick(0), pick(1)],
-        out_specs=pl.BlockSpec((2, blk, 2 * width), lambda d, t: (d, 0, 0)),
+        grid=(count // slots,),
+        in_specs=[pick(k) for k in range(slots)] * 2,
+        out_specs=pl.BlockSpec((slots, blk, 2 * width), lambda d, t: (d, 0, 0)),
     )
     return pl.pallas_call(
         _send_kernel,
         grid_spec=grid_spec,
         out_shape=jax.ShapeDtypeStruct((count, blk, 2 * width), key_blocks.dtype),
         cost_estimate=pl.CostEstimate(flops=0, transcendentals=0, bytes_accessed=count * blk * width * 8),
-    )(send_index, key_blocks, key_blocks, value_blocks, value_blocks)
+    )(send_index, *([key_blocks] * slots), *([value_blocks] * slots))
 
 
 def softmax_rows(scores):

time: 510 us -> 509 us (level)
  no operation moved by 1% of the time
where the time goes in v11:
time: 509 us; the launch traced here: 508 us
  waiting for transfers between devices  281 us (55%)
  blocking collectives  94 us (18%)
  Pallas kernels  50.9 us (10%)
  matrix products  35.3 us (7%)
  starting transfers between devices  16.1 us (3%)
  between operations  14.2 us (3%)
  local copies, waits for them, and re-layouts  9.7 us (2%)
  other arithmetic  6.8 us (1%)
    all_to_all x1, waiting for transfers between devices, local(): lax.all_to_all(send_buffer(key_blocks, value_blocks, send_index), 'ctx',...  223 us
    all_to_all x1, blocking collectives, local(): lax.all_to_all(jnp.broadcast_to(own_half[None], (data_count,) + own_half....  53.2 us
    reduce_scatter x1, waiting for transfers between devices, local(): stage = lax.psum_scatter(partial, 'ctx', scatter_dimension=0, tiled=True)  44.5 us
    all_to_all x1, blocking collectives, local(): lax.all_to_all(jnp.broadcast_to(piece[None], (ctx_count,) + piece.shape),...  23.3 us
    pallas_call x1, Pallas kernels, backward_attention(): pl.pallas_call(_bwd_kernel, grid_spec=grid_spec, out_shape=jax.ShapeDtype...  23.3 us
    all_to_all x1, blocking collectives, local(): lax.all_to_all(stage.reshape(data_count, split, width), 'dp', split_axis=...  17.5 us
    pallas_call x1, Pallas kernels, send_buffer(): pl.pallas_call(_send_kernel, grid_spec=grid_spec, out_shape=jax.ShapeDtyp...  14.2 us
    pallas_call x1, Pallas kernels, forward_attention(): pl.pallas_call(_fwd_kernel, grid_spec=grid_spec, out_shape=jax.ShapeDtype...  13.4 us
  transfers between devices with their start and end apart: 4, of which 4 were waited for; matrix products, arithmetic and copies ran while one was open for 6% of the time, Pallas kernels for 5%

profile of v11, /device:TPU:1, one launch (start us, length us, event | category | flops | bytes accessed | tf_op | source)
XLA Modules:
  0.0 508.1 jit_solution(16039564730146283861)
XLA Ops:
  7.2 0.9 copy.28
  8.0 0.1 squeeze.10
  8.1 0.6 broadcast_in_dim.12
  8.7 9.1 %all-to-all-start = ((s32[16,1,12]{2,1,0:T(1,128)}), s32[16,1,12]{2,1,0:T(1,128)S(1)}, u32[]{:S(2)}, u32[]{:S(2)}) async-start(s32[16,1,12]{2,1,0:T(1,128)} %broadcast_in_dim.12), calls=%async_computation | async-start | bytes 16384 | tf_op jit(solution)/shard_map/all_to_all | solution.py:171
  17.8 6.9 %all-to-all-done = s32[16,1,12]{2,1,0:T(1,128)S(1)} async-done(((s32[16,1,12]{2,1,0:T(1,128)}), s32[16,1,12]{2,1,0:T(1,128)S(1)}, u32[]{:S(2)}, u32[]{:S(2)}) %all-to-all-start) | async-done | bytes 800 | tf_op jit(solution)/shard_map/all_to_all | solution.py:171
  24.8 0.7 div.17
  25.5 0.6 fusion.6.index
  26.1 14.2 %shard_map.85 = bf16[16,128,4096]{2,1,0:T(8,128)(2,1)} custom-call(s32[16]{0:T(128)} %fusion.6.index, bf16[6,128,2048]{2,1,0:T(8,128)(2,1)} %bitcast.44, bf16[6,128,2048]{2,1,0:T(8,128)(2,1)} %bitcast.45, bf16[6,128,2048]{2,1,0:T(8,128)(2,1)} %bitcast.46, bf16[6,128,2048]{2,1,0:T(8,128)(2,1)} %bitcast.47, bf16[6,128,2048]{2,1,0:T(8,128)(2,1)} %bitcast.48, ...), custom_call_target="tpu_custom_call" | custom-call | bytes 33554432 | tf_op jit(solution)/shard_map/pallas_call | solution.py:144
  40.3 5.1 all-to-all-start.1
  45.5 0.5 and_select_fusion.table
  46.0 222.7 %all-to-all-done.1.k0_ref.k1_ref.v0_ref.v1_ref = bf16[16,128,4096]{2,1,0:T(8,128)(2,1)} async-done(((bf16[16,128,4096]{2,1,0:T(8,128)(2,1)}), bf16[16,128,4096]{2,1,0:T(8,128)(2,1)}, u32[]{:S(2)}, u32[]{:S(2)}) %all-to-all-start.1) | async-done | bytes 16777248 | tf_op jit(solution)/shard_map/all_to_all | solution.py:180
  268.7 13.4 %shard_map.86.att_ref = bf16[768,2048]{1,0:T(8,128)(2,1)} custom-call(s32[12]{0:T(128)} %and_select_fusion.table, bf16[768,2048]{1,0:T(8,128)(2,1)} %bitcast.52, bf16[16,128,4096]{2,1,0:T(8,128)(2,1)} %all-to-all-done.1.k0_ref.k1_ref.v0_ref.v1_ref, bf16[16,128,4096]{2,1,0:T(8,128)(2,1)} %all-to-all-done.1.k0_ref.k1_ref.v0_ref.v1_ref, ...), custom_call_target="tpu_custom_call" | custom-call | flops 1610612736 | bytes 18874368 | tf_op jit(solution)/shard_map/pallas_call | solution.py:57
  282.1 4.6 copy.32
  286.7 2.4 copy.33
  289.1 0.4 copy-done.3
  289.6 9.5 %fusion.10 = f32[2048,2048]{1,0:T(8,128)} fusion(bf16[768,2048]{0,1:T(8,128)(2,1)S(1)} %bitcast.58, bf16[1,768,2048]{2,1,0:T(8,128)(2,1)S(1)} %copy-done.3), kind=kOutput, calls=%fused_computation.25 | convolution fusion | flops 6442450944 | bytes 23068672 | tf_op jit(solution)/shard_map/dot_general | solution.py:223
  299.1 0.5 broadcast_in_dim.13
  299.7 53.2 %all_to_all.26 = bf16[8,256,1024]{2,1,0:T(8,128)(2,1)} all-to-all(bf16[8,256,1024]{2,1,0:T(8,128)(2,1)S(1)} %broadcast_in_dim.13), channel_id=1, replica_groups=mesh['dp'=8,'ctx'=16] {'dp'}, dimensions={0} | all-to-all | bytes 8388608 | tf_op jit(solution)/shard_map/all_to_all | solution.py:194
  352.8 1.8 collective-permute-start
  354.6 7.1 %collective-permute-done = bf16[2048,1024]{1,0:T(8,128)(2,1)} collective-permute-done((bf16[2048,1024]{1,0:T(8,128)(2,1)}, bf16[2048,1024]{1,0:T(8,128)(2,1)}, u32[]{:S(2)}, u32[]{:S(2)}) %collective-permute-start) | collective-permute-done | bytes 4194336 | tf_op jit(solution)/shard_map/ppermute | solution.py:201
  361.8 5.9 %fusion.1 = f32[2048,768]{0,1:T(8,128)S(1)} fusion(bf16[2048,1024]{1,0:T(8,128)(2,1)} %collective-permute-done, bf16[2048,1024]{1,0:T(8,128)(2,1)} %bitcast.13, pred[]{:T(512)S(6)} %eq.16, bf16[768,2048]{1,0:T(8,128)(2,1)} %bitcast.62), kind=kOutput, calls=%fused_computation.7 | convolution fusion | flops 3223322624 | bytes 16252929 | tf_op jit(solution)/shard_map/dot_general | solution.py:214
  367.7 7.3 %fusion.back_ref = bf16[768,2048]{1,0:T(8,128)(2,1)} fusion(f32[2048,768]{0,1:T(8,128)S(1)} %fusion.1, bf16[2048,1024]{1,0:T(8,128)(2,1)} %bitcast.13, bf16[2048,1024]{1,0:T(8,128)(2,1)} %collective-permute-done, pred[]{:T(512)S(6)} %eq.16, bf16[768,2048]{1,0:T(8,128)(2,1)S(1)} %bitcast.63), kind=kOutput, calls=%fused_computation.4 | convolution fusion | flops 3226468352 | bytes 19398656 | tf_op jit(solution)/shard_map/dot_general | solution.py:212
  375.0 23.3 %shard_map.87 = bf16[768,2048]{1,0:T(8,128)(2,1)} custom-call(s32[12]{0:T(128)} %and_select_fusion.table, bf16[768,2048]{1,0:T(8,128)(2,1)} %bitcast.53, bf16[768,2048]{1,0:T(8,128)(2,1)} %fusion.back_ref, bf16[768,2048]{1,0:T(8,128)(2,1)} %shard_map.86.att_ref, bf16[16,128,4096]{2,1,0:T(8,128)(2,1)} %all-to-all-done.1.k0_ref.k1_ref.v0_ref.v1_ref, ...), custom_call_target="tpu_custom_call" | custom-call | flops 1610612736 | bytes 25165824 | tf_op jit(solution)/shard_map/pallas_call | solution.py:110
  398.3 6.7 %convolution_convert_fusion.1 = bf16[768,1024]{1,0:T(8,128)(2,1)S(1)} fusion(bf16[768,2048]{1,0:T(8,128)(2,1)} %shard_map.86.att_ref, bf16[2048,1024]{1,0:T(8,128)(2,1)} %bitcast.13, bf16[2048,1024]{1,0:T(8,128)(2,1)} %collective-permute-done, pred[]{:T(512)S(6)} %eq.16), kind=kOutput, calls=%fused_computation.6 | convolution fusion | flops 3224109056 | bytes 13107201 | tf_op jit(solution)/shard_map/dot_general | solution.py:206
  405.0 5.9 %convolution_convert_fusion = bf16[768,1024]{1,0:T(8,128)(2,1)S(1)} fusion(bf16[768,2048]{1,0:T(8,128)(2,1)S(1)} %copy-done.2, bf16[2048,1024]{1,0:T(8,128)(2,1)} %collective-permute-done, bf16[2048,1024]{1,0:T(8,128)(2,1)} %bitcast.13, pred[]{:T(512)S(6)} %eq.16), kind=kOutput, calls=%fused_computation.5 | convolution fusion | flops 3224109056 | bytes 13107201 | tf_op jit(solution)/shard_map/dot_general | solution.py:207
  410.9 2.0 pad_maximum_fusion
  412.9 44.5 %reduce-scatter.2.cloned.1.call-done = f32[128,2048]{1,0:T(8,128)} async-done(((f32[2048,2048]{1,0:T(8,128)}), f32[128,2048]{1,0:T(8,128)}) %reduce-scatter.2.cloned.1.call-update) | async-done | bytes 1048592 | tf_op jit(solution)/shard_map/reduce_scatter | solution.py:226
  457.3 1.3 broadcast_multiply_fusion
  458.7 17.5 %all_to_all.27 = f32[8,16,2048]{2,1,0:T(8,128)S(1)} all-to-all(f32[8,16,2048]{2,1,0:T(8,128)S(1)} %bitcast.55), channel_id=1, replica_groups=mesh['dp'=8,'ctx'=16] {'dp'}, dimensions={0} | all-to-all | bytes 2097152 | tf_op jit(solution)/shard_map/all_to_all | solution.py:231
  476.2 0.1 broadcast_in_dim.29
  476.3 23.3 %all_to_all.28 = bf16[16,16,2048]{2,1,0:T(8,128)(2,1)S(1)} all-to-all(bf16[16,16,2048]{2,1,0:T(8,128)(2,1)S(1)} %broadcast_in_dim.29), channel_id=1, replica_groups=mesh['dp'=8,'ctx'=16] {'ctx'}, dimensions={0} | all-to-all | bytes 2097152 | tf_op jit(solution)/shard_map/all_to_all | solution.py:237
  499.6 1.6 bitcast_convert_fusion
  (14 shorter events, 0.2 us)
Async XLA Ops:
  7.2 38.3 %copy-start = (bf16[256,2048]{1,0:T(8,128)(2,1)S(1)}, bf16[256,2048]{1,0:T(8,128)(2,1)}, u32[]{:S(2)}) copy-start(bf16[256,2048]{1,0:T(8,128)(2,1)} %param.10) | copy-start | bytes 3145732
  8.7 16.1 %all-to-all-start = ((s32[16,1,12]{2,1,0:T(1,128)}), s32[16,1,12]{2,1,0:T(1,128)S(1)}, u32[]{:S(2)}, u32[]{:S(2)}) async-start(s32[16,1,12]{2,1,0:T(1,128)} %broadcast_in_dim.12), calls=%async_computation | async-start | bytes 16384 | tf_op jit(solution)/shard_map/all_to_all | solution.py:171
  40.3 228.4 %all-to-all-start.1 = ((bf16[16,128,4096]{2,1,0:T(8,128)(2,1)}), bf16[16,128,4096]{2,1,0:T(8,128)(2,1)}, u32[]{:S(2)}, u32[]{:S(2)}) async-start(bf16[16,128,4096]{2,1,0:T(8,128)(2,1)} %shard_map.85), calls=%async_computation.1 | async-start | bytes 33554432 | tf_op jit(solution)/shard_map/all_to_all | solution.py:180
  45.3 412.0 %reduce-scatter.2.cloned.1.call-start = ((), (), s32[]{:S(2)}) async-start(), calls=%async_computation.6 | async-start | bytes 17825792 | tf_op jit(solution)/shard_map/reduce_scatter | solution.py:226
  286.7 2.8 copy-start.3
  352.8 9.0 %collective-permute-start = (bf16[2048,1024]{1,0:T(8,128)(2,1)}, bf16[2048,1024]{1,0:T(8,128)(2,1)}, u32[]{:S(2)}, u32[]{:S(2)}) collective-permute-start(bf16[2048,1024]{1,0:T(8,128)(2,1)} %bitcast.13), channel_id=1, source_target_pairs={{0,1},{1,0},{2,3},{3,2},{4,5},{5,4},{6,7},{7,6},{8,9},{9,8},{10,11... | collective-permute-start | bytes 12582920 | tf_op jit(solution)/shard_map/ppermute | solution.py:201
  361.8 5.9 %copy-start.4 = (bf16[1,768,2048]{2,1,0:T(8,128)(2,1)S(1)}, bf16[1,768,2048]{2,1,0:T(8,128)(2,1)}, u32[]{:S(2)}) copy-start(bf16[1,768,2048]{2,1,0:T(8,128)(2,1)} %param.9) | copy-start | bytes 9437188
  398.3 6.7 %copy-start.2 = (bf16[768,2048]{1,0:T(8,128)(2,1)S(1)}, bf16[768,2048]{1,0:T(8,128)(2,1)}, u32[]{:S(2)}) copy-start(bf16[768,2048]{1,0:T(8,128)(2,1)} %shard_map.86.att_ref) | copy-start | bytes 9437188
  476.1 25.1 %copy-start.1 = (bf16[256,2048]{1,0:T(8,128)(2,1)S(1)}, bf16[256,2048]{1,0:T(8,128)(2,1)}, u32[]{:S(2)}) copy-start(bf16[256,2048]{1,0:T(8,128)(2,1)} %param.10) | copy-start | bytes 3145732
Sparse Core Ops, SparseCore 0:
  299.2 158.0 reduce-scatter.1
